TPU v7x, 256 devices: a whole 4x4x8 slice. The times are simulated.
256 devices in a mesh: member: 128 (over z, x, y), segment: 2 (over core).
Axes of the slice: x: 4, y: 4, z: 8, core: 2. Of those that a mesh axis runs over, the one named last changes fastest.
Arguments:
- start_noise: float32 [128, 4, 4, 256], P('member'), may hold values from -6 to 6
- reg_means: float32 [128, 4, 32, 4, 256], P('member'), may hold values from -6 to 6
- hour_owner: int32 [4], replicated, may hold values from 0 to 127
- member_tile: int32 [128], P('member'), may hold values from 0 to 31
- sigmas: float32 [9], replicated, may hold values from 0.3 to 22, as said below
- lift_weight: float32 [8, 128], replicated, may hold values from -2 to 2
- noise_embed: float32 [128], replicated, may hold values from -6 to 6
- section_conv: bfloat16 [2, 9, 128, 128], P('segment'), may hold values from -0.1875 to 0.1875
- section_gain: bfloat16 [2, 128], P('segment'), may hold values from 0.5 to 2
- out_weight: float32 [128, 4], replicated, may hold values from -0.5 to 0.5
Outputs:
- downscaled: float32 [4, 128, 4, 256], P('segment', 'member')
Inputs may be any that keep to these rules, and one draw needn't show every extreme that they name: `sigmas`: strictly decreasing and positive.
All inputs are finite; a program needn't handle non-finite values.
Results may differ from a plain program's by a relative error of at most 0.00038.
Values may be sent and summed in bfloat16 or wider, within the bound.
No kernel may reach another device: no remote copies, remote signals or barrier semaphores. Data moves between devices by JAX's collectives and lax.ppermute only.
A program may use at most 64 MiB of HBM per device.

v0:
```python
import jax
import jax.numpy as jnp
from jax import lax
from jax.sharding import PartitionSpec as P

SIDE = 16
HOURS = 4
STEPS = 8


EPSILON = 1e-06
DATA_VAR = 0.25


def from_root(value, axis, source):
    kept = jnp.where(lax.axis_index(axis) == source, value, 0).astype(value.dtype)
    return lax.psum(kept, axis)


def shifted(block, axis, distance):
    devices = range(lax.axis_size(axis))
    route = [(i - distance, i) for i in devices if i - distance in devices]
    return lax.ppermute(block, axis, route)


def rms_scale(values):
    return values * lax.rsqrt(jnp.mean(values * values, axis=-1, keepdims=True) + EPSILON)


def conv_three(gated, kernel, tile_side):
    batched = gated.shape[0]
    channels = gated.shape[-1]
    grid_view = gated.reshape(batched, tile_side, tile_side, channels)
    padded = jnp.pad(grid_view, ((0, 0), (1, 1), (1, 1), (0, 0)))
    windows = [
        padded[:, vertical : vertical + tile_side, lateral : lateral + tile_side, :]
        for vertical in range(3)
        for lateral in range(3)
    ]
    stacked = jnp.concatenate(windows, axis=-1).reshape(
        batched * tile_side * tile_side, 9 * channels
    )
    summed = jnp.dot(
        stacked, kernel.reshape(9 * channels, kernel.shape[-1]), preferred_element_type=jnp.float32
    )
    return summed.reshape(batched, tile_side * tile_side, kernel.shape[-1])


def lift_inputs(state_now, mean_now, sigma_now, lift_weight, noise_embed):
    scale_in = lax.rsqrt(sigma_now * sigma_now + DATA_VAR)
    stacked = jnp.concatenate([state_now * scale_in, mean_now], axis=1)
    lifted = jnp.einsum("bcp,cd->bpd", stacked, lift_weight, precision=lax.Precision.HIGHEST)
    return lifted + jnp.log(sigma_now) / 4.0 * noise_embed


def encode(lifted, kernel, gain, tile_side):
    gated = jax.nn.silu(rms_scale(lifted) * gain.astype(jnp.float32)).astype(jnp.bfloat16)
    return (lifted + conv_three(gated, kernel, tile_side)).astype(jnp.bfloat16)


def decode(encoded, skipped, kernel, gain, out_weight, tile_side):
    widened = encoded.astype(jnp.float32)
    gated = jax.nn.silu(rms_scale(widened) * gain.astype(jnp.float32)).astype(jnp.bfloat16)
    merged = widened + conv_three(gated, kernel, tile_side) + skipped.astype(jnp.float32)
    return jnp.einsum(
        "bpd,dc->bcp", jax.nn.silu(rms_scale(merged)), out_weight, precision=lax.Precision.HIGHEST
    )


def euler_step(state_now, net_out, sigma_now, sigma_next):
    spread = sigma_now * sigma_now + DATA_VAR
    denoised = DATA_VAR / spread * state_now + 0.5 * sigma_now * lax.rsqrt(spread) * net_out
    return state_now + (sigma_next - sigma_now) / sigma_now * (state_now - denoised)


def body(
    start_noise,
    reg_means,
    hour_owner,
    member_tile,
    sigmas,
    lift_weight,
    noise_embed,
    section_conv,
    section_gain,
    out_weight,
):
    tile_side = SIDE
    segment_index = lax.axis_index("segment")
    is_first = segment_index == 0
    half_hours = HOURS // lax.axis_size("segment")
    pixels = tile_side * tile_side
    channels = section_conv.shape[-1]
    variables = start_noise.shape[2]

    def sigma_at(level):
        return lax.dynamic_index_in_dim(sigmas, level, 0, keepdims=False)

    picked = []
    for hour_index in range(HOURS):
        arrived = from_root(reg_means[0, hour_index], "member", hour_owner[hour_index])
        picked.append(lax.dynamic_index_in_dim(arrived, member_tile[0], 0, keepdims=False))
    all_means = jnp.stack(picked)
    kernel = section_conv[0]
    gain = section_gain[0]
    states = sigmas[0] * start_noise[0]
    zero_lifted = jnp.zeros((1, pixels, channels), jnp.float32)
    zero_out = jnp.zeros((1, variables, pixels), jnp.float32)

    def lifted_for(states, hour_index, step_index):
        state_now = lax.dynamic_index_in_dim(states, hour_index, 0, keepdims=True)
        mean_now = lax.dynamic_index_in_dim(all_means, hour_index, 0, keepdims=True)
        return lift_inputs(state_now, mean_now, sigma_at(step_index), lift_weight, noise_embed)

    def make_payload(encoded, lifted):
        return (encoded, lifted.astype(jnp.bfloat16))

    def skip_for(payload):
        return payload[1]

    def send_forward(payload):
        return shifted((payload[0], payload[1]), "segment", 1)

    def send_back(net_out):
        return shifted(net_out, "segment", -1)

    zero_payload = make_payload(zero_lifted.astype(jnp.bfloat16), zero_lifted)

    def encode_item(states, hour_index, step_index):
        lifted = lifted_for(states, hour_index, step_index)
        return make_payload(encode(lifted, kernel, gain, tile_side), lifted)

    def decode_item(payload):
        skipped = skip_for(payload)
        return decode(payload[0], skipped, kernel, gain, out_weight, tile_side)

    def update_state(states, net_out, hour_index, step_index):
        state_now = lax.dynamic_index_in_dim(states, hour_index, 0, keepdims=True)
        moved = euler_step(state_now, net_out, sigma_at(step_index), sigma_at(step_index + 1))
        moved = jnp.where(True, moved, state_now)
        return lax.dynamic_update_slice_in_dim(states, moved, hour_index, 0)

    def one_hour(hour_index, states):
        for step_index in range(STEPS):
            outgoing = lax.cond(
                is_first, lambda: encode_item(states, hour_index, step_index), lambda: zero_payload
            )
            received = send_forward(outgoing)
            net_out = lax.cond(is_first, lambda: zero_out, lambda: decode_item(received))
            returned = send_back(net_out)
            used = jnp.where(is_first, returned, net_out)
            states = update_state(states, used, hour_index, step_index)
        return states

    states = lax.fori_loop(0, HOURS, one_hour, states)
    finished = all_means + states
    return lax.dynamic_slice_in_dim(finished, segment_index * half_hours, half_hours, 0)[:, None]


def solution(mesh):
    placed = (
        P("member", None, None, None),
        P("member", None, None, None, None),
        P(),
        P("member"),
        P(),
        P(),
        P(),
        P("segment", None, None, None),
        P("segment", None),
        P(),
    )
    return jax.shard_map(
        body,
        mesh=mesh,
        in_specs=placed,
        out_specs=P("segment", "member", None, None),
        check_vma=False,
    )
```

profile of v0, /device:TPU:32, one launch (start us, length us, event | category | flops | bytes accessed | tf_op | source)
XLA Modules:
  0.0 618.4 jit_solution(16559562325831433011)
XLA Ops:
  46.2 188.5 %all-reduce.19.cloned.1.call-done = (f32[32,4,256]{2,1,0:T(4,128)}, f32[32,4,256]{2,1,0:T(4,128)}, f32[32,4,256]{2,1,0:T(4,128)}, f32[32,4,256]{2,1,0:T(4,128)}) async-done(((f32[32,4,256]{2,1,0:T(4,128)}, f32[32,4,256]{2,1,0:T(4,128)}, f32[32,4,256]{2,1,0:T(4,128)}, f32[32,4,256]{2,1,0:T(4,128)}), (f32[32,4,256]{2,1,0:T(4,128)}, f32[32,4,256]{2,1,0:T(4,128)}, f32[32,4,256]{2,1,0:T(4,128)}, ...) | async-done | bytes 524304 | tf_op jit(solution)/shard_map/psum | solution.py:17
  236.8 374.2 %while.15 = (s32[]{:T(128)}, f32[4,4,256]{2,1,0:T(4,128)S(1)}, f32[]{:T(128)}, f32[]{:T(128)}, f32[]{:T(128)}, /*index=5*/pred[]{:T(512)}, f32[9]{0:T(128)S(1)},...) while((s32[]{:T(128)}, f32[4,4,256]{2,1,0:T(4,128)S(1)}, ...), condition=%wide.region_61.62_spmd, body=%wide.region_4.61_spmd.sunk | while | flops 1257071616 | bytes 68320448 | solution.py:155
  243.2 3.1 collective-permute-done.2
  246.3 3.9 conditional.34
  255.2 3.1 collective-permute-done.5
  258.3 3.9 conditional.36
  267.2 3.1 collective-permute-done.8
  270.3 3.9 conditional.38
  282.3 3.9 conditional.40
  291.2 3.1 collective-permute-done.14
  294.3 3.9 conditional.42
  303.2 3.1 collective-permute-done.17
  306.3 3.9 conditional.44
  318.3 3.9 conditional.46
  327.2 3.1 collective-permute-done.23
  336.8 3.1 collective-permute-done.2
  339.9 3.9 conditional.34
  351.8 3.9 conditional.36
  360.8 3.1 collective-permute-done.8
  363.8 3.9 conditional.38
  372.8 3.1 collective-permute-done.11
  375.8 3.9 conditional.40
  387.8 3.9 conditional.42
  396.8 3.1 collective-permute-done.17
  399.8 3.9 conditional.44
  408.7 3.1 collective-permute-done.20
  411.8 3.9 conditional.46
  430.3 3.1 collective-permute-done.2
  433.4 3.9 conditional.34
  442.3 3.1 collective-permute-done.5
  445.4 3.9 conditional.36
  457.4 3.9 conditional.38
  466.3 3.1 collective-permute-done.11
  469.4 3.9 conditional.40
  478.3 3.1 collective-permute-done.14
  481.4 3.9 conditional.42
  493.4 3.9 conditional.44
  502.3 3.1 collective-permute-done.20
  505.4 3.9 conditional.46
  526.9 3.9 conditional.34
  538.9 3.9 conditional.36
  550.9 3.9 conditional.38
  562.9 3.9 conditional.40
  571.8 3.1 collective-permute-done.14
  574.9 3.9 conditional.42
  586.9 3.9 conditional.44
  598.9 3.9 conditional.46
  607.8 3.1 collective-permute-done.23
  (936 shorter events, 271.2 us)
Async XLA Ops:
  6.5 228.2 %all-reduce.19.cloned.1.call-start = ((), (), s32[]{:S(2)}) async-start(), calls=%async_computation | async-start | bytes 1048576 | tf_op jit(solution)/shard_map/psum | solution.py:17
  238.3 2.7 collective-permute-start
  241.9 4.4 collective-permute-start.2
  250.3 2.7 collective-permute-start.3
  253.9 4.4 collective-permute-start.5
  262.3 2.7 collective-permute-start.6
  265.9 4.4 collective-permute-start.8
  274.3 2.7 collective-permute-start.10
  277.9 4.4 collective-permute-start.11
  286.3 2.7 collective-permute-start.12
  289.9 4.4 collective-permute-start.14
  298.3 2.7 collective-permute-start.15
  301.9 4.4 collective-permute-start.17
  310.3 2.7 collective-permute-start.18
  313.9 4.4 collective-permute-start.20
  325.9 4.4 collective-permute-start.23
  335.5 4.4 collective-permute-start.2
  347.5 4.4 collective-permute-start.5
  359.5 4.4 collective-permute-start.8
  371.5 4.4 collective-permute-start.11
  383.5 4.4 collective-permute-start.14
  395.5 4.4 collective-permute-start.17
  407.5 4.4 collective-permute-start.20
  419.5 4.4 collective-permute-start.23
  429.0 4.4 collective-permute-start.2
  441.0 4.4 collective-permute-start.5
  449.4 2.7 collective-permute-start.6
  453.0 4.4 collective-permute-start.8
  461.4 2.7 collective-permute-start.10
  465.0 4.4 collective-permute-start.11
  477.0 4.4 collective-permute-start.14
  485.4 2.7 collective-permute-start.15
  489.0 4.4 collective-permute-start.17
  497.4 2.7 collective-permute-start.18
  501.0 4.4 collective-permute-start.20
  509.4 2.7 collective-permute-start.21
  513.0 4.4 collective-permute-start.23
  519.0 2.7 collective-permute-start
  522.6 4.4 collective-permute-start.2
  534.6 4.4 collective-permute-start.5
  543.0 2.7 collective-permute-start.6
  546.6 4.4 collective-permute-start.8
  558.5 4.4 collective-permute-start.11
  570.6 4.4 collective-permute-start.14
  578.9 2.7 collective-permute-start.15
  582.5 4.4 collective-permute-start.17
  594.5 4.4 collective-permute-start.20
  606.5 4.4 collective-permute-start.23
  (57 other events, 344.6 us)
Sparse Core Ops, SparseCore 0:
  13.1 221.5 all-reduce.18
where the time goes:
time: 624 us; the launch traced here: 618 us
  waiting for transfers between devices  315 us (50%)
  starting transfers between devices  124 us (20%)
  loops' own time  62.1 us (10%)
  between operations  47.2 us (8%)
  local copies, waits for them, and re-layouts  36.8 us (6%)
  matrix products  25.3 us (4%)
  other arithmetic  8.46 us (1%)
    psum x1, waiting for transfers between devices, from_root(): return lax.psum(kept, axis)  188 us
    ppermute x96, waiting for transfers between devices, shifted(): return lax.ppermute(block, axis, route)  126 us
    ppermute x96, starting transfers between devices, shifted(): return lax.ppermute(block, axis, route)  124 us
    another operation x32, loops' own time, one_hour(): lax.cond(is_first, lambda: encode_item(states, hour_index, step_index), l...  60.4 us
    dynamic_slice x29, local copies, waits for them, and re-layouts, sigma_at(): return lax.dynamic_index_in_dim(sigmas, level, 0, keepdims=False)  17.6 us
    dot_general x32, matrix products, lift_inputs(): jnp.einsum('bcp,cd->bpd', stacked, lift_weight, precision=lax.Precision.H...  15.5 us
  transfers between devices with their start and end apart: 97, of which 65 were waited for; matrix products, arithmetic and copies ran while one was open for 1% of the time, Pallas kernels for 0%

commit v1 on v0

v1 whole, which is shorter than its diff:
```python
import numpy as np
import jax
import jax.numpy as jnp
from jax import lax
from jax.sharding import PartitionSpec as P

SIDE = 16
HOURS = 4
STEPS = 8


EPSILON = 1e-06
DATA_VAR = 0.25


def ring_routes(mesh):
    devices = np.asarray(mesh.devices)[:, 0]
    coords = [tuple(d.coords[:3]) for d in devices]
    where = {c: i for i, c in enumerate(coords)}
    sizes = [len({c[a] for c in coords}) for a in range(3)]
    routes = []
    for axis in sorted(range(3), key=lambda a: -sizes[a]):
        n = sizes[axis]
        if n == 1:
            continue
        shifts = []
        distance = 1
        while distance < n:
            pairs = {}
            for sign in (1, -1):
                pair = []
                for i, c in enumerate(coords):
                    moved = list(c)
                    moved[axis] = (c[axis] + sign * distance) % n
                    pair.append((i, where[tuple(moved)]))
                pairs[sign] = tuple(pair)
            shifts.append(pairs)
            distance *= 2
        routes.append((n, shifts))
    return routes


def broadcast_sum(block, routes):
    half = block.shape[0] // 2
    up, down = block[:half], block[half:]
    for n, shifts in routes:
        if n & (n - 1):
            raise ValueError("ring size")
        for pairs in shifts:
            up = up + lax.ppermute(up, "member", pairs[1])
            down = down + lax.ppermute(down, "member", pairs[-1])
    return jnp.concatenate([up, down], axis=0)


def rms_scale(values):
    return values * lax.rsqrt(jnp.mean(values * values, axis=-1, keepdims=True) + EPSILON)


def conv_three(gated, kernel, tile_side):
    batched = gated.shape[0]
    channels = gated.shape[-1]
    grid_view = gated.reshape(batched, tile_side, tile_side, channels)
    padded = jnp.pad(grid_view, ((0, 0), (1, 1), (1, 1), (0, 0)))
    windows = [
        padded[:, vertical : vertical + tile_side, lateral : lateral + tile_side, :]
        for vertical in range(3)
        for lateral in range(3)
    ]
    stacked = jnp.concatenate(windows, axis=-1).reshape(
        batched * tile_side * tile_side, 9 * channels
    )
    summed = jnp.dot(
        stacked, kernel.reshape(9 * channels, kernel.shape[-1]), preferred_element_type=jnp.float32
    )
    return summed.reshape(batched, tile_side * tile_side, kernel.shape[-1])


def network(lifted, kernels, gains, out_weight, tile_side):
    gated = jax.nn.silu(rms_scale(lifted) * gains[0].astype(jnp.float32)).astype(jnp.bfloat16)
    encoded = (lifted + conv_three(gated, kernels[0], tile_side)).astype(jnp.bfloat16)
    widened = encoded.astype(jnp.float32)
    gated = jax.nn.silu(rms_scale(widened) * gains[1].astype(jnp.float32)).astype(jnp.bfloat16)
    skipped = lifted.astype(jnp.bfloat16).astype(jnp.float32)
    merged = widened + conv_three(gated, kernels[1], tile_side) + skipped
    return jnp.einsum(
        "bpd,dc->bcp", jax.nn.silu(rms_scale(merged)), out_weight, precision=lax.Precision.HIGHEST
    )


def euler_step(state_now, net_out, sigma_now, sigma_next):
    spread = sigma_now * sigma_now + DATA_VAR
    denoised = DATA_VAR / spread * state_now + 0.5 * sigma_now * lax.rsqrt(spread) * net_out
    return state_now + (sigma_next - sigma_now) / sigma_now * (state_now - denoised)


def make_body(routes):
    def body(
        start_noise,
        reg_means,
        hour_owner,
        member_tile,
        sigmas,
        lift_weight,
        noise_embed,
        section_conv,
        section_gain,
        out_weight,
    ):
        tile_side = SIDE
        segment_index = lax.axis_index("segment")
        is_first = segment_index == 0
        half_hours = HOURS // lax.axis_size("segment")
        first_hour = segment_index * half_hours
        variables = start_noise.shape[2]

        swap = [(0, 1), (1, 0)]
        other_conv = lax.ppermute(section_conv, "segment", swap)
        other_gain = lax.ppermute(section_gain, "segment", swap)
        kernels = (
            jnp.where(is_first, section_conv[0], other_conv[0]),
            jnp.where(is_first, other_conv[0], section_conv[0]),
        )
        gains = (
            jnp.where(is_first, section_gain[0], other_gain[0]),
            jnp.where(is_first, other_gain[0], section_gain[0]),
        )

        owners = lax.dynamic_slice_in_dim(hour_owner, first_hour, half_hours, 0)
        mine = lax.dynamic_slice_in_dim(reg_means[0], first_hour, half_hours, 0)
        is_owner = lax.axis_index("member") == owners
        kept = jnp.where(is_owner[:, None, None, None], mine, 0).astype(mine.dtype)
        arrived = broadcast_sum(kept, routes)
        means = lax.dynamic_index_in_dim(arrived, member_tile[0], 1, keepdims=False)

        noise = lax.dynamic_slice_in_dim(start_noise[0], first_hour, half_hours, 0)
        states = sigmas[0] * noise
        mean_lift = jnp.einsum(
            "bcp,cd->bpd", means, lift_weight[variables:], precision=lax.Precision.HIGHEST
        )
        def one_step(step_index, states):
            sigma_now = lax.dynamic_index_in_dim(sigmas, step_index, 0, keepdims=False)
            sigma_next = lax.dynamic_index_in_dim(sigmas, step_index + 1, 0, keepdims=False)
            scale_in = lax.rsqrt(sigma_now * sigma_now + DATA_VAR)
            lifted = jnp.einsum(
                "bcp,cd->bpd",
                states * scale_in,
                lift_weight[:variables],
                precision=lax.Precision.HIGHEST,
            )
            lifted = lifted + mean_lift + jnp.log(sigma_now) / 4.0 * noise_embed
            net_out = network(lifted, kernels, gains, out_weight, tile_side)
            return euler_step(states, net_out, sigma_now, sigma_next)

        states = lax.fori_loop(0, STEPS, one_step, states)
        return (means + states)[:, None]

    return body


def solution(mesh):
    placed = (
        P("member", None, None, None),
        P("member", None, None, None, None),
        P(),
        P("member"),
        P(),
        P(),
        P(),
        P("segment", None, None, None),
        P("segment", None),
        P(),
    )
    return jax.shard_map(
        make_body(ring_routes(mesh)),
        mesh=mesh,
        in_specs=placed,
        out_specs=P("segment", "member", None, None),
        check_vma=False,
    )
```

time: 624 us -> 144 us (0.23)
  the two profiles are of different devices: /device:TPU:32 before, /device:TPU:16 now
where the time goes in v1:
time: 144 us
  loops' own time  39.9 us (28%)
  waiting for transfers between devices  36.2 us (25%)
  starting transfers between devices  26.9 us (19%)
  matrix products  19.3 us (13%)
  local copies, waits for them, and re-layouts  12.9 us (9%)
  other arithmetic  7.71 us (5%)
    another operation x1, loops' own time, body(): states = lax.fori_loop(0, STEPS, one_step, states)  39.9 us
    ppermute x7, waiting for transfers between devices, broadcast_sum(): up = up + lax.ppermute(up, 'member', pairs[1])  19.6 us
    ppermute x7, waiting for transfers between devices, broadcast_sum(): down = down + lax.ppermute(down, 'member', pairs[-1])  16.6 us
    ppermute x7, starting transfers between devices, broadcast_sum(): down = down + lax.ppermute(down, 'member', pairs[-1])  15.1 us
    ppermute x7, starting transfers between devices, broadcast_sum(): up = up + lax.ppermute(up, 'member', pairs[1])  11.3 us
    dot_general x16, matrix products, conv_three(): jnp.dot(stacked, kernel.reshape(9 * channels, kernel.shape[-1]), preferre...  9.31 us
    dot_general x8, matrix products, one_step(): jnp.einsum('bcp,cd->bpd', states * scale_in, lift_weight[:variables], pre...  5.47 us
    dynamic_slice x8, local copies, waits for them, and re-layouts, one_step(): lax.dynamic_index_in_dim(sigmas, step_index + 1, 0, keepdims=False)  5.24 us
  transfers between devices with their start and end apart: 16, of which 12 were waited for; matrix products, arithmetic and copies ran while one was open for 0% of the time, Pallas kernels for 0%

profile of v1, /device:TPU:16, one launch (start us, length us, event | category | flops | bytes accessed | tf_op | source)
XLA Modules:
  0.0 143.8 jit_solution(10192684341310221425)
XLA Ops:
  0.0 1.0 copy-done
  1.1 0.7 dynamic-slice_compare_fusion
  1.9 5.9 %collective-permute-start.7 = (f32[1,32,4,256]{3,1,2,0:T(8,128)S(1)}, f32[1,32,4,256]{3,1,2,0:T(8,128)S(1)}, u32[]{:S(2)}, u32[]{:S(2)}) collective-permute-start(f32[1,32,4,256]{3,1,2,0:T(8,128)S(1)} %get-tuple-element.321), channel_id=1, source_target_pairs={{0,224},{2,226},{4,228},{6,230},{8,232},{10,234},{12,236},{14,238}... | collective-permute-start | bytes 393224 | tf_op jit(solution)/shard_map/ppermute | solution.py:51
  7.9 2.8 %collective-permute-done.7 = f32[1,32,4,256]{3,1,2,0:T(8,128)S(1)} collective-permute-done((f32[1,32,4,256]{3,1,2,0:T(8,128)S(1)}, f32[1,32,4,256]{3,1,2,0:T(8,128)S(1)}, u32[]{:S(2)}, u32[]{:S(2)}) %collective-permute-start.7) | collective-permute-done | bytes 131104 | tf_op jit(solution)/shard_map/ppermute | solution.py:51
  10.6 3.4 %collective-permute-done = f32[1,32,4,256]{3,1,2,0:T(8,128)S(1)} collective-permute-done((f32[1,32,4,256]{3,1,2,0:T(8,128)S(1)}, f32[1,32,4,256]{3,1,2,0:T(8,128)S(1)}, u32[]{:S(2)}, u32[]{:S(2)}) %collective-permute-start) | collective-permute-done | bytes 131104 | tf_op jit(solution)/shard_map/ppermute | solution.py:50
  14.4 2.8 %collective-permute-start.1 = (f32[1,32,4,256]{3,1,2,0:T(8,128)S(1)}, f32[1,32,4,256]{3,1,2,0:T(8,128)S(1)}, u32[]{:S(2)}, u32[]{:S(2)}) collective-permute-start(f32[1,32,4,256]{3,1,2,0:T(8,128)S(1)} %get-tuple-element.320), channel_id=1, source_target_pairs={{0,64},{2,66},{4,68},{6,70},{8,72},{10,74},{12,76},{14,78},{16,80}... | collective-permute-start | bytes 393224 | tf_op jit(solution)/shard_map/ppermute | solution.py:50
  17.2 3.9 %collective-permute-done.8 = f32[1,32,4,256]{3,1,2,0:T(8,128)S(1)} collective-permute-done((f32[1,32,4,256]{3,1,2,0:T(8,128)S(1)}, f32[1,32,4,256]{3,1,2,0:T(8,128)S(1)}, u32[]{:S(2)}, u32[]{:S(2)}) %collective-permute-start.8) | collective-permute-done | bytes 131104 | tf_op jit(solution)/shard_map/ppermute | solution.py:51
  21.1 2.6 %collective-permute-start.9 = (f32[1,32,4,256]{3,1,2,0:T(8,128)S(1)}, f32[1,32,4,256]{3,1,2,0:T(8,128)S(1)}, u32[]{:S(2)}, u32[]{:S(2)}) collective-permute-start(f32[1,32,4,256]{3,1,2,0:T(8,128)S(1)} %add.295), channel_id=1, source_target_pairs={{0,128},{2,130},{4,132},{6,134},{8,136},{10,138},{12,140},{14,142}... | collective-permute-start | bytes 393224 | tf_op jit(solution)/shard_map/ppermute | solution.py:51
  23.7 3.5 %collective-permute-start.2 = (f32[1,32,4,256]{3,1,2,0:T(8,128)S(1)}, f32[1,32,4,256]{3,1,2,0:T(8,128)S(1)}, u32[]{:S(2)}, u32[]{:S(2)}) collective-permute-start(f32[1,32,4,256]{3,1,2,0:T(8,128)S(1)} %add.288), channel_id=1, source_target_pairs={{0,128},{2,130},{4,132},{6,134},{8,136},{10,138},{12,140},{14,142}... | collective-permute-start | bytes 393224 | tf_op jit(solution)/shard_map/ppermute | solution.py:50
  27.2 6.8 %collective-permute-done.9 = f32[1,32,4,256]{3,1,2,0:T(8,128)S(1)} collective-permute-done((f32[1,32,4,256]{3,1,2,0:T(8,128)S(1)}, f32[1,32,4,256]{3,1,2,0:T(8,128)S(1)}, u32[]{:S(2)}, u32[]{:S(2)}) %collective-permute-start.9) | collective-permute-done | bytes 131104 | tf_op jit(solution)/shard_map/ppermute | solution.py:51
  34.0 2.8 %collective-permute-start.10 = (f32[1,32,4,256]{3,1,2,0:T(8,128)S(1)}, f32[1,32,4,256]{3,1,2,0:T(8,128)S(1)}, u32[]{:S(2)}, u32[]{:S(2)}) collective-permute-start(f32[1,32,4,256]{3,1,2,0:T(8,128)S(1)} %add.296), channel_id=1, source_target_pairs={{0,24},{2,26},{4,28},{6,30},{8,0},{10,2},{12,4},{14,6},{16,8},{18,... | collective-permute-start | bytes 393224 | tf_op jit(solution)/shard_map/ppermute | solution.py:51
  37.2 1.6 %collective-permute-start.3 = (f32[1,32,4,256]{3,1,2,0:T(8,128)S(1)}, f32[1,32,4,256]{3,1,2,0:T(8,128)S(1)}, u32[]{:S(2)}, u32[]{:S(2)}) collective-permute-start(f32[1,32,4,256]{3,1,2,0:T(8,128)S(1)} %add.289), channel_id=1, source_target_pairs={{0,8},{2,10},{4,12},{6,14},{8,16},{10,18},{12,20},{14,22},{16,24},... | collective-permute-start | bytes 393224 | tf_op jit(solution)/shard_map/ppermute | solution.py:50
  38.8 1.8 %collective-permute-done.10 = f32[1,32,4,256]{3,1,2,0:T(8,128)S(1)} collective-permute-done((f32[1,32,4,256]{3,1,2,0:T(8,128)S(1)}, f32[1,32,4,256]{3,1,2,0:T(8,128)S(1)}, u32[]{:S(2)}, u32[]{:S(2)}) %collective-permute-start.10) | collective-permute-done | bytes 131104 | tf_op jit(solution)/shard_map/ppermute | solution.py:51
  40.6 1.9 %collective-permute-start.11 = (f32[1,32,4,256]{3,1,2,0:T(8,128)S(1)}, f32[1,32,4,256]{3,1,2,0:T(8,128)S(1)}, u32[]{:S(2)}, u32[]{:S(2)}) collective-permute-start(f32[1,32,4,256]{3,1,2,0:T(8,128)S(1)} %add.297), channel_id=1, source_target_pairs={{0,16},{2,18},{4,20},{6,22},{8,24},{10,26},{12,28},{14,30},{16,0},... | collective-permute-start | bytes 393224 | tf_op jit(solution)/shard_map/ppermute | solution.py:51
  42.5 1.1 collective-permute-done.3
  43.6 1.8 %collective-permute-start.4 = (f32[1,32,4,256]{3,1,2,0:T(8,128)S(1)}, f32[1,32,4,256]{3,1,2,0:T(8,128)S(1)}, u32[]{:S(2)}, u32[]{:S(2)}) collective-permute-start(f32[1,32,4,256]{3,1,2,0:T(8,128)S(1)} %add.290), channel_id=1, source_target_pairs={{0,16},{2,18},{4,20},{6,22},{8,24},{10,26},{12,28},{14,30},{16,0},... | collective-permute-start | bytes 393224 | tf_op jit(solution)/shard_map/ppermute | solution.py:50
  46.7 0.6 collective-permute-done.11
  47.8 2.3 %collective-permute-done.4 = f32[1,32,4,256]{3,1,2,0:T(8,128)S(1)} collective-permute-done((f32[1,32,4,256]{3,1,2,0:T(8,128)S(1)}, f32[1,32,4,256]{3,1,2,0:T(8,128)S(1)}, u32[]{:S(2)}, u32[]{:S(2)}) %collective-permute-start.4) | collective-permute-done | bytes 131104 | tf_op jit(solution)/shard_map/ppermute | solution.py:50
  50.2 1.4 collective-permute-start.5
  51.5 0.8 collective-permute-done.12
  52.4 1.0 collective-permute-start.13
  53.4 6.1 %collective-permute-done.5 = f32[1,32,4,256]{3,1,2,0:T(8,128)S(1)} collective-permute-done((f32[1,32,4,256]{3,1,2,0:T(8,128)S(1)}, f32[1,32,4,256]{3,1,2,0:T(8,128)S(1)}, u32[]{:S(2)}, u32[]{:S(2)}) %collective-permute-start.5) | collective-permute-done | bytes 131104 | tf_op jit(solution)/shard_map/ppermute | solution.py:50
  59.9 6.4 %collective-permute-done.6 = f32[1,32,4,256]{3,1,2,0:T(8,128)S(1)} collective-permute-done((f32[1,32,4,256]{3,1,2,0:T(8,128)S(1)}, f32[1,32,4,256]{3,1,2,0:T(8,128)S(1)}, u32[]{:S(2)}, u32[]{:S(2)}) %collective-permute-start.6) | collective-permute-done | bytes 131104 | tf_op jit(solution)/shard_map/ppermute | solution.py:50
  66.3 0.6 fusion.25
  66.9 76.3 %while.15 = (s32[]{:T(128)}, f32[2,4,256]{2,1,0:T(4,128)S(1)}, f32[9]{0:T(128)S(1)}, f32[8,128]{1,0:T(8,128)S(1)}, f32[2,256,128]{2,1,0:T(8,128)S(1)}, /*index=5...) while((s32[]{:T(128)}, f32[2,4,256]{2,1,0:T(4,128)S(1)}, ...), condition=%wide.region_4.5_spmd, body=%wide.region_0.4_spmd.sunk | while | flops 311443328 | bytes 13235547 | solution.py:154
  66.9 0.7 fusion.53
  72.4 0.7 multiply_reduce_fusion.6
  75.3 0.6 multiply_reduce_fusion.8
  76.4 0.7 fusion.53
  81.9 0.7 multiply_reduce_fusion.6
  84.9 0.6 multiply_reduce_fusion.8
  86.0 0.7 fusion.53
  91.4 0.7 multiply_reduce_fusion.6
  94.4 0.6 multiply_reduce_fusion.8
  95.5 0.7 fusion.53
  101.0 0.7 multiply_reduce_fusion.6
  104.0 0.6 multiply_reduce_fusion.8
  105.1 0.7 fusion.53
  110.5 0.7 multiply_reduce_fusion.6
  114.6 0.7 fusion.53
  120.1 0.7 multiply_reduce_fusion.6
  123.0 0.6 multiply_reduce_fusion.8
  124.1 0.7 fusion.53
  129.6 0.7 multiply_reduce_fusion.6
  132.6 0.6 multiply_reduce_fusion.8
  133.7 0.7 fusion.53
  139.1 0.7 multiply_reduce_fusion.6
  143.2 0.6 fusion.27
  (288 shorter events, 24.8 us)
Async XLA Ops:
  0.0 1.0 copy-start
  1.9 8.7 %collective-permute-start.7 = (f32[1,32,4,256]{3,1,2,0:T(8,128)S(1)}, f32[1,32,4,256]{3,1,2,0:T(8,128)S(1)}, u32[]{:S(2)}, u32[]{:S(2)}) collective-permute-start(f32[1,32,4,256]{3,1,2,0:T(8,128)S(1)} %get-tuple-element.321), channel_id=1, source_target_pairs={{0,224},{2,226},{4,228},{6,230},{8,232},{10,234},{12,236},{14,238}... | collective-permute-start | bytes 393224 | tf_op jit(solution)/shard_map/ppermute | solution.py:51
  7.9 6.2 %collective-permute-start = (f32[1,32,4,256]{3,1,2,0:T(8,128)S(1)}, f32[1,32,4,256]{3,1,2,0:T(8,128)S(1)}, u32[]{:S(2)}, u32[]{:S(2)}) collective-permute-start(f32[1,32,4,256]{3,1,2,0:T(8,128)S(1)} %get-tuple-element.322), channel_id=1, source_target_pairs={{0,32},{2,34},{4,36},{6,38},{8,40},{10,42},{12,44},{14,46},{16,48}... | collective-permute-start | bytes 393224 | tf_op jit(solution)/shard_map/ppermute | solution.py:50
  14.1 7.0 %collective-permute-start.8 = (f32[1,32,4,256]{3,1,2,0:T(8,128)S(1)}, f32[1,32,4,256]{3,1,2,0:T(8,128)S(1)}, u32[]{:S(2)}, u32[]{:S(2)}) collective-permute-start(f32[1,32,4,256]{3,1,2,0:T(8,128)S(1)} %get-tuple-element.319), channel_id=1, source_target_pairs={{0,192},{2,194},{4,196},{6,198},{8,200},{10,202},{12,204},{14,206}... | collective-permute-start | bytes 393224 | tf_op jit(solution)/shard_map/ppermute | solution.py:51
  14.4 31.0 %copy-start.5 = (bf16[1,128]{1,0:T(2,128)(2,1)S(1)}, bf16[1,128]{1,0:T(2,128)(2,1)}, u32[]{:S(2)}) copy-start(bf16[1,128]{1,0:T(2,128)(2,1)} %param.20) | copy-start | bytes 772
  14.4 31.0 %copy-start.1 = (bf16[1,9,128,128]{3,2,1,0:T(8,128)(2,1)S(1)}, bf16[1,9,128,128]{3,2,1,0:T(8,128)(2,1)}, u32[]{:S(2)}) copy-start(bf16[1,9,128,128]{3,2,1,0:T(8,128)(2,1)} %param.19) | copy-start | bytes 884740
  14.4 32.2 %copy-start.3 = (f32[9]{0:T(128)S(1)}, f32[9]{0:T(128)}, u32[]{:S(2)}) copy-start(f32[9]{0:T(128)} %param.16) | copy-start | bytes 112
  14.4 32.2 %copy-start.4 = (f32[1,4,4,256]{3,2,1,0:T(4,128)S(1)}, f32[1,4,4,256]{3,2,1,0:T(4,128)}, u32[]{:S(2)}) copy-start(f32[1,4,4,256]{3,2,1,0:T(4,128)} %param.12) | copy-start | bytes 49156
  14.4 9.3 %collective-permute-start.1 = (f32[1,32,4,256]{3,1,2,0:T(8,128)S(1)}, f32[1,32,4,256]{3,1,2,0:T(8,128)S(1)}, u32[]{:S(2)}, u32[]{:S(2)}) collective-permute-start(f32[1,32,4,256]{3,1,2,0:T(8,128)S(1)} %get-tuple-element.320), channel_id=1, source_target_pairs={{0,64},{2,66},{4,68},{6,70},{8,72},{10,74},{12,76},{14,78},{16,80}... | collective-permute-start | bytes 393224 | tf_op jit(solution)/shard_map/ppermute | solution.py:50
  21.1 12.9 %collective-permute-start.9 = (f32[1,32,4,256]{3,1,2,0:T(8,128)S(1)}, f32[1,32,4,256]{3,1,2,0:T(8,128)S(1)}, u32[]{:S(2)}, u32[]{:S(2)}) collective-permute-start(f32[1,32,4,256]{3,1,2,0:T(8,128)S(1)} %add.295), channel_id=1, source_target_pairs={{0,128},{2,130},{4,132},{6,134},{8,136},{10,138},{12,140},{14,142}... | collective-permute-start | bytes 393224 | tf_op jit(solution)/shard_map/ppermute | solution.py:51
  23.7 13.5 %collective-permute-start.2 = (f32[1,32,4,256]{3,1,2,0:T(8,128)S(1)}, f32[1,32,4,256]{3,1,2,0:T(8,128)S(1)}, u32[]{:S(2)}, u32[]{:S(2)}) collective-permute-start(f32[1,32,4,256]{3,1,2,0:T(8,128)S(1)} %add.288), channel_id=1, source_target_pairs={{0,128},{2,130},{4,132},{6,134},{8,136},{10,138},{12,140},{14,142}... | collective-permute-start | bytes 393224 | tf_op jit(solution)/shard_map/ppermute | solution.py:50
  34.0 6.6 %collective-permute-start.10 = (f32[1,32,4,256]{3,1,2,0:T(8,128)S(1)}, f32[1,32,4,256]{3,1,2,0:T(8,128)S(1)}, u32[]{:S(2)}, u32[]{:S(2)}) collective-permute-start(f32[1,32,4,256]{3,1,2,0:T(8,128)S(1)} %add.296), channel_id=1, source_target_pairs={{0,24},{2,26},{4,28},{6,30},{8,0},{10,2},{12,4},{14,6},{16,8},{18,... | collective-permute-start | bytes 393224 | tf_op jit(solution)/shard_map/ppermute | solution.py:51
  37.2 6.3 %collective-permute-start.3 = (f32[1,32,4,256]{3,1,2,0:T(8,128)S(1)}, f32[1,32,4,256]{3,1,2,0:T(8,128)S(1)}, u32[]{:S(2)}, u32[]{:S(2)}) collective-permute-start(f32[1,32,4,256]{3,1,2,0:T(8,128)S(1)} %add.289), channel_id=1, source_target_pairs={{0,8},{2,10},{4,12},{6,14},{8,16},{10,18},{12,20},{14,22},{16,24},... | collective-permute-start | bytes 393224 | tf_op jit(solution)/shard_map/ppermute | solution.py:50
  40.6 6.6 %collective-permute-start.11 = (f32[1,32,4,256]{3,1,2,0:T(8,128)S(1)}, f32[1,32,4,256]{3,1,2,0:T(8,128)S(1)}, u32[]{:S(2)}, u32[]{:S(2)}) collective-permute-start(f32[1,32,4,256]{3,1,2,0:T(8,128)S(1)} %add.297), channel_id=1, source_target_pairs={{0,16},{2,18},{4,20},{6,22},{8,24},{10,26},{12,28},{14,30},{16,0},... | collective-permute-start | bytes 393224 | tf_op jit(solution)/shard_map/ppermute | solution.py:51
  43.6 6.6 %collective-permute-start.4 = (f32[1,32,4,256]{3,1,2,0:T(8,128)S(1)}, f32[1,32,4,256]{3,1,2,0:T(8,128)S(1)}, u32[]{:S(2)}, u32[]{:S(2)}) collective-permute-start(f32[1,32,4,256]{3,1,2,0:T(8,128)S(1)} %add.290), channel_id=1, source_target_pairs={{0,16},{2,18},{4,20},{6,22},{8,24},{10,26},{12,28},{14,30},{16,0},... | collective-permute-start | bytes 393224 | tf_op jit(solution)/shard_map/ppermute | solution.py:50
  45.4 6.1 %collective-permute-start.14 = (bf16[1,128]{1,0:T(2,128)(2,1)S(1)}, bf16[1,128]{1,0:T(2,128)(2,1)S(1)}, u32[]{:S(2)}, u32[]{:S(2)}) collective-permute-start(bf16[1,128]{1,0:T(2,128)(2,1)S(1)} %copy-done.5), channel_id=1, source_target_pairs={{0,1},{1,0},{2,3},{3,2},{4,5},{5,4},{6,7},{7,6},{8,9},{9,8},{10,11... | collective-permute-start | bytes 776 | tf_op jit(solution)/shard_map/ppermute | solution.py:118
  45.4 14.3 %collective-permute-start.15 = (bf16[1,9,128,128]{3,2,1,0:T(8,128)(2,1)S(1)}, bf16[1,9,128,128]{3,2,1,0:T(8,128)(2,1)S(1)}, u32[]{:S(2)}, u32[]{:S(2)}) collective-permute-start(bf16[1,9,128,128]{3,2,1,0:T(8,128)(2,1)S(1)} %copy-done.1), channel_id=1, source_target_pairs={{0,1},{1,0},{2,3},{3,2},{4,5},{5,4},{6,7},{7,6},{8,9},{9,8},{10,11... | collective-permute-start | bytes 884744 | tf_op jit(solution)/shard_map/ppermute | solution.py:117
  47.3 5.0 %collective-permute-start.12 = (f32[1,32,4,256]{3,1,2,0:T(8,128)S(1)}, f32[1,32,4,256]{3,1,2,0:T(8,128)S(1)}, u32[]{:S(2)}, u32[]{:S(2)}) collective-permute-start(f32[1,32,4,256]{3,1,2,0:T(8,128)S(1)} %add.298), channel_id=1, source_target_pairs={{0,6},{2,0},{4,2},{6,4},{8,14},{10,8},{12,10},{14,12},{16,22},{18,... | collective-permute-start | bytes 393224 | tf_op jit(solution)/shard_map/ppermute | solution.py:51
  50.2 9.3 %collective-permute-start.5 = (f32[1,32,4,256]{3,1,2,0:T(8,128)S(1)}, f32[1,32,4,256]{3,1,2,0:T(8,128)S(1)}, u32[]{:S(2)}, u32[]{:S(2)}) collective-permute-start(f32[1,32,4,256]{3,1,2,0:T(8,128)S(1)} %add.291), channel_id=1, source_target_pairs={{0,2},{2,4},{4,6},{6,0},{8,10},{10,12},{12,14},{14,8},{16,18},{18,... | collective-permute-start | bytes 393224 | tf_op jit(solution)/shard_map/ppermute | solution.py:50
  52.4 7.4 %collective-permute-start.13 = (f32[1,32,4,256]{3,1,2,0:T(8,128)S(1)}, f32[1,32,4,256]{3,1,2,0:T(8,128)S(1)}, u32[]{:S(2)}, u32[]{:S(2)}) collective-permute-start(f32[1,32,4,256]{3,1,2,0:T(8,128)S(1)} %add.299), channel_id=1, source_target_pairs={{0,4},{2,6},{4,0},{6,2},{8,12},{10,14},{12,8},{14,10},{16,20},{18,... | collective-permute-start | bytes 393224 | tf_op jit(solution)/shard_map/ppermute | solution.py:51
  59.4 6.8 %copy-start.2 = (f32[8,128]{1,0:T(8,128)S(1)}, f32[8,128]{1,0:T(8,128)}, u32[]{:S(2)}) copy-start(f32[8,128]{1,0:T(8,128)} %param.17) | copy-start | bytes 12292
  59.4 7.4 %copy-start.6 = (f32[128,4]{0,1:T(4,128)S(1)}, f32[128,4]{0,1:T(4,128)}, u32[]{:S(2)}) copy-start(f32[128,4]{0,1:T(4,128)} %param.21) | copy-start | bytes 6148
  59.5 7.4 %copy-start.7 = (f32[128]{0:T(128)S(1)}, f32[128]{0:T(128)}, u32[]{:S(2)}) copy-start(f32[128]{0:T(128)} %param.18) | copy-start | bytes 1540
  59.5 6.7 %collective-permute-start.6 = (f32[1,32,4,256]{3,1,2,0:T(8,128)S(1)}, f32[1,32,4,256]{3,1,2,0:T(8,128)S(1)}, u32[]{:S(2)}, u32[]{:S(2)}) collective-permute-start(f32[1,32,4,256]{3,1,2,0:T(8,128)S(1)} %add.292), channel_id=1, source_target_pairs={{0,4},{2,6},{4,0},{6,2},{8,12},{10,14},{12,8},{14,10},{16,20},{18,... | collective-permute-start | bytes 393224 | tf_op jit(solution)/shard_map/ppermute | solution.py:50

commit v2 on v1

v2 whole, which is shorter than its diff:
```python
import numpy as np
import jax
import jax.numpy as jnp
from jax import lax
from jax.sharding import PartitionSpec as P
from jax.experimental import pallas as pl
from jax.experimental.pallas import tpu as pltpu

SIDE = 16
HOURS = 4
STEPS = 8


EPSILON = 1e-06
DATA_VAR = 0.25


def ring_routes(mesh):
    devices = np.asarray(mesh.devices)[:, 0]
    coords = [tuple(d.coords[:3]) for d in devices]
    where = {c: i for i, c in enumerate(coords)}
    sizes = [len({c[a] for c in coords}) for a in range(3)]

    def shift_pairs(axis, distance):
        n = sizes[axis]
        pairs = []
        for i, c in enumerate(coords):
            moved = list(c)
            moved[axis] = (c[axis] + distance) % n
            pairs.append((i, where[tuple(moved)]))
        return tuple(pairs)

    stages = []
    for axis in sorted(range(3), key=lambda a: sizes[a]):
        n = sizes[axis]
        if n == 1:
            continue
        if n & (n - 1):
            raise ValueError("ring size")
        if n == 2:
            stages.append((shift_pairs(axis, 1),))
            continue
        stages.append(tuple(shift_pairs(axis, d) for d in (1, -1, 2)))
        distance = 4
        while distance < n:
            stages.append((shift_pairs(axis, distance),))
            distance *= 2
    return stages


def broadcast_sum(block, stages):
    for stage in stages:
        arrived = [lax.ppermute(block, "member", pairs) for pairs in stage]
        for part in arrived:
            block = block + part
    return block


def rms_scale(values):
    return values * lax.rsqrt(jnp.mean(values * values, axis=-1, keepdims=True) + EPSILON)


def silu(values):
    return values / (1.0 + jnp.exp(-values))


def chain_kernel(coef_ref, state_ref, means_ref, lift_ref, embed_ref, conv_ref, gain_ref, out_ref, result_ref):
    rows, lanes = state_ref.shape
    pixel = lax.broadcasted_iota(jnp.int32, (rows, lanes), 0) % (SIDE * SIDE)
    row = pixel // SIDE
    col = pixel % SIDE
    offsets = [(a, b) for a in (-1, 0, 1) for b in (-1, 0, 1)]
    valid = [
        (row + a >= 0) & (row + a < SIDE) & (col + b >= 0) & (col + b < SIDE) for a, b in offsets
    ]

    def conv(gated, index):
        windows = []
        for (a, b), keep in zip(offsets, valid):
            distance = a * SIDE + b
            moved = gated if distance == 0 else pltpu.roll(gated, (-distance) % rows, 0)
            windows.append(jnp.where(keep, moved, 0.0).astype(jnp.bfloat16))
        stacked = jnp.concatenate(windows, axis=1)
        return jnp.dot(stacked, conv_ref[index], preferred_element_type=jnp.float32)

    means = means_ref[...]
    embed = embed_ref[...]
    gain_enc = gain_ref[0:1, :]
    gain_dec = gain_ref[1:2, :]

    def one_step(step, state):
        scale_in = coef_ref[step * 5 + 0]
        level = coef_ref[step * 5 + 1]
        keep_state = coef_ref[step * 5 + 2]
        keep_net = coef_ref[step * 5 + 3]
        move = coef_ref[step * 5 + 4]
        inputs = state * scale_in + means
        lifted = jnp.dot(
            inputs, lift_ref[...], precision=lax.Precision.HIGHEST, preferred_element_type=jnp.float32
        )
        lifted = lifted + level * embed
        gated = silu(rms_scale(lifted) * gain_enc)
        encoded = (lifted + conv(gated, 0)).astype(jnp.bfloat16).astype(jnp.float32)
        gated = silu(rms_scale(encoded) * gain_dec)
        skipped = lifted.astype(jnp.bfloat16).astype(jnp.float32)
        merged = encoded + conv(gated, 1) + skipped
        net_out = jnp.dot(
            silu(rms_scale(merged)),
            out_ref[...],
            precision=lax.Precision.HIGHEST,
            preferred_element_type=jnp.float32,
        )
        denoised = keep_state * state + keep_net * net_out
        return state + move * (state - denoised)

    result_ref[...] = lax.fori_loop(0, STEPS, one_step, state_ref[...])


def run_chain(coefs, state, means, lift, embed, kernels, gains, out_weight):
    vmem = pltpu.MemorySpace.VMEM
    return pl.pallas_call(
        chain_kernel,
        out_shape=jax.ShapeDtypeStruct(state.shape, jnp.float32),
        in_specs=[pl.BlockSpec(memory_space=pltpu.MemorySpace.SMEM)]
        + [pl.BlockSpec(memory_space=vmem)] * 7,
        out_specs=pl.BlockSpec(memory_space=vmem),
    )(coefs, state, means, lift, embed, kernels, gains, out_weight)


def step_coefficients(sigmas):
    sigma_now = sigmas[:-1]
    sigma_next = sigmas[1:]
    spread = sigma_now * sigma_now + DATA_VAR
    return jnp.stack(
        [
            lax.rsqrt(spread),
            jnp.log(sigma_now) / 4.0,
            DATA_VAR / spread,
            0.5 * sigma_now * lax.rsqrt(spread),
            (sigma_next - sigma_now) / sigma_now,
        ],
        axis=1,
    ).reshape(-1)


def to_lanes(fields, first_lane, lanes):
    batched, variables, pixels = fields.shape
    flat = jnp.transpose(fields, (0, 2, 1)).reshape(batched * pixels, variables)
    return jnp.pad(flat, ((0, 0), (first_lane, lanes - first_lane - variables)))


def make_body(routes):
    def body(
        start_noise,
        reg_means,
        hour_owner,
        member_tile,
        sigmas,
        lift_weight,
        noise_embed,
        section_conv,
        section_gain,
        out_weight,
    ):
        segment_index = lax.axis_index("segment")
        is_first = segment_index == 0
        half_hours = HOURS // lax.axis_size("segment")
        first_hour = segment_index * half_hours
        variables = start_noise.shape[2]
        pixels = start_noise.shape[3]
        channels = section_conv.shape[-1]

        swap = [(0, 1), (1, 0)]
        other_conv = lax.ppermute(section_conv, "segment", swap)
        other_gain = lax.ppermute(section_gain, "segment", swap)
        kernels = jnp.stack(
            [
                jnp.where(is_first, section_conv[0], other_conv[0]),
                jnp.where(is_first, other_conv[0], section_conv[0]),
            ]
        ).reshape(2, 9 * channels, channels)
        gains = jnp.stack(
            [
                jnp.where(is_first, section_gain[0], other_gain[0]),
                jnp.where(is_first, other_gain[0], section_gain[0]),
            ]
        ).astype(jnp.float32)

        owners = lax.dynamic_slice_in_dim(hour_owner, first_hour, half_hours, 0)
        mine = lax.dynamic_slice_in_dim(reg_means[0], first_hour, half_hours, 0)
        is_owner = lax.axis_index("member") == owners
        kept = jnp.where(is_owner[:, None, None, None], mine, 0).astype(mine.dtype)
        arrived = broadcast_sum(kept, routes)
        means = lax.dynamic_index_in_dim(arrived, member_tile[0], 1, keepdims=False)

        noise = lax.dynamic_slice_in_dim(start_noise[0], first_hour, half_hours, 0)
        states = sigmas[0] * noise
        lift = jnp.pad(lift_weight, ((0, channels - 2 * variables), (0, 0)))
        out_pad = jnp.pad(out_weight, ((0, 0), (0, channels - variables)))
        finished = run_chain(
            step_coefficients(sigmas),
            to_lanes(states, 0, channels),
            to_lanes(means, variables, channels),
            lift,
            noise_embed[None, :],
            kernels,
            gains,
            out_pad,
        )
        finished = finished[:, :variables].reshape(half_hours, pixels, variables)
        return (means + jnp.transpose(finished, (0, 2, 1)))[:, None]

    return body


def solution(mesh):
    placed = (
        P("member", None, None, None),
        P("member", None, None, None, None),
        P(),
        P("member"),
        P(),
        P(),
        P(),
        P("segment", None, None, None),
        P("segment", None),
        P(),
    )
    return jax.shard_map(
        make_body(ring_routes(mesh)),
        mesh=mesh,
        in_specs=placed,
        out_specs=P("segment", "member", None, None),
        check_vma=False,
    )
```

time: 144 us -> 104 us (0.72)
  the two profiles are of different devices: /device:TPU:16 before, /device:TPU:32 now
where the time goes in v2:
time: 104 us
  waiting for transfers between devices  36.9 us (35%)
  starting transfers between devices  30.3 us (29%)
  Pallas kernels  25.9 us (25%)
  local copies, waits for them, and re-layouts  7.33 us (7%)
  other arithmetic  2.69 us (3%)
    ppermute x10, waiting for transfers between devices, broadcast_sum(): arrived = [lax.ppermute(block, 'member', pairs) for pairs in stage]  36.9 us
    ppermute x10, starting transfers between devices, broadcast_sum(): arrived = [lax.ppermute(block, 'member', pairs) for pairs in stage]  29.8 us
    pallas_call x1, Pallas kernels, run_chain(): pl.pallas_call(chain_kernel, out_shape=jax.ShapeDtypeStruct(state.shape,...  25.9 us
    unnamed x18, local copies, waits for them, and re-layouts  2.38 us
  transfers between devices with their start and end apart: 12, of which 9 were waited for; matrix products, arithmetic and copies ran while one was open for 5% of the time, Pallas kernels for 0%

profile of v2, /device:TPU:32, one launch (start us, length us, event | category | flops | bytes accessed | tf_op | source)
XLA Modules:
  0.0 103.9 jit_solution(17811997048562046535)
XLA Ops:
  0.0 1.0 %copy-done = f32[1,4,32,4,256]{4,3,2,1,0:T(4,128)S(1)} copy-done((f32[1,4,32,4,256]{4,3,2,1,0:T(4,128)S(1)}, f32[1,4,32,4,256]{4,3,2,1,0:T(4,128)}, u32[]{:S(2)}) %copy-start) | copy-done | bytes 524312
  1.1 0.6 copy-done.7
  1.7 0.1 dynamic-slice_compare_fusion
  1.8 0.1 fusion
  1.9 1.6 %collective-permute-start = (f32[2,32,4,256]{3,1,2,0:T(8,128)S(1)}, f32[2,32,4,256]{3,1,2,0:T(8,128)S(1)}, u32[]{:S(2)}, u32[]{:S(2)}) collective-permute-start(f32[2,32,4,256]{3,1,2,0:T(8,128)S(1)} %fusion), channel_id=1, source_target_pairs={{0,8},{2,10},{4,12},{6,14},{8,16},{10,18},{12,20},{14,22},{16,24},... | collective-permute-start | bytes 786440 | tf_op jit(solution)/shard_map/ppermute | solution.py:53
  3.4 1.7 %collective-permute-start.1 = (f32[2,32,4,256]{3,1,2,0:T(8,128)S(1)}, f32[2,32,4,256]{3,1,2,0:T(8,128)S(1)}, u32[]{:S(2)}, u32[]{:S(2)}) collective-permute-start(f32[2,32,4,256]{3,1,2,0:T(8,128)S(1)} %fusion), channel_id=1, source_target_pairs={{0,24},{2,26},{4,28},{6,30},{8,0},{10,2},{12,4},{14,6},{16,8},{18,... | collective-permute-start | bytes 786440 | tf_op jit(solution)/shard_map/ppermute | solution.py:53
  5.2 1.8 %collective-permute-start.2 = (f32[2,32,4,256]{3,1,2,0:T(8,128)S(1)}, f32[2,32,4,256]{3,1,2,0:T(8,128)S(1)}, u32[]{:S(2)}, u32[]{:S(2)}) collective-permute-start(f32[2,32,4,256]{3,1,2,0:T(8,128)S(1)} %fusion), channel_id=1, source_target_pairs={{0,16},{2,18},{4,20},{6,22},{8,24},{10,26},{12,28},{14,30},{16,0},... | collective-permute-start | bytes 786440 | tf_op jit(solution)/shard_map/ppermute | solution.py:53
  7.0 0.0 collective-permute-start.10
  7.0 0.5 collective-permute-start.11
  8.2 3.2 %collective-permute-done = f32[2,32,4,256]{3,1,2,0:T(8,128)S(1)} collective-permute-done((f32[2,32,4,256]{3,1,2,0:T(8,128)S(1)}, f32[2,32,4,256]{3,1,2,0:T(8,128)S(1)}, u32[]{:S(2)}, u32[]{:S(2)}) %collective-permute-start) | collective-permute-done | bytes 262176 | tf_op jit(solution)/shard_map/ppermute | solution.py:53
  11.4 4.8 %collective-permute-done.1 = f32[2,32,4,256]{3,1,2,0:T(8,128)S(1)} collective-permute-done((f32[2,32,4,256]{3,1,2,0:T(8,128)S(1)}, f32[2,32,4,256]{3,1,2,0:T(8,128)S(1)}, u32[]{:S(2)}, u32[]{:S(2)}) %collective-permute-start.1) | collective-permute-done | bytes 262176 | tf_op jit(solution)/shard_map/ppermute | solution.py:53
  16.1 1.7 %collective-permute-done.2 = f32[2,32,4,256]{3,1,2,0:T(8,128)S(1)} collective-permute-done((f32[2,32,4,256]{3,1,2,0:T(8,128)S(1)}, f32[2,32,4,256]{3,1,2,0:T(8,128)S(1)}, u32[]{:S(2)}, u32[]{:S(2)}) %collective-permute-start.2) | collective-permute-done | bytes 262176 | tf_op jit(solution)/shard_map/ppermute | solution.py:53
  17.8 0.1 add_add_fusion.2
  18.0 1.7 %collective-permute-start.3 = (f32[2,32,4,256]{3,1,2,0:T(8,128)S(1)}, f32[2,32,4,256]{3,1,2,0:T(8,128)S(1)}, u32[]{:S(2)}, u32[]{:S(2)}) collective-permute-start(f32[2,32,4,256]{3,1,2,0:T(8,128)S(1)} %add_add_fusion.2), channel_id=1, source_target_pairs={{0,2},{2,4},{4,6},{6,0},{8,10},{10,12},{12,14},{14,8},{16,18},{18,... | collective-permute-start | bytes 786440 | tf_op jit(solution)/shard_map/ppermute | solution.py:53
  19.6 1.7 %collective-permute-start.4 = (f32[2,32,4,256]{3,1,2,0:T(8,128)S(1)}, f32[2,32,4,256]{3,1,2,0:T(8,128)S(1)}, u32[]{:S(2)}, u32[]{:S(2)}) collective-permute-start(f32[2,32,4,256]{3,1,2,0:T(8,128)S(1)} %add_add_fusion.2), channel_id=1, source_target_pairs={{0,6},{2,0},{4,2},{6,4},{8,14},{10,8},{12,10},{14,12},{16,22},{18,... | collective-permute-start | bytes 786440 | tf_op jit(solution)/shard_map/ppermute | solution.py:53
  21.3 2.0 %collective-permute-start.5 = (f32[2,32,4,256]{3,1,2,0:T(8,128)S(1)}, f32[2,32,4,256]{3,1,2,0:T(8,128)S(1)}, u32[]{:S(2)}, u32[]{:S(2)}) collective-permute-start(f32[2,32,4,256]{3,1,2,0:T(8,128)S(1)} %add_add_fusion.2), channel_id=1, source_target_pairs={{0,4},{2,6},{4,0},{6,2},{8,12},{10,14},{12,8},{14,10},{16,20},{18,... | collective-permute-start | bytes 786440 | tf_op jit(solution)/shard_map/ppermute | solution.py:53
  23.3 0.1 fusion.2
  23.4 0.1 copy.17
  23.4 0.6 reshape.20.coef_ref
  24.1 0.0 copy-start.5
  24.2 0.1 copy.18
  24.3 0.5 copy-done.5
  24.8 0.1 copy.20
  24.9 0.7 pad.16.state_ref
  25.7 0.6 pad.19.out_ref
  26.3 0.0 copy-done.3
  26.3 0.6 pad.18.lift_ref
  27.0 0.3 collective-permute-done.3
  27.3 4.2 %collective-permute-done.4 = f32[2,32,4,256]{3,1,2,0:T(8,128)S(1)} collective-permute-done((f32[2,32,4,256]{3,1,2,0:T(8,128)S(1)}, f32[2,32,4,256]{3,1,2,0:T(8,128)S(1)}, u32[]{:S(2)}, u32[]{:S(2)}) %collective-permute-start.4) | collective-permute-done | bytes 262176 | tf_op jit(solution)/shard_map/ppermute | solution.py:53
  31.5 1.8 %collective-permute-done.5 = f32[2,32,4,256]{3,1,2,0:T(8,128)S(1)} collective-permute-done((f32[2,32,4,256]{3,1,2,0:T(8,128)S(1)}, f32[2,32,4,256]{3,1,2,0:T(8,128)S(1)}, u32[]{:S(2)}, u32[]{:S(2)}) %collective-permute-start.5) | collective-permute-done | bytes 262176 | tf_op jit(solution)/shard_map/ppermute | solution.py:53
  33.3 0.1 add_add_fusion.1
  33.4 2.0 %collective-permute-start.6 = (f32[2,32,4,256]{3,1,2,0:T(8,128)S(1)}, f32[2,32,4,256]{3,1,2,0:T(8,128)S(1)}, u32[]{:S(2)}, u32[]{:S(2)}) collective-permute-start(f32[2,32,4,256]{3,1,2,0:T(8,128)S(1)} %add_add_fusion.1), channel_id=1, source_target_pairs={{0,32},{2,34},{4,36},{6,38},{8,40},{10,42},{12,44},{14,46},{16,48}... | collective-permute-start | bytes 786440 | tf_op jit(solution)/shard_map/ppermute | solution.py:53
  35.4 0.1 collective-permute-start.7
  35.5 4.4 %collective-permute-start.8 = (f32[2,32,4,256]{3,1,2,0:T(8,128)S(1)}, f32[2,32,4,256]{3,1,2,0:T(8,128)S(1)}, u32[]{:S(2)}, u32[]{:S(2)}) collective-permute-start(f32[2,32,4,256]{3,1,2,0:T(8,128)S(1)} %add_add_fusion.1), channel_id=1, source_target_pairs={{0,64},{2,66},{4,68},{6,70},{8,72},{10,74},{12,76},{14,78},{16,80}... | collective-permute-start | bytes 786440 | tf_op jit(solution)/shard_map/ppermute | solution.py:53
  39.8 0.0 collective-permute-done.11
  39.9 0.6 maximum_convert_fusion.gain_ref
  40.4 4.9 %collective-permute-done.6 = f32[2,32,4,256]{3,1,2,0:T(8,128)S(1)} collective-permute-done((f32[2,32,4,256]{3,1,2,0:T(8,128)S(1)}, f32[2,32,4,256]{3,1,2,0:T(8,128)S(1)}, u32[]{:S(2)}, u32[]{:S(2)}) %collective-permute-start.6) | collective-permute-done | bytes 262176 | tf_op jit(solution)/shard_map/ppermute | solution.py:53
  45.3 0.0 collective-permute-done.7
  45.3 9.8 %collective-permute-done.8 = f32[2,32,4,256]{3,1,2,0:T(8,128)S(1)} collective-permute-done((f32[2,32,4,256]{3,1,2,0:T(8,128)S(1)}, f32[2,32,4,256]{3,1,2,0:T(8,128)S(1)}, u32[]{:S(2)}, u32[]{:S(2)}) %collective-permute-start.8) | collective-permute-done | bytes 262176 | tf_op jit(solution)/shard_map/ppermute | solution.py:53
  55.1 0.1 add_add_fusion
  55.2 12.9 %collective-permute-start.9 = (f32[2,32,4,256]{3,1,2,0:T(8,128)S(1)}, f32[2,32,4,256]{3,1,2,0:T(8,128)S(1)}, u32[]{:S(2)}, u32[]{:S(2)}) collective-permute-start(f32[2,32,4,256]{3,1,2,0:T(8,128)S(1)} %add_add_fusion), channel_id=1, source_target_pairs={{0,128},{2,130},{4,132},{6,134},{8,136},{10,138},{12,140},{14,142}... | collective-permute-start | bytes 786440 | tf_op jit(solution)/shard_map/ppermute | solution.py:53
  68.2 0.9 pad_maximum_fusion.conv_ref
  69.0 6.2 %collective-permute-done.9 = f32[2,32,4,256]{3,1,2,0:T(8,128)S(1)} collective-permute-done((f32[2,32,4,256]{3,1,2,0:T(8,128)S(1)}, f32[2,32,4,256]{3,1,2,0:T(8,128)S(1)}, u32[]{:S(2)}, u32[]{:S(2)}) %collective-permute-start.9) | collective-permute-done | bytes 262176 | tf_op jit(solution)/shard_map/ppermute | solution.py:53
  75.3 0.1 copy.19
  75.5 0.9 pad.17.means_ref
  76.3 25.9 %shard_map.100 = f32[512,128]{1,0:T(8,128)} custom-call(f32[40]{0:T(128)} %reshape.20.coef_ref, f32[512,128]{1,0:T(8,128)} %pad.16.state_ref, f32[512,128]{1,0:T(8,128)} %pad.17.means_ref, f32[128,128]{1,0:T(8,128)} %pad.18.lift_ref, f32[1,128]{1,0:T(1,128)} %bitcast.52, bf16[2,1152,128]{2,1,0:T(8,128)(2,1)} %pad_maximum_fusion.conv_ref, ...), custom_call_target="tpu_custom_call" | custom-call | tf_op jit(solution)/shard_map/pallas_call | solution.py:121
  102.2 1.1 %copy.21 = f32[2,256,4]{1,2,0:T(4,128)S(1)} copy(f32[2,256,4]{2,1,0:T(8,128)} %bitcast.49) | data formatting | bytes 16384 | tf_op jit(solution)/shard_map/reshape | solution.py:210
  103.3 0.6 fusion.1
  (19 shorter events, 0.2 us)
Async XLA Ops:
  0.0 1.0 %copy-start = (f32[1,4,32,4,256]{4,3,2,1,0:T(4,128)S(1)}, f32[1,4,32,4,256]{4,3,2,1,0:T(4,128)}, u32[]{:S(2)}) copy-start(f32[1,4,32,4,256]{4,3,2,1,0:T(4,128)} %param.11) | copy-start | bytes 1572868
  1.0 0.7 copy-start.7
  1.7 5.3 %copy-start.1 = (bf16[1,9,128,128]{3,2,1,0:T(8,128)(2,1)S(1)}, bf16[1,9,128,128]{3,2,1,0:T(8,128)(2,1)}, u32[]{:S(2)}) copy-start(bf16[1,9,128,128]{3,2,1,0:T(8,128)(2,1)} %param.17) | copy-start | bytes 884740
  1.8 5.2 %copy-start.6 = (bf16[1,128]{1,0:T(2,128)(2,1)S(1)}, bf16[1,128]{1,0:T(2,128)(2,1)}, u32[]{:S(2)}) copy-start(bf16[1,128]{1,0:T(2,128)(2,1)} %param.18) | copy-start | bytes 772
  1.9 9.5 %collective-permute-start = (f32[2,32,4,256]{3,1,2,0:T(8,128)S(1)}, f32[2,32,4,256]{3,1,2,0:T(8,128)S(1)}, u32[]{:S(2)}, u32[]{:S(2)}) collective-permute-start(f32[2,32,4,256]{3,1,2,0:T(8,128)S(1)} %fusion), channel_id=1, source_target_pairs={{0,8},{2,10},{4,12},{6,14},{8,16},{10,18},{12,20},{14,22},{16,24},... | collective-permute-start | bytes 786440 | tf_op jit(solution)/shard_map/ppermute | solution.py:53
  3.4 12.7 %collective-permute-start.1 = (f32[2,32,4,256]{3,1,2,0:T(8,128)S(1)}, f32[2,32,4,256]{3,1,2,0:T(8,128)S(1)}, u32[]{:S(2)}, u32[]{:S(2)}) collective-permute-start(f32[2,32,4,256]{3,1,2,0:T(8,128)S(1)} %fusion), channel_id=1, source_target_pairs={{0,24},{2,26},{4,28},{6,30},{8,0},{10,2},{12,4},{14,6},{16,8},{18,... | collective-permute-start | bytes 786440 | tf_op jit(solution)/shard_map/ppermute | solution.py:53
  5.2 12.6 %collective-permute-start.2 = (f32[2,32,4,256]{3,1,2,0:T(8,128)S(1)}, f32[2,32,4,256]{3,1,2,0:T(8,128)S(1)}, u32[]{:S(2)}, u32[]{:S(2)}) collective-permute-start(f32[2,32,4,256]{3,1,2,0:T(8,128)S(1)} %fusion), channel_id=1, source_target_pairs={{0,16},{2,18},{4,20},{6,22},{8,24},{10,26},{12,28},{14,30},{16,0},... | collective-permute-start | bytes 786440 | tf_op jit(solution)/shard_map/ppermute | solution.py:53
  7.0 61.1 %collective-permute-start.10 = (bf16[1,9,128,128]{3,2,1,0:T(8,128)(2,1)S(1)}, bf16[1,9,128,128]{3,2,1,0:T(8,128)(2,1)S(1)}, u32[]{:S(2)}, u32[]{:S(2)}) collective-permute-start(bf16[1,9,128,128]{3,2,1,0:T(8,128)(2,1)S(1)} %copy-done.1), channel_id=1, source_target_pairs={{0,1},{1,0},{2,3},{3,2},{4,5},{5,4},{6,7},{7,6},{8,9},{9,8},{10,11... | collective-permute-start | bytes 884744 | tf_op jit(solution)/shard_map/ppermute | solution.py:174
  7.0 32.8 %collective-permute-start.11 = (bf16[1,128]{1,0:T(2,128)(2,1)S(1)}, bf16[1,128]{1,0:T(2,128)(2,1)S(1)}, u32[]{:S(2)}, u32[]{:S(2)}) collective-permute-start(bf16[1,128]{1,0:T(2,128)(2,1)S(1)} %copy-done.6), channel_id=1, source_target_pairs={{0,1},{1,0},{2,3},{3,2},{4,5},{5,4},{6,7},{7,6},{8,9},{9,8},{10,11... | collective-permute-start | bytes 776 | tf_op jit(solution)/shard_map/ppermute | solution.py:175
  17.8 5.4 %copy-start.2 = (f32[9]{0:T(128)S(1)}, f32[9]{0:T(128)}, u32[]{:S(2)}) copy-start(f32[9]{0:T(128)} %param.14) | copy-start | bytes 112
  18.0 9.3 %collective-permute-start.3 = (f32[2,32,4,256]{3,1,2,0:T(8,128)S(1)}, f32[2,32,4,256]{3,1,2,0:T(8,128)S(1)}, u32[]{:S(2)}, u32[]{:S(2)}) collective-permute-start(f32[2,32,4,256]{3,1,2,0:T(8,128)S(1)} %add_add_fusion.2), channel_id=1, source_target_pairs={{0,2},{2,4},{4,6},{6,0},{8,10},{10,12},{12,14},{14,8},{16,18},{18,... | collective-permute-start | bytes 786440 | tf_op jit(solution)/shard_map/ppermute | solution.py:53
  19.6 11.9 %collective-permute-start.4 = (f32[2,32,4,256]{3,1,2,0:T(8,128)S(1)}, f32[2,32,4,256]{3,1,2,0:T(8,128)S(1)}, u32[]{:S(2)}, u32[]{:S(2)}) collective-permute-start(f32[2,32,4,256]{3,1,2,0:T(8,128)S(1)} %add_add_fusion.2), channel_id=1, source_target_pairs={{0,6},{2,0},{4,2},{6,4},{8,14},{10,8},{12,10},{14,12},{16,22},{18,... | collective-permute-start | bytes 786440 | tf_op jit(solution)/shard_map/ppermute | solution.py:53
  21.3 12.0 %collective-permute-start.5 = (f32[2,32,4,256]{3,1,2,0:T(8,128)S(1)}, f32[2,32,4,256]{3,1,2,0:T(8,128)S(1)}, u32[]{:S(2)}, u32[]{:S(2)}) collective-permute-start(f32[2,32,4,256]{3,1,2,0:T(8,128)S(1)} %add_add_fusion.2), channel_id=1, source_target_pairs={{0,4},{2,6},{4,0},{6,2},{8,12},{10,14},{12,8},{14,10},{16,20},{18,... | collective-permute-start | bytes 786440 | tf_op jit(solution)/shard_map/ppermute | solution.py:53
  23.3 0.8 copy-start.4
  24.1 0.7 copy-start.5
  25.7 0.7 copy-start.3
  33.4 12.0 %collective-permute-start.6 = (f32[2,32,4,256]{3,1,2,0:T(8,128)S(1)}, f32[2,32,4,256]{3,1,2,0:T(8,128)S(1)}, u32[]{:S(2)}, u32[]{:S(2)}) collective-permute-start(f32[2,32,4,256]{3,1,2,0:T(8,128)S(1)} %add_add_fusion.1), channel_id=1, source_target_pairs={{0,32},{2,34},{4,36},{6,38},{8,40},{10,42},{12,44},{14,46},{16,48}... | collective-permute-start | bytes 786440 | tf_op jit(solution)/shard_map/ppermute | solution.py:53
  35.4 10.0 %collective-permute-start.7 = (f32[2,32,4,256]{3,1,2,0:T(8,128)S(1)}, f32[2,32,4,256]{3,1,2,0:T(8,128)S(1)}, u32[]{:S(2)}, u32[]{:S(2)}) collective-permute-start(f32[2,32,4,256]{3,1,2,0:T(8,128)S(1)} %add_add_fusion.1), channel_id=1, source_target_pairs={{0,224},{2,226},{4,228},{6,230},{8,232},{10,234},{12,236},{14,238}... | collective-permute-start | bytes 786440 | tf_op jit(solution)/shard_map/ppermute | solution.py:53
  35.5 19.7 %collective-permute-start.8 = (f32[2,32,4,256]{3,1,2,0:T(8,128)S(1)}, f32[2,32,4,256]{3,1,2,0:T(8,128)S(1)}, u32[]{:S(2)}, u32[]{:S(2)}) collective-permute-start(f32[2,32,4,256]{3,1,2,0:T(8,128)S(1)} %add_add_fusion.1), channel_id=1, source_target_pairs={{0,64},{2,66},{4,68},{6,70},{8,72},{10,74},{12,76},{14,78},{16,80}... | collective-permute-start | bytes 786440 | tf_op jit(solution)/shard_map/ppermute | solution.py:53
  55.2 20.1 %collective-permute-start.9 = (f32[2,32,4,256]{3,1,2,0:T(8,128)S(1)}, f32[2,32,4,256]{3,1,2,0:T(8,128)S(1)}, u32[]{:S(2)}, u32[]{:S(2)}) collective-permute-start(f32[2,32,4,256]{3,1,2,0:T(8,128)S(1)} %add_add_fusion), channel_id=1, source_target_pairs={{0,128},{2,130},{4,132},{6,134},{8,136},{10,138},{12,140},{14,142}... | collective-permute-start | bytes 786440 | tf_op jit(solution)/shard_map/ppermute | solution.py:53

commit v3 on v2

--- a/solution.py
+++ b/solution.py
@@ -20,40 +20,85 @@
     coords = [tuple(d.coords[:3]) for d in devices]
     where = {c: i for i, c in enumerate(coords)}
     sizes = [len({c[a] for c in coords}) for a in range(3)]
+    axes = [a for a in sorted(range(3), key=lambda a: sizes[a]) if sizes[a] > 1]
 
     def shift_pairs(axis, distance):
-        n = sizes[axis]
         pairs = []
         for i, c in enumerate(coords):
             moved = list(c)
-            moved[axis] = (c[axis] + distance) % n
+            moved[axis] = (c[axis] + distance) % sizes[axis]
             pairs.append((i, where[tuple(moved)]))
         return tuple(pairs)
 
-    stages = []
-    for axis in sorted(range(3), key=lambda a: sizes[a]):
+    rings = []
+    for axis in axes:
         n = sizes[axis]
-        if n == 1:
-            continue
-        if n & (n - 1):
-            raise ValueError("ring size")
-        if n == 2:
-            stages.append((shift_pairs(axis, 1),))
-            continue
-        stages.append(tuple(shift_pairs(axis, d) for d in (1, -1, 2)))
-        distance = 4
-        while distance < n:
-            stages.append((shift_pairs(axis, distance),))
-            distance *= 2
+        shifts = {d: shift_pairs(axis, d) for d in range(-n + 1, n) if d}
+        position = tuple(c[axis] for c in coords)
+        rings.append((n, shifts, position))
+    return rings
+
+
+def window_stages(n):
+    if n & (n - 1):
+        raise ValueError("ring size")
+    if n == 2:
+        return [(1,)]
+    stages = [(1, -1, 2)]
+    distance = 4
+    while distance < n:
+        stages.append((distance,))
+        distance *= 2
     return stages
 
 
-def broadcast_sum(block, stages):
-    for stage in stages:
-        arrived = [lax.ppermute(block, "member", pairs) for pairs in stage]
-        for part in arrived:
-            block = block + part
+def broadcast_sum(block, rings):
+    for n, shifts, _ in rings:
+        for stage in window_stages(n):
+            arrived = [lax.ppermute(block, "member", shifts[d]) for d in stage]
+            for part in arrived:
+                block = block + part
     return block
+
+
+def reversed_pairs(pairs):
+    return tuple((j, i) for i, j in pairs)
+
+
+def targeted_mean(kept, tile, rings):
+    (_, shifts_a, _), (_, shifts_b, _), (size_z, shifts_z, position_z) = rings
+    member = lax.axis_index("member")
+    at_z = jnp.asarray(position_z, jnp.int32)[member]
+    slots = jnp.arange(size_z, dtype=jnp.int32)
+
+    tiles_z = jnp.where(slots == at_z, tile, 0)
+    for d in range(1, size_z):
+        came = lax.ppermute(tile[None], "member", shifts_z[d])
+        tiles_z = tiles_z + jnp.where(slots == (at_z - d) % size_z, came[0], 0)
+    wanted = {d: lax.ppermute(tiles_z, "member", reversed_pairs(shifts_b[d])) for d in (1, -1, 2)}
+
+    block = kept
+    arrived = [lax.ppermute(block, "member", shifts_a[d]) for d in (1, -1, 2)]
+    for part in arrived:
+        block = block + part
+
+    sent = {d: jnp.take(block, wanted[d], axis=1, mode="clip") for d in (1, -1, 2)}
+    arrived = [lax.ppermute(sent[d], "member", shifts_b[d]) for d in (1, -1, 2)]
+    block = jnp.take(block, tiles_z, axis=1, mode="clip")
+    for part in arrived:
+        block = block + part
+
+    def pick(block, first):
+        served = jnp.stack([first % size_z, (first + size_z // 2) % size_z])
+        return jnp.take(block, served, axis=1, mode="clip")
+
+    arrived = [lax.ppermute(pick(block, at_z + d), "member", shifts_z[d]) for d in (1, -1, 2)]
+    block = pick(block, at_z)
+    for part in arrived:
+        block = block + part
+
+    arrived = lax.ppermute(block[:, 1], "member", shifts_z[size_z // 2])
+    return block[:, 0] + arrived
 
 
 def rms_scale(values):
@@ -190,8 +235,11 @@
         mine = lax.dynamic_slice_in_dim(reg_means[0], first_hour, half_hours, 0)
         is_owner = lax.axis_index("member") == owners
         kept = jnp.where(is_owner[:, None, None, None], mine, 0).astype(mine.dtype)
-        arrived = broadcast_sum(kept, routes)
-        means = lax.dynamic_index_in_dim(arrived, member_tile[0], 1, keepdims=False)
+        if [n for n, _, _ in routes] == [4, 4, 8]:
+            means = targeted_mean(kept, member_tile[0], routes)
+        else:
+            arrived = broadcast_sum(kept, routes)
+            means = lax.dynamic_index_in_dim(arrived, member_tile[0], 1, keepdims=False)
 
         noise = lax.dynamic_slice_in_dim(start_noise[0], first_hour, half_hours, 0)
         states = sigmas[0] * noise

time: 104 us -> 125 us (1.20)
  waiting for transfers between devices: 36.9 us -> 25.6 us
  between operations: 0.75 us -> 11.4 us
  other arithmetic: 2.69 us -> 12.9 us
  local copies, waits for them, and re-layouts: 7.33 us -> 12.8 us
  starting transfers between devices: 30.3 us -> 35.2 us
    ppermute x10 -> x20, waiting for transfers between devices: 36.9 us -> 24.4 us  [the longest x3 9.34 us: targeted_mean(): lax.ppermute(tiles_z, 'member', reversed_pairs(shifts_b[d]))]
    add x4 -> x5, other arithmetic: 0.3 us -> 10.2 us  [the longest x2 9.9 us: targeted_mean(): tiles_z = tiles_z + jnp.where(slots == (at_z - d) % size_z, came[0], 0)]
    ppermute x10 -> x20, starting transfers between devices: 29.8 us -> 35.2 us  [the longest x7 17.6 us: targeted_mean(): came = lax.ppermute(tile[None], 'member', shifts_z[d])]
    gather x0 -> x8, local copies, waits for them, and re-layouts: none -> 4.65 us  [the longest x4 2.29 us: pick(): return jnp.take(block, served, axis=1, mode='clip')]
    unnamed x18 -> x19, local copies, waits for them, and re-layouts: 2.38 us -> 2.61 us
  transfers between devices with their start and end apart: 12 -> 22, of which waited for: 9 -> 9; matrix products, arithmetic and copies ran while one was open for 5% -> 17% of each run, Pallas kernels for 0% -> 0%
where the time goes in v3:
time: 125 us; the launch traced here: 124 us
  starting transfers between devices  35.2 us (28%)
  Pallas kernels  25.9 us (21%)
  waiting for transfers between devices  25.6 us (20%)
  other arithmetic  12.9 us (10%)
  local copies, waits for them, and re-layouts  12.8 us (10%)
  between operations  11.4 us (9%)
    pallas_call x1, Pallas kernels, run_chain(): pl.pallas_call(chain_kernel, out_shape=jax.ShapeDtypeStruct(state.shape,...  25.9 us
    ppermute x7, starting transfers between devices, targeted_mean(): came = lax.ppermute(tile[None], 'member', shifts_z[d])  17.6 us
    add x2, other arithmetic, targeted_mean(): tiles_z = tiles_z + jnp.where(slots == (at_z - d) % size_z, came[0], 0)  9.9 us
    ppermute x3, waiting for transfers between devices, targeted_mean(): lax.ppermute(tiles_z, 'member', reversed_pairs(shifts_b[d]))  9.34 us
    ppermute x1, waiting for transfers between devices, targeted_mean(): arrived = lax.ppermute(block[:, 1], 'member', shifts_z[size_z // 2])  5.78 us
    ppermute x3, starting transfers between devices, targeted_mean(): lax.ppermute(tiles_z, 'member', reversed_pairs(shifts_b[d]))  5.14 us
    ppermute x3, starting transfers between devices, targeted_mean(): arrived = [lax.ppermute(block, 'member', shifts_a[d]) for d in (1, -1, 2)]  5.05 us
    ppermute x3, waiting for transfers between devices, targeted_mean(): lax.ppermute(pick(block, at_z + d), 'member', shifts_z[d])  4.96 us
  transfers between devices with their start and end apart: 22, of which 9 were waited for; matrix products, arithmetic and copies ran while one was open for 17% of the time, Pallas kernels for 0%

profile of v3, /device:TPU:32, one launch (start us, length us, event | category | flops | bytes accessed | tf_op | source)
XLA Modules:
  0.0 123.8 jit_solution(8565207926265484069)
XLA Ops:
  0.0 1.9 %collective-permute-start.3 = (s32[1]{0:T(128)}, s32[1]{0:T(128)}, u32[]{:S(2)}, u32[]{:S(2)}) collective-permute-start(s32[1]{0:T(128)} %param.14), channel_id=1, source_target_pairs={{0,32},{2,34},{4,36},{6,38},{8,40},{10,42},{12,44},{14,46},{16,48}... | collective-permute-start | bytes 20 | tf_op jit(solution)/shard_map/ppermute | solution.py:76
  1.9 4.5 %collective-permute-start.4 = (s32[1]{0:T(128)}, s32[1]{0:T(128)}, u32[]{:S(2)}, u32[]{:S(2)}) collective-permute-start(s32[1]{0:T(128)} %param.14), channel_id=1, source_target_pairs={{0,64},{2,66},{4,68},{6,70},{8,72},{10,74},{12,76},{14,78},{16,80}... | collective-permute-start | bytes 20 | tf_op jit(solution)/shard_map/ppermute | solution.py:76
  6.4 1.9 %collective-permute-start.5 = (s32[1]{0:T(128)}, s32[1]{0:T(128)}, u32[]{:S(2)}, u32[]{:S(2)}) collective-permute-start(s32[1]{0:T(128)} %param.14), channel_id=1, source_target_pairs={{0,96},{2,98},{4,100},{6,102},{8,104},{10,106},{12,108},{14,110},{... | collective-permute-start | bytes 20 | tf_op jit(solution)/shard_map/ppermute | solution.py:76
  8.3 1.4 %collective-permute-start.6 = (s32[1]{0:T(128)}, s32[1]{0:T(128)}, u32[]{:S(2)}, u32[]{:S(2)}) collective-permute-start(s32[1]{0:T(128)} %param.14), channel_id=1, source_target_pairs={{0,128},{2,130},{4,132},{6,134},{8,136},{10,138},{12,140},{14,142}... | collective-permute-start | bytes 20 | tf_op jit(solution)/shard_map/ppermute | solution.py:76
  9.8 3.0 %collective-permute-start.7 = (s32[1]{0:T(128)}, s32[1]{0:T(128)}, u32[]{:S(2)}, u32[]{:S(2)}) collective-permute-start(s32[1]{0:T(128)} %param.14), channel_id=1, source_target_pairs={{0,160},{2,162},{4,164},{6,166},{8,168},{10,170},{12,172},{14,174}... | collective-permute-start | bytes 20 | tf_op jit(solution)/shard_map/ppermute | solution.py:76
  12.8 0.7 copy-done.8
  13.5 0.6 dynamic_slice.17
  25.5 0.6 copy-done.2
  26.4 0.7 reshape.114.coef_ref
  27.1 0.7 copy-done.7
  28.0 0.5 copy-done.5
  28.6 0.7 pad.16.state_ref
  29.3 0.6 pad.19.out_ref
  30.0 0.6 pad.18.lift_ref
  30.7 2.5 %collective-permute-start.8 = (s32[1]{0:T(128)}, s32[1]{0:T(128)}, u32[]{:S(2)}, u32[]{:S(2)}) collective-permute-start(s32[1]{0:T(128)} %param.14), channel_id=1, source_target_pairs={{0,192},{2,194},{4,196},{6,198},{8,200},{10,202},{12,204},{14,206}... | collective-permute-start | bytes 20 | tf_op jit(solution)/shard_map/ppermute | solution.py:76
  33.3 2.2 %collective-permute-start.9 = (s32[1]{0:T(128)}, s32[1]{0:T(128)}, u32[]{:S(2)}, u32[]{:S(2)}) collective-permute-start(s32[1]{0:T(128)} %param.14), channel_id=1, source_target_pairs={{0,224},{2,226},{4,228},{6,230},{8,232},{10,234},{12,236},{14,238}... | collective-permute-start | bytes 20 | tf_op jit(solution)/shard_map/ppermute | solution.py:76
  35.5 1.5 %collective-permute-start = (f32[2,32,4,256]{3,2,1,0:T(4,128)S(1)}, f32[2,32,4,256]{3,2,1,0:T(4,128)S(1)}, u32[]{:S(2)}, u32[]{:S(2)}) collective-permute-start(f32[2,32,4,256]{3,2,1,0:T(4,128)S(1)} %bitcast_select_fusion), channel_id=1, source_target_pairs={{0,8},{2,10},{4,12},{6,14},{8,16},{10,18},{12,20},{14,22},{16,24},... | collective-permute-start | bytes 786440 | tf_op jit(solution)/shard_map/ppermute | solution.py:81
  37.0 1.7 %collective-permute-start.1 = (f32[2,32,4,256]{3,2,1,0:T(4,128)S(1)}, f32[2,32,4,256]{3,2,1,0:T(4,128)S(1)}, u32[]{:S(2)}, u32[]{:S(2)}) collective-permute-start(f32[2,32,4,256]{3,2,1,0:T(4,128)S(1)} %bitcast_select_fusion), channel_id=1, source_target_pairs={{0,24},{2,26},{4,28},{6,30},{8,0},{10,2},{12,4},{14,6},{16,8},{18,... | collective-permute-start | bytes 786440 | tf_op jit(solution)/shard_map/ppermute | solution.py:81
  38.8 1.8 %collective-permute-start.2 = (f32[2,32,4,256]{3,2,1,0:T(4,128)S(1)}, f32[2,32,4,256]{3,2,1,0:T(4,128)S(1)}, u32[]{:S(2)}, u32[]{:S(2)}) collective-permute-start(f32[2,32,4,256]{3,2,1,0:T(4,128)S(1)} %bitcast_select_fusion), channel_id=1, source_target_pairs={{0,16},{2,18},{4,20},{6,22},{8,24},{10,26},{12,28},{14,30},{16,0},... | collective-permute-start | bytes 786440 | tf_op jit(solution)/shard_map/ppermute | solution.py:81
  40.6 5.0 %fusion.21 = s32[8]{0:T(128)S(1)} fusion(s32[]{:T(128)} %bitcast.9, s32[]{:T(128)S(6)} %select_n.214, s32[]{:T(128)} %bitcast.8, s32[]{:T(128)S(6)} %select_n.212, s32[]{:T(128)} %bitcast.7, s32[]{:T(128)S(6)} %select_n.210, s32[]{:T(128)} %bitcast.6, s32[]{:T(128)S(6)} %select_n.208, s32[]{:T(128)} %bitcast.5, s32[]{:T(128)S(6)} %select_n.206, s32[]{:T(128)} %bitcast.4, ...), kind=kLoop, calls=%fused_computation.76 | loop fusion | flops 184 | bytes 96 | tf_op jit(solution)/shard_map/add | solution.py:77
  45.6 5.0 %fusion.20 = s32[8]{0:T(128)S(1)} fusion(s32[]{:T(128)} %bitcast.9, s32[]{:T(128)S(6)} %select_n.214, s32[]{:T(128)} %bitcast.8, s32[]{:T(128)S(6)} %select_n.212, s32[]{:T(128)} %bitcast.7, s32[]{:T(128)S(6)} %select_n.210, s32[]{:T(128)} %bitcast.6, s32[]{:T(128)S(6)} %select_n.208, s32[]{:T(128)} %bitcast.5, s32[]{:T(128)S(6)} %select_n.206, s32[]{:T(128)} %bitcast.4, ...), kind=kLoop, calls=%fused_computation.66 | loop fusion | flops 184 | bytes 96 | tf_op jit(solution)/shard_map/add | solution.py:77
  50.5 3.1 %collective-permute-start.10 = (s32[8]{0:T(128)S(1)}, s32[8]{0:T(128)S(1)}, u32[]{:S(2)}, u32[]{:S(2)}) collective-permute-start(s32[8]{0:T(128)S(1)} %fusion.20), channel_id=1, source_target_pairs={{2,0},{4,2},{6,4},{0,6},{10,8},{12,10},{14,12},{8,14},{18,16},{20,... | collective-permute-start | bytes 104 | tf_op jit(solution)/shard_map/ppermute | solution.py:78
  53.6 1.3 %collective-permute-done.10 = s32[8]{0:T(128)S(1)} collective-permute-done((s32[8]{0:T(128)S(1)}, s32[8]{0:T(128)S(1)}, u32[]{:S(2)}, u32[]{:S(2)}) %collective-permute-start.10) | collective-permute-done | bytes 64 | tf_op jit(solution)/shard_map/ppermute | solution.py:78
  54.9 0.8 collective-permute-start.12
  55.8 4.2 %collective-permute-done.12 = s32[8]{0:T(128)S(1)} collective-permute-done((s32[8]{0:T(128)S(1)}, s32[8]{0:T(128)S(1)}, u32[]{:S(2)}, u32[]{:S(2)}) %collective-permute-start.12) | collective-permute-done | bytes 64 | tf_op jit(solution)/shard_map/ppermute | solution.py:78
  59.9 1.2 collective-permute-start.14
  61.2 3.9 %collective-permute-done.14 = s32[8]{0:T(128)S(1)} collective-permute-done((s32[8]{0:T(128)S(1)}, s32[8]{0:T(128)S(1)}, u32[]{:S(2)}, u32[]{:S(2)}) %collective-permute-start.14) | collective-permute-done | bytes 64 | tf_op jit(solution)/shard_map/ppermute | solution.py:78
  65.0 1.1 collective-permute-done.21
  66.4 0.6 gather_fusion.1
  67.3 0.6 gather_fusion.2
  67.9 3.3 %collective-permute-start.13 = (f32[2,8,4,256]{3,2,0,1:T(4,128)S(1)}, f32[2,8,4,256]{3,2,0,1:T(4,128)S(1)}, u32[]{:S(2)}, u32[]{:S(2)}) collective-permute-start(f32[2,8,4,256]{3,2,0,1:T(4,128)S(1)} %bitcast.90), channel_id=1, source_target_pairs={{0,6},{2,0},{4,2},{6,4},{8,14},{10,8},{12,10},{14,12},{16,22},{18,... | collective-permute-start | bytes 196616 | tf_op jit(solution)/shard_map/ppermute | solution.py:86
  71.2 0.6 gather_fusion.3
  72.1 0.6 maximum_convert_fusion.gain_ref
  72.7 0.6 gather_fusion
  73.7 3.9 %collective-permute-done.15 = f32[2,8,4,256]{3,2,0,1:T(4,128)S(1)} collective-permute-done((f32[2,8,4,256]{3,2,0,1:T(4,128)S(1)}, f32[2,8,4,256]{3,2,0,1:T(4,128)S(1)}, u32[]{:S(2)}, u32[]{:S(2)}) %collective-permute-start.15) | collective-permute-done | bytes 65568 | tf_op jit(solution)/shard_map/ppermute | solution.py:86
  77.7 0.6 gather_fusion.5
  78.3 0.6 gather_fusion.6
  78.9 2.1 %collective-permute-start.17 = (f32[2,2,4,256]{3,2,0,1:T(4,128)S(1)}, f32[2,2,4,256]{3,2,0,1:T(4,128)S(1)}, u32[]{:S(2)}, u32[]{:S(2)}) collective-permute-start(f32[2,2,4,256]{3,2,0,1:T(4,128)S(1)} %bitcast.93), channel_id=1, source_target_pairs={{0,224},{2,226},{4,228},{6,230},{8,232},{10,234},{12,236},{14,238}... | collective-permute-start | bytes 49160 | tf_op jit(solution)/shard_map/ppermute | solution.py:95
  81.0 0.6 gather_fusion.7
  82.0 0.6 gather_fusion.4
  82.7 4.8 %collective-permute-done.18 = f32[2,2,4,256]{3,2,0,1:T(4,128)S(1)} collective-permute-done((f32[2,2,4,256]{3,2,0,1:T(4,128)S(1)}, f32[2,2,4,256]{3,2,0,1:T(4,128)S(1)}, u32[]{:S(2)}, u32[]{:S(2)}) %collective-permute-start.18) | collective-permute-done | bytes 16416 | tf_op jit(solution)/shard_map/ppermute | solution.py:95
  87.5 1.0 collective-permute-start.19
  88.5 0.9 pad_maximum_fusion.conv_ref
  89.4 5.8 %collective-permute-done.19 = f32[2,4,256]{2,1,0:T(4,128)S(1)} collective-permute-done((f32[2,4,256]{2,1,0:T(4,128)S(1)}, f32[2,4,256]{2,1,0:T(4,128)S(1)}, u32[]{:S(2)}, u32[]{:S(2)}) %collective-permute-start.19) | collective-permute-done | bytes 8224 | tf_op jit(solution)/shard_map/ppermute | solution.py:100
  95.3 0.8 pad.17.means_ref
  96.2 25.9 %shard_map.109 = f32[512,128]{1,0:T(8,128)} custom-call(f32[40]{0:T(128)} %reshape.114.coef_ref, f32[512,128]{1,0:T(8,128)} %pad.16.state_ref, f32[512,128]{1,0:T(8,128)} %pad.17.means_ref, f32[128,128]{1,0:T(8,128)} %pad.18.lift_ref, f32[1,128]{1,0:T(1,128)} %bitcast.96, bf16[2,1152,128]{2,1,0:T(8,128)(2,1)} %pad_maximum_fusion.conv_ref, ...), custom_call_target="tpu_custom_call" | custom-call | tf_op jit(solution)/shard_map/pallas_call | solution.py:166
  122.1 1.1 copy.16
  123.2 0.6 fusion.5
  (63 shorter events, 3.2 us)
Async XLA Ops:
  0.0 30.7 %collective-permute-start.3 = (s32[1]{0:T(128)}, s32[1]{0:T(128)}, u32[]{:S(2)}, u32[]{:S(2)}) collective-permute-start(s32[1]{0:T(128)} %param.14), channel_id=1, source_target_pairs={{0,32},{2,34},{4,36},{6,38},{8,40},{10,42},{12,44},{14,46},{16,48}... | collective-permute-start | bytes 20 | tf_op jit(solution)/shard_map/ppermute | solution.py:76
  1.9 31.4 %collective-permute-start.4 = (s32[1]{0:T(128)}, s32[1]{0:T(128)}, u32[]{:S(2)}, u32[]{:S(2)}) collective-permute-start(s32[1]{0:T(128)} %param.14), channel_id=1, source_target_pairs={{0,64},{2,66},{4,68},{6,70},{8,72},{10,74},{12,76},{14,78},{16,80}... | collective-permute-start | bytes 20 | tf_op jit(solution)/shard_map/ppermute | solution.py:76
  6.4 29.1 %collective-permute-start.5 = (s32[1]{0:T(128)}, s32[1]{0:T(128)}, u32[]{:S(2)}, u32[]{:S(2)}) collective-permute-start(s32[1]{0:T(128)} %param.14), channel_id=1, source_target_pairs={{0,96},{2,98},{4,100},{6,102},{8,104},{10,106},{12,108},{14,110},{... | collective-permute-start | bytes 20 | tf_op jit(solution)/shard_map/ppermute | solution.py:76
  8.3 28.7 %collective-permute-start.6 = (s32[1]{0:T(128)}, s32[1]{0:T(128)}, u32[]{:S(2)}, u32[]{:S(2)}) collective-permute-start(s32[1]{0:T(128)} %param.14), channel_id=1, source_target_pairs={{0,128},{2,130},{4,132},{6,134},{8,136},{10,138},{12,140},{14,142}... | collective-permute-start | bytes 20 | tf_op jit(solution)/shard_map/ppermute | solution.py:76
  9.8 29.0 %collective-permute-start.7 = (s32[1]{0:T(128)}, s32[1]{0:T(128)}, u32[]{:S(2)}, u32[]{:S(2)}) collective-permute-start(s32[1]{0:T(128)} %param.14), channel_id=1, source_target_pairs={{0,160},{2,162},{4,164},{6,166},{8,168},{10,170},{12,172},{14,174}... | collective-permute-start | bytes 20 | tf_op jit(solution)/shard_map/ppermute | solution.py:76
  12.8 0.7 copy-start.8
  25.5 0.7 copy-start.2
  26.3 1.5 %copy-start.4 = (f32[1,4,4,256]{3,2,1,0:T(4,128)S(1)}, f32[1,4,4,256]{3,2,1,0:T(4,128)}, u32[]{:S(2)}) copy-start(f32[1,4,4,256]{3,2,1,0:T(4,128)} %param.11) | copy-start | bytes 49156
  27.1 0.7 copy-start.7
  27.8 0.7 copy-start.5
  27.8 2.8 %copy-start = (f32[1,4,32,4,256]{4,3,2,1,0:T(4,128)S(1)}, f32[1,4,32,4,256]{4,3,2,1,0:T(4,128)}, u32[]{:S(2)}) copy-start(f32[1,4,32,4,256]{4,3,2,1,0:T(4,128)} %param.12) | copy-start | bytes 1572868
  29.3 0.7 copy-start.3
  30.0 10.6 %copy-start.1 = (bf16[1,9,128,128]{3,2,1,0:T(8,128)(2,1)S(1)}, bf16[1,9,128,128]{3,2,1,0:T(8,128)(2,1)}, u32[]{:S(2)}) copy-start(bf16[1,9,128,128]{3,2,1,0:T(8,128)(2,1)} %param.18) | copy-start | bytes 884740
  30.7 9.8 %collective-permute-start.8 = (s32[1]{0:T(128)}, s32[1]{0:T(128)}, u32[]{:S(2)}, u32[]{:S(2)}) collective-permute-start(s32[1]{0:T(128)} %param.14), channel_id=1, source_target_pairs={{0,192},{2,194},{4,196},{6,198},{8,200},{10,202},{12,204},{14,206}... | collective-permute-start | bytes 20 | tf_op jit(solution)/shard_map/ppermute | solution.py:76
  33.3 7.3 %collective-permute-start.9 = (s32[1]{0:T(128)}, s32[1]{0:T(128)}, u32[]{:S(2)}, u32[]{:S(2)}) collective-permute-start(s32[1]{0:T(128)} %param.14), channel_id=1, source_target_pairs={{0,224},{2,226},{4,228},{6,230},{8,232},{10,234},{12,236},{14,238}... | collective-permute-start | bytes 20 | tf_op jit(solution)/shard_map/ppermute | solution.py:76
  35.5 30.7 %collective-permute-start = (f32[2,32,4,256]{3,2,1,0:T(4,128)S(1)}, f32[2,32,4,256]{3,2,1,0:T(4,128)S(1)}, u32[]{:S(2)}, u32[]{:S(2)}) collective-permute-start(f32[2,32,4,256]{3,2,1,0:T(4,128)S(1)} %bitcast_select_fusion), channel_id=1, source_target_pairs={{0,8},{2,10},{4,12},{6,14},{8,16},{10,18},{12,20},{14,22},{16,24},... | collective-permute-start | bytes 786440 | tf_op jit(solution)/shard_map/ppermute | solution.py:81
  37.0 29.2 %collective-permute-start.1 = (f32[2,32,4,256]{3,2,1,0:T(4,128)S(1)}, f32[2,32,4,256]{3,2,1,0:T(4,128)S(1)}, u32[]{:S(2)}, u32[]{:S(2)}) collective-permute-start(f32[2,32,4,256]{3,2,1,0:T(4,128)S(1)} %bitcast_select_fusion), channel_id=1, source_target_pairs={{0,24},{2,26},{4,28},{6,30},{8,0},{10,2},{12,4},{14,6},{16,8},{18,... | collective-permute-start | bytes 786440 | tf_op jit(solution)/shard_map/ppermute | solution.py:81
  38.8 27.4 %collective-permute-start.2 = (f32[2,32,4,256]{3,2,1,0:T(4,128)S(1)}, f32[2,32,4,256]{3,2,1,0:T(4,128)S(1)}, u32[]{:S(2)}, u32[]{:S(2)}) collective-permute-start(f32[2,32,4,256]{3,2,1,0:T(4,128)S(1)} %bitcast_select_fusion), channel_id=1, source_target_pairs={{0,16},{2,18},{4,20},{6,22},{8,24},{10,26},{12,28},{14,30},{16,0},... | collective-permute-start | bytes 786440 | tf_op jit(solution)/shard_map/ppermute | solution.py:81
  40.6 41.3 %collective-permute-start.20 = (bf16[1,9,128,128]{3,2,1,0:T(8,128)(2,1)S(1)}, bf16[1,9,128,128]{3,2,1,0:T(8,128)(2,1)S(1)}, u32[]{:S(2)}, u32[]{:S(2)}) collective-permute-start(bf16[1,9,128,128]{3,2,1,0:T(8,128)(2,1)S(1)} %copy-done.1), channel_id=1, source_target_pairs={{0,1},{1,0},{2,3},{3,2},{4,5},{5,4},{6,7},{7,6},{8,9},{9,8},{10,11... | collective-permute-start | bytes 884744 | tf_op jit(solution)/shard_map/ppermute | solution.py:219
  50.5 4.4 %collective-permute-start.10 = (s32[8]{0:T(128)S(1)}, s32[8]{0:T(128)S(1)}, u32[]{:S(2)}, u32[]{:S(2)}) collective-permute-start(s32[8]{0:T(128)S(1)} %fusion.20), channel_id=1, source_target_pairs={{2,0},{4,2},{6,4},{0,6},{10,8},{12,10},{14,12},{8,14},{18,16},{20,... | collective-permute-start | bytes 104 | tf_op jit(solution)/shard_map/ppermute | solution.py:78
  54.9 5.0 %collective-permute-start.12 = (s32[8]{0:T(128)S(1)}, s32[8]{0:T(128)S(1)}, u32[]{:S(2)}, u32[]{:S(2)}) collective-permute-start(s32[8]{0:T(128)S(1)} %fusion.20), channel_id=1, source_target_pairs={{6,0},{0,2},{2,4},{4,6},{14,8},{8,10},{10,12},{12,14},{22,16},{16,... | collective-permute-start | bytes 104 | tf_op jit(solution)/shard_map/ppermute | solution.py:78
  55.7 9.3 %copy-start.6 = (bf16[1,128]{1,0:T(2,128)(2,1)S(1)}, bf16[1,128]{1,0:T(2,128)(2,1)}, u32[]{:S(2)}) copy-start(bf16[1,128]{1,0:T(2,128)(2,1)} %param.19) | copy-start | bytes 772
  59.9 5.1 %collective-permute-start.14 = (s32[8]{0:T(128)S(1)}, s32[8]{0:T(128)S(1)}, u32[]{:S(2)}, u32[]{:S(2)}) collective-permute-start(s32[8]{0:T(128)S(1)} %fusion.20), channel_id=1, source_target_pairs={{4,0},{6,2},{0,4},{2,6},{12,8},{14,10},{8,12},{10,14},{20,16},{22,... | collective-permute-start | bytes 104 | tf_op jit(solution)/shard_map/ppermute | solution.py:78
  65.0 1.2 collective-permute-start.21
  67.0 6.3 %collective-permute-start.11 = (f32[2,8,4,256]{3,2,0,1:T(4,128)S(1)}, f32[2,8,4,256]{3,2,0,1:T(4,128)S(1)}, u32[]{:S(2)}, u32[]{:S(2)}) collective-permute-start(f32[2,8,4,256]{3,2,0,1:T(4,128)S(1)} %bitcast.89), channel_id=1, source_target_pairs={{0,2},{2,4},{4,6},{6,0},{8,10},{10,12},{12,14},{14,8},{16,18},{18,... | collective-permute-start | bytes 196616 | tf_op jit(solution)/shard_map/ppermute | solution.py:86
  67.9 5.8 %collective-permute-start.13 = (f32[2,8,4,256]{3,2,0,1:T(4,128)S(1)}, f32[2,8,4,256]{3,2,0,1:T(4,128)S(1)}, u32[]{:S(2)}, u32[]{:S(2)}) collective-permute-start(f32[2,8,4,256]{3,2,0,1:T(4,128)S(1)} %bitcast.90), channel_id=1, source_target_pairs={{0,6},{2,0},{4,2},{6,4},{8,14},{10,8},{12,10},{14,12},{16,22},{18,... | collective-permute-start | bytes 196616 | tf_op jit(solution)/shard_map/ppermute | solution.py:86
  71.8 5.9 %collective-permute-start.15 = (f32[2,8,4,256]{3,2,0,1:T(4,128)S(1)}, f32[2,8,4,256]{3,2,0,1:T(4,128)S(1)}, u32[]{:S(2)}, u32[]{:S(2)}) collective-permute-start(f32[2,8,4,256]{3,2,0,1:T(4,128)S(1)} %bitcast.91), channel_id=1, source_target_pairs={{0,4},{2,6},{4,0},{6,2},{8,12},{10,14},{12,8},{14,10},{16,20},{18,... | collective-permute-start | bytes 196616 | tf_op jit(solution)/shard_map/ppermute | solution.py:86
  78.3 4.3 %collective-permute-start.16 = (f32[2,2,4,256]{3,2,0,1:T(4,128)S(1)}, f32[2,2,4,256]{3,2,0,1:T(4,128)S(1)}, u32[]{:S(2)}, u32[]{:S(2)}) collective-permute-start(f32[2,2,4,256]{3,2,0,1:T(4,128)S(1)} %bitcast.92), channel_id=1, source_target_pairs={{0,32},{2,34},{4,36},{6,38},{8,40},{10,42},{12,44},{14,46},{16,48}... | collective-permute-start | bytes 49160 | tf_op jit(solution)/shard_map/ppermute | solution.py:95
  78.9 3.8 %collective-permute-start.17 = (f32[2,2,4,256]{3,2,0,1:T(4,128)S(1)}, f32[2,2,4,256]{3,2,0,1:T(4,128)S(1)}, u32[]{:S(2)}, u32[]{:S(2)}) collective-permute-start(f32[2,2,4,256]{3,2,0,1:T(4,128)S(1)} %bitcast.93), channel_id=1, source_target_pairs={{0,224},{2,226},{4,228},{6,230},{8,232},{10,234},{12,236},{14,238}... | collective-permute-start | bytes 49160 | tf_op jit(solution)/shard_map/ppermute | solution.py:95
  81.6 5.9 %collective-permute-start.18 = (f32[2,2,4,256]{3,2,0,1:T(4,128)S(1)}, f32[2,2,4,256]{3,2,0,1:T(4,128)S(1)}, u32[]{:S(2)}, u32[]{:S(2)}) collective-permute-start(f32[2,2,4,256]{3,2,0,1:T(4,128)S(1)} %bitcast.94), channel_id=1, source_target_pairs={{0,64},{2,66},{4,68},{6,70},{8,72},{10,74},{12,76},{14,78},{16,80}... | collective-permute-start | bytes 49160 | tf_op jit(solution)/shard_map/ppermute | solution.py:95
  87.5 7.6 %collective-permute-start.19 = (f32[2,4,256]{2,1,0:T(4,128)S(1)}, f32[2,4,256]{2,1,0:T(4,128)S(1)}, u32[]{:S(2)}, u32[]{:S(2)}) collective-permute-start(f32[2,4,256]{2,1,0:T(4,128)S(1)} %slice_bitcast_fusion), channel_id=1, source_target_pairs={{0,128},{2,130},{4,132},{6,134},{8,136},{10,138},{12,140},{14,142}... | collective-permute-start | bytes 24584 | tf_op jit(solution)/shard_map/ppermute | solution.py:100

commit v4 on v3

--- a/solution.py
+++ b/solution.py
@@ -65,40 +65,22 @@
     return tuple((j, i) for i, j in pairs)
 
 
-def targeted_mean(kept, tile, rings):
-    (_, shifts_a, _), (_, shifts_b, _), (size_z, shifts_z, position_z) = rings
-    member = lax.axis_index("member")
-    at_z = jnp.asarray(position_z, jnp.int32)[member]
-    slots = jnp.arange(size_z, dtype=jnp.int32)
-
-    tiles_z = jnp.where(slots == at_z, tile, 0)
-    for d in range(1, size_z):
-        came = lax.ppermute(tile[None], "member", shifts_z[d])
-        tiles_z = tiles_z + jnp.where(slots == (at_z - d) % size_z, came[0], 0)
-    wanted = {d: lax.ppermute(tiles_z, "member", reversed_pairs(shifts_b[d])) for d in (1, -1, 2)}
-
+def broadcast_mean(kept, tile, rings):
+    stages = [(shifts, stage) for n, shifts, _ in rings for stage in window_stages(n)]
+    last_shifts, last_stage = stages[-1]
+    if len(last_stage) != 1:
+        block = broadcast_sum(kept, rings)
+        return lax.dynamic_index_in_dim(block, tile, 1, keepdims=False)
+    last_pairs = last_shifts[last_stage[0]]
+    wanted = lax.ppermute(tile[None], "member", reversed_pairs(last_pairs))[0]
     block = kept
-    arrived = [lax.ppermute(block, "member", shifts_a[d]) for d in (1, -1, 2)]
-    for part in arrived:
-        block = block + part
-
-    sent = {d: jnp.take(block, wanted[d], axis=1, mode="clip") for d in (1, -1, 2)}
-    arrived = [lax.ppermute(sent[d], "member", shifts_b[d]) for d in (1, -1, 2)]
-    block = jnp.take(block, tiles_z, axis=1, mode="clip")
-    for part in arrived:
-        block = block + part
-
-    def pick(block, first):
-        served = jnp.stack([first % size_z, (first + size_z // 2) % size_z])
-        return jnp.take(block, served, axis=1, mode="clip")
-
-    arrived = [lax.ppermute(pick(block, at_z + d), "member", shifts_z[d]) for d in (1, -1, 2)]
-    block = pick(block, at_z)
-    for part in arrived:
-        block = block + part
-
-    arrived = lax.ppermute(block[:, 1], "member", shifts_z[size_z // 2])
-    return block[:, 0] + arrived
+    for shifts, stage in stages[:-1]:
+        arrived = [lax.ppermute(block, "member", shifts[d]) for d in stage]
+        for part in arrived:
+            block = block + part
+    sent = lax.dynamic_index_in_dim(block, wanted, 1, keepdims=False)
+    arrived = lax.ppermute(sent, "member", last_pairs)
+    return lax.dynamic_index_in_dim(block, tile, 1, keepdims=False) + arrived
 
 
 def rms_scale(values):
@@ -114,17 +96,27 @@
     pixel = lax.broadcasted_iota(jnp.int32, (rows, lanes), 0) % (SIDE * SIDE)
     row = pixel // SIDE
     col = pixel % SIDE
-    offsets = [(a, b) for a in (-1, 0, 1) for b in (-1, 0, 1)]
-    valid = [
-        (row + a >= 0) & (row + a < SIDE) & (col + b >= 0) & (col + b < SIDE) for a, b in offsets
-    ]
+    row_ok = {a: (row + a >= 0) & (row + a < SIDE) for a in (-1, 1)}
+    col_ok = {b: (col + b >= 0) & (col + b < SIDE) for b in (-1, 1)}
 
     def conv(gated, index):
+        columns = {}
+        for b in (-1, 0, 1):
+            moved = gated
+            if b:
+                moved = jnp.where(col_ok[b], pltpu.roll(gated, (-b) % rows, 0), 0.0)
+            columns[b] = moved
         windows = []
-        for (a, b), keep in zip(offsets, valid):
-            distance = a * SIDE + b
-            moved = gated if distance == 0 else pltpu.roll(gated, (-distance) % rows, 0)
-            windows.append(jnp.where(keep, moved, 0.0).astype(jnp.bfloat16))
+        for a in (-1, 0, 1):
+            for b in (-1, 0, 1):
+                moved = columns[b]
+                if a == 1:
+                    moved = jnp.concatenate([moved[SIDE:], moved[:SIDE]], axis=0)
+                if a == -1:
+                    moved = jnp.concatenate([moved[-SIDE:], moved[:-SIDE]], axis=0)
+                if a:
+                    moved = jnp.where(row_ok[a], moved, 0.0)
+                windows.append(moved.astype(jnp.bfloat16))
         stacked = jnp.concatenate(windows, axis=1)
         return jnp.dot(stacked, conv_ref[index], preferred_element_type=jnp.float32)
 
@@ -235,11 +227,7 @@
         mine = lax.dynamic_slice_in_dim(reg_means[0], first_hour, half_hours, 0)
         is_owner = lax.axis_index("member") == owners
         kept = jnp.where(is_owner[:, None, None, None], mine, 0).astype(mine.dtype)
-        if [n for n, _, _ in routes] == [4, 4, 8]:
-            means = targeted_mean(kept, member_tile[0], routes)
-        else:
-            arrived = broadcast_sum(kept, routes)
-            means = lax.dynamic_index_in_dim(arrived, member_tile[0], 1, keepdims=False)
+        means = broadcast_mean(kept, member_tile[0], routes)
 
         noise = lax.dynamic_slice_in_dim(start_noise[0], first_hour, half_hours, 0)
         states = sigmas[0] * noise

time: 125 us -> 91.7 us (0.73)
  other arithmetic: 12.9 us -> 2.71 us
  between operations: 11.4 us -> 2.84 us
  starting transfers between devices: 35.2 us -> 27.7 us
  local copies, waits for them, and re-layouts: 12.8 us -> 7.3 us
    add x5 -> x3, other arithmetic: 10.2 us -> 0.3 us  [broadcast_mean(): block = block + part]
    ppermute x20 -> x11, starting transfers between devices: 35.2 us -> 27.7 us  [the longest x9 16.9 us: broadcast_mean(): arrived = [lax.ppermute(block, 'member', shifts[d]) for d in stage]]
    gather x8 -> x0, local copies, waits for them, and re-layouts: 4.65 us -> none  [the longest x4 2.29 us: pick(): return jnp.take(block, served, axis=1, mode='clip')]
    ppermute x20 -> x11, waiting for transfers between devices: 24.4 us -> 24.9 us  [the longest x9 22.5 us: broadcast_mean(): arrived = [lax.ppermute(block, 'member', shifts[d]) for d in stage]]
    unnamed x19 -> x18, local copies, waits for them, and re-layouts: 2.61 us -> 2.4 us
  transfers between devices with their start and end apart: 22 -> 13, of which waited for: 9 -> 7; matrix products, arithmetic and copies ran while one was open for 17% -> 5% of each run, Pallas kernels for 0% -> 0%
where the time goes in v4:
time: 91.7 us; the launch traced here: 91.4 us
  starting transfers between devices  27.7 us (30%)
  Pallas kernels  25.9 us (28%)
  waiting for transfers between devices  24.9 us (27%)
  local copies, waits for them, and re-layouts  7.3 us (8%)
  between operations  2.84 us (3%)
  other arithmetic  2.71 us (3%)
    pallas_call x1, Pallas kernels, run_chain(): pl.pallas_call(chain_kernel, out_shape=jax.ShapeDtypeStruct(state.shape,...  25.9 us
    ppermute x9, waiting for transfers between devices, broadcast_mean(): arrived = [lax.ppermute(block, 'member', shifts[d]) for d in stage]  22.5 us
    ppermute x9, starting transfers between devices, broadcast_mean(): arrived = [lax.ppermute(block, 'member', shifts[d]) for d in stage]  16.9 us
    ppermute x1, starting transfers between devices, broadcast_mean(): wanted = lax.ppermute(tile[None], 'member', reversed_pairs(last_pairs))[0]  6.29 us
    ppermute x1, starting transfers between devices, broadcast_mean(): arrived = lax.ppermute(sent, 'member', last_pairs)  4.53 us
    ppermute x1, waiting for transfers between devices, broadcast_mean(): arrived = lax.ppermute(sent, 'member', last_pairs)  2.42 us
    unnamed x18, local copies, waits for them, and re-layouts  2.4 us
  transfers between devices with their start and end apart: 13, of which 7 were waited for; matrix products, arithmetic and copies ran while one was open for 5% of the time, Pallas kernels for 0%

profile of v4, /device:TPU:32, one launch (start us, length us, event | category | flops | bytes accessed | tf_op | source)
XLA Modules:
  0.0 91.4 jit_solution(4351784930290408949)
XLA Ops:
  0.0 1.0 %copy-done = f32[1,4,32,4,256]{4,3,2,1,0:T(4,128)S(1)} copy-done((f32[1,4,32,4,256]{4,3,2,1,0:T(4,128)S(1)}, f32[1,4,32,4,256]{4,3,2,1,0:T(4,128)}, u32[]{:S(2)}) %copy-start) | copy-done | bytes 524312
  1.1 0.6 copy-done.7
  1.7 0.1 dynamic-slice_compare_fusion
  1.8 0.1 fusion
  1.9 1.6 %collective-permute-start = (f32[2,32,4,256]{3,1,2,0:T(8,128)S(1)}, f32[2,32,4,256]{3,1,2,0:T(8,128)S(1)}, u32[]{:S(2)}, u32[]{:S(2)}) collective-permute-start(f32[2,32,4,256]{3,1,2,0:T(8,128)S(1)} %fusion), channel_id=1, source_target_pairs={{0,8},{2,10},{4,12},{6,14},{8,16},{10,18},{12,20},{14,22},{16,24},... | collective-permute-start | bytes 786440 | tf_op jit(solution)/shard_map/ppermute | solution.py:78
  3.4 1.7 %collective-permute-start.1 = (f32[2,32,4,256]{3,1,2,0:T(8,128)S(1)}, f32[2,32,4,256]{3,1,2,0:T(8,128)S(1)}, u32[]{:S(2)}, u32[]{:S(2)}) collective-permute-start(f32[2,32,4,256]{3,1,2,0:T(8,128)S(1)} %fusion), channel_id=1, source_target_pairs={{0,24},{2,26},{4,28},{6,30},{8,0},{10,2},{12,4},{14,6},{16,8},{18,... | collective-permute-start | bytes 786440 | tf_op jit(solution)/shard_map/ppermute | solution.py:78
  5.2 1.8 %collective-permute-start.2 = (f32[2,32,4,256]{3,1,2,0:T(8,128)S(1)}, f32[2,32,4,256]{3,1,2,0:T(8,128)S(1)}, u32[]{:S(2)}, u32[]{:S(2)}) collective-permute-start(f32[2,32,4,256]{3,1,2,0:T(8,128)S(1)} %fusion), channel_id=1, source_target_pairs={{0,16},{2,18},{4,20},{6,22},{8,24},{10,26},{12,28},{14,30},{16,0},... | collective-permute-start | bytes 786440 | tf_op jit(solution)/shard_map/ppermute | solution.py:78
  7.0 6.3 %collective-permute-start.9 = (s32[1]{0:T(128)}, s32[1]{0:T(128)}, u32[]{:S(2)}, u32[]{:S(2)}) collective-permute-start(s32[1]{0:T(128)} %param.13), channel_id=1, source_target_pairs={{128,0},{130,2},{132,4},{134,6},{136,8},{138,10},{140,12},{142,14}... | collective-permute-start | bytes 20 | tf_op jit(solution)/shard_map/ppermute | solution.py:75
  13.3 0.0 collective-permute-start.12
  13.3 0.1 fusion.3
  13.4 0.0 collective-permute-done
  13.4 2.7 %collective-permute-done.1 = f32[2,32,4,256]{3,1,2,0:T(8,128)S(1)} collective-permute-done((f32[2,32,4,256]{3,1,2,0:T(8,128)S(1)}, f32[2,32,4,256]{3,1,2,0:T(8,128)S(1)}, u32[]{:S(2)}, u32[]{:S(2)}) %collective-permute-start.1) | collective-permute-done | bytes 262176 | tf_op jit(solution)/shard_map/ppermute | solution.py:78
  16.1 1.7 %collective-permute-done.2 = f32[2,32,4,256]{3,1,2,0:T(8,128)S(1)} collective-permute-done((f32[2,32,4,256]{3,1,2,0:T(8,128)S(1)}, f32[2,32,4,256]{3,1,2,0:T(8,128)S(1)}, u32[]{:S(2)}, u32[]{:S(2)}) %collective-permute-start.2) | collective-permute-done | bytes 262176 | tf_op jit(solution)/shard_map/ppermute | solution.py:78
  17.8 0.2 add_add_fusion.2
  18.0 1.7 %collective-permute-start.3 = (f32[2,32,4,256]{3,1,2,0:T(8,128)S(1)}, f32[2,32,4,256]{3,1,2,0:T(8,128)S(1)}, u32[]{:S(2)}, u32[]{:S(2)}) collective-permute-start(f32[2,32,4,256]{3,1,2,0:T(8,128)S(1)} %add_add_fusion.2), channel_id=1, source_target_pairs={{0,2},{2,4},{4,6},{6,0},{8,10},{10,12},{12,14},{14,8},{16,18},{18,... | collective-permute-start | bytes 786440 | tf_op jit(solution)/shard_map/ppermute | solution.py:78
  19.6 1.7 %collective-permute-start.4 = (f32[2,32,4,256]{3,1,2,0:T(8,128)S(1)}, f32[2,32,4,256]{3,1,2,0:T(8,128)S(1)}, u32[]{:S(2)}, u32[]{:S(2)}) collective-permute-start(f32[2,32,4,256]{3,1,2,0:T(8,128)S(1)} %add_add_fusion.2), channel_id=1, source_target_pairs={{0,6},{2,0},{4,2},{6,4},{8,14},{10,8},{12,10},{14,12},{16,22},{18,... | collective-permute-start | bytes 786440 | tf_op jit(solution)/shard_map/ppermute | solution.py:78
  21.3 2.0 %collective-permute-start.5 = (f32[2,32,4,256]{3,1,2,0:T(8,128)S(1)}, f32[2,32,4,256]{3,1,2,0:T(8,128)S(1)}, u32[]{:S(2)}, u32[]{:S(2)}) collective-permute-start(f32[2,32,4,256]{3,1,2,0:T(8,128)S(1)} %add_add_fusion.2), channel_id=1, source_target_pairs={{0,4},{2,6},{4,0},{6,2},{8,12},{10,14},{12,8},{14,10},{16,20},{18,... | collective-permute-start | bytes 786440 | tf_op jit(solution)/shard_map/ppermute | solution.py:78
  24.0 0.1 copy.17
  24.1 0.6 reshape.20.coef_ref
  24.6 0.1 copy.18
  24.8 0.5 copy-done.5
  25.3 0.1 copy.20
  25.4 0.7 pad.16.state_ref
  26.2 0.6 pad.19.out_ref
  26.8 0.1 copy-done.3
  26.9 0.6 pad.18.lift_ref
  27.5 0.0 collective-permute-done.9
  27.5 0.0 collective-permute-start.11
  29.6 0.0 collective-permute-done.12
  29.6 1.9 %collective-permute-done.4 = f32[2,32,4,256]{3,1,2,0:T(8,128)S(1)} collective-permute-done((f32[2,32,4,256]{3,1,2,0:T(8,128)S(1)}, f32[2,32,4,256]{3,1,2,0:T(8,128)S(1)}, u32[]{:S(2)}, u32[]{:S(2)}) %collective-permute-start.4) | collective-permute-done | bytes 262176 | tf_op jit(solution)/shard_map/ppermute | solution.py:78
  31.5 1.8 %collective-permute-done.5 = f32[2,32,4,256]{3,1,2,0:T(8,128)S(1)} collective-permute-done((f32[2,32,4,256]{3,1,2,0:T(8,128)S(1)}, f32[2,32,4,256]{3,1,2,0:T(8,128)S(1)}, u32[]{:S(2)}, u32[]{:S(2)}) %collective-permute-start.5) | collective-permute-done | bytes 262176 | tf_op jit(solution)/shard_map/ppermute | solution.py:78
  33.3 0.1 add_add_fusion.1
  33.4 2.0 %collective-permute-start.6 = (f32[2,32,4,256]{3,1,2,0:T(8,128)S(1)}, f32[2,32,4,256]{3,1,2,0:T(8,128)S(1)}, u32[]{:S(2)}, u32[]{:S(2)}) collective-permute-start(f32[2,32,4,256]{3,1,2,0:T(8,128)S(1)} %add_add_fusion.1), channel_id=1, source_target_pairs={{0,32},{2,34},{4,36},{6,38},{8,40},{10,42},{12,44},{14,46},{16,48}... | collective-permute-start | bytes 786440 | tf_op jit(solution)/shard_map/ppermute | solution.py:78
  35.4 0.1 collective-permute-start.7
  35.5 4.4 %collective-permute-start.8 = (f32[2,32,4,256]{3,1,2,0:T(8,128)S(1)}, f32[2,32,4,256]{3,1,2,0:T(8,128)S(1)}, u32[]{:S(2)}, u32[]{:S(2)}) collective-permute-start(f32[2,32,4,256]{3,1,2,0:T(8,128)S(1)} %add_add_fusion.1), channel_id=1, source_target_pairs={{0,64},{2,66},{4,68},{6,70},{8,72},{10,74},{12,76},{14,78},{16,80}... | collective-permute-start | bytes 786440 | tf_op jit(solution)/shard_map/ppermute | solution.py:78
  39.9 0.6 maximum_convert_fusion.gain_ref
  40.4 0.0 collective-permute-done.11
  40.5 4.9 %collective-permute-done.6 = f32[2,32,4,256]{3,1,2,0:T(8,128)S(1)} collective-permute-done((f32[2,32,4,256]{3,1,2,0:T(8,128)S(1)}, f32[2,32,4,256]{3,1,2,0:T(8,128)S(1)}, u32[]{:S(2)}, u32[]{:S(2)}) %collective-permute-start.6) | collective-permute-done | bytes 262176 | tf_op jit(solution)/shard_map/ppermute | solution.py:78
  45.3 9.5 %collective-permute-done.8 = f32[2,32,4,256]{3,1,2,0:T(8,128)S(1)} collective-permute-done((f32[2,32,4,256]{3,1,2,0:T(8,128)S(1)}, f32[2,32,4,256]{3,1,2,0:T(8,128)S(1)}, u32[]{:S(2)}, u32[]{:S(2)}) %collective-permute-start.8) | collective-permute-done | bytes 262176 | tf_op jit(solution)/shard_map/ppermute | solution.py:78
  54.9 0.1 add_add_fusion
  55.0 4.5 %collective-permute-start.10 = (f32[2,4,256]{2,1,0:T(4,128)S(1)}, f32[2,4,256]{2,1,0:T(4,128)S(1)}, u32[]{:S(2)}, u32[]{:S(2)}) collective-permute-start(f32[2,4,256]{2,1,0:T(4,128)S(1)} %bitcast.56), channel_id=1, source_target_pairs={{0,128},{2,130},{4,132},{6,134},{8,136},{10,138},{12,140},{14,142}... | collective-permute-start | bytes 24584 | tf_op jit(solution)/shard_map/ppermute | solution.py:82
  59.5 0.9 pad_maximum_fusion.conv_ref
  60.4 2.4 %collective-permute-done.10 = f32[2,4,256]{2,1,0:T(4,128)S(1)} collective-permute-done((f32[2,4,256]{2,1,0:T(4,128)S(1)}, f32[2,4,256]{2,1,0:T(4,128)S(1)}, u32[]{:S(2)}, u32[]{:S(2)}) %collective-permute-start.10) | collective-permute-done | bytes 8224 | tf_op jit(solution)/shard_map/ppermute | solution.py:82
  62.8 0.1 copy.19
  63.0 0.9 pad.17.means_ref
  63.8 25.9 %shard_map.100 = f32[512,128]{1,0:T(8,128)} custom-call(f32[40]{0:T(128)} %reshape.20.coef_ref, f32[512,128]{1,0:T(8,128)} %pad.16.state_ref, f32[512,128]{1,0:T(8,128)} %pad.17.means_ref, f32[128,128]{1,0:T(8,128)} %pad.18.lift_ref, f32[1,128]{1,0:T(1,128)} %bitcast.58, bf16[2,1152,128]{2,1,0:T(8,128)(2,1)} %pad_maximum_fusion.conv_ref, ...), custom_call_target="tpu_custom_call" | custom-call | tf_op jit(solution)/shard_map/pallas_call | solution.py:158
  89.7 1.1 %copy.21 = f32[2,256,4]{1,2,0:T(4,128)S(1)} copy(f32[2,256,4]{2,1,0:T(8,128)} %bitcast.55) | data formatting | bytes 16384 | tf_op jit(solution)/shard_map/reshape | solution.py:246
  90.8 0.6 fusion.1
  (22 shorter events, 0.2 us)
Async XLA Ops:
  0.0 1.0 %copy-start = (f32[1,4,32,4,256]{4,3,2,1,0:T(4,128)S(1)}, f32[1,4,32,4,256]{4,3,2,1,0:T(4,128)}, u32[]{:S(2)}) copy-start(f32[1,4,32,4,256]{4,3,2,1,0:T(4,128)} %param.11) | copy-start | bytes 1572868
  1.0 0.7 copy-start.7
  1.8 11.5 %copy-start.6 = (bf16[1,128]{1,0:T(2,128)(2,1)S(1)}, bf16[1,128]{1,0:T(2,128)(2,1)}, u32[]{:S(2)}) copy-start(bf16[1,128]{1,0:T(2,128)(2,1)} %param.18) | copy-start | bytes 772
  1.8 11.5 %copy-start.2 = (f32[9]{0:T(128)S(1)}, f32[9]{0:T(128)}, u32[]{:S(2)}) copy-start(f32[9]{0:T(128)} %param.14) | copy-start | bytes 112
  1.9 11.5 %collective-permute-start = (f32[2,32,4,256]{3,1,2,0:T(8,128)S(1)}, f32[2,32,4,256]{3,1,2,0:T(8,128)S(1)}, u32[]{:S(2)}, u32[]{:S(2)}) collective-permute-start(f32[2,32,4,256]{3,1,2,0:T(8,128)S(1)} %fusion), channel_id=1, source_target_pairs={{0,8},{2,10},{4,12},{6,14},{8,16},{10,18},{12,20},{14,22},{16,24},... | collective-permute-start | bytes 786440 | tf_op jit(solution)/shard_map/ppermute | solution.py:78
  3.4 12.7 %collective-permute-start.1 = (f32[2,32,4,256]{3,1,2,0:T(8,128)S(1)}, f32[2,32,4,256]{3,1,2,0:T(8,128)S(1)}, u32[]{:S(2)}, u32[]{:S(2)}) collective-permute-start(f32[2,32,4,256]{3,1,2,0:T(8,128)S(1)} %fusion), channel_id=1, source_target_pairs={{0,24},{2,26},{4,28},{6,30},{8,0},{10,2},{12,4},{14,6},{16,8},{18,... | collective-permute-start | bytes 786440 | tf_op jit(solution)/shard_map/ppermute | solution.py:78
  5.2 12.6 %collective-permute-start.2 = (f32[2,32,4,256]{3,1,2,0:T(8,128)S(1)}, f32[2,32,4,256]{3,1,2,0:T(8,128)S(1)}, u32[]{:S(2)}, u32[]{:S(2)}) collective-permute-start(f32[2,32,4,256]{3,1,2,0:T(8,128)S(1)} %fusion), channel_id=1, source_target_pairs={{0,16},{2,18},{4,20},{6,22},{8,24},{10,26},{12,28},{14,30},{16,0},... | collective-permute-start | bytes 786440 | tf_op jit(solution)/shard_map/ppermute | solution.py:78
  7.0 20.5 %collective-permute-start.9 = (s32[1]{0:T(128)}, s32[1]{0:T(128)}, u32[]{:S(2)}, u32[]{:S(2)}) collective-permute-start(s32[1]{0:T(128)} %param.13), channel_id=1, source_target_pairs={{128,0},{130,2},{132,4},{134,6},{136,8},{138,10},{140,12},{142,14}... | collective-permute-start | bytes 20 | tf_op jit(solution)/shard_map/ppermute | solution.py:75
  13.3 16.3 %collective-permute-start.12 = (bf16[1,128]{1,0:T(2,128)(2,1)S(1)}, bf16[1,128]{1,0:T(2,128)(2,1)S(1)}, u32[]{:S(2)}, u32[]{:S(2)}) collective-permute-start(bf16[1,128]{1,0:T(2,128)(2,1)S(1)} %copy-done.6), channel_id=1, source_target_pairs={{0,1},{1,0},{2,3},{3,2},{4,5},{5,4},{6,7},{7,6},{8,9},{9,8},{10,11... | collective-permute-start | bytes 776 | tf_op jit(solution)/shard_map/ppermute | solution.py:212
  13.4 9.9 %copy-start.4 = (f32[1,4,4,256]{3,2,1,0:T(4,128)S(1)}, f32[1,4,4,256]{3,2,1,0:T(4,128)}, u32[]{:S(2)}) copy-start(f32[1,4,4,256]{3,2,1,0:T(4,128)} %param.10) | copy-start | bytes 49156
  18.0 11.6 %collective-permute-start.3 = (f32[2,32,4,256]{3,1,2,0:T(8,128)S(1)}, f32[2,32,4,256]{3,1,2,0:T(8,128)S(1)}, u32[]{:S(2)}, u32[]{:S(2)}) collective-permute-start(f32[2,32,4,256]{3,1,2,0:T(8,128)S(1)} %add_add_fusion.2), channel_id=1, source_target_pairs={{0,2},{2,4},{4,6},{6,0},{8,10},{10,12},{12,14},{14,8},{16,18},{18,... | collective-permute-start | bytes 786440 | tf_op jit(solution)/shard_map/ppermute | solution.py:78
  19.6 11.9 %collective-permute-start.4 = (f32[2,32,4,256]{3,1,2,0:T(8,128)S(1)}, f32[2,32,4,256]{3,1,2,0:T(8,128)S(1)}, u32[]{:S(2)}, u32[]{:S(2)}) collective-permute-start(f32[2,32,4,256]{3,1,2,0:T(8,128)S(1)} %add_add_fusion.2), channel_id=1, source_target_pairs={{0,6},{2,0},{4,2},{6,4},{8,14},{10,8},{12,10},{14,12},{16,22},{18,... | collective-permute-start | bytes 786440 | tf_op jit(solution)/shard_map/ppermute | solution.py:78
  21.3 12.0 %collective-permute-start.5 = (f32[2,32,4,256]{3,1,2,0:T(8,128)S(1)}, f32[2,32,4,256]{3,1,2,0:T(8,128)S(1)}, u32[]{:S(2)}, u32[]{:S(2)}) collective-permute-start(f32[2,32,4,256]{3,1,2,0:T(8,128)S(1)} %add_add_fusion.2), channel_id=1, source_target_pairs={{0,4},{2,6},{4,0},{6,2},{8,12},{10,14},{12,8},{14,10},{16,20},{18,... | collective-permute-start | bytes 786440 | tf_op jit(solution)/shard_map/ppermute | solution.py:78
  24.6 0.7 copy-start.5
  25.4 2.1 %copy-start.1 = (bf16[1,9,128,128]{3,2,1,0:T(8,128)(2,1)S(1)}, bf16[1,9,128,128]{3,2,1,0:T(8,128)(2,1)}, u32[]{:S(2)}) copy-start(bf16[1,9,128,128]{3,2,1,0:T(8,128)(2,1)} %param.17) | copy-start | bytes 884740
  26.2 0.7 copy-start.3
  27.5 12.9 %collective-permute-start.11 = (bf16[1,9,128,128]{3,2,1,0:T(8,128)(2,1)S(1)}, bf16[1,9,128,128]{3,2,1,0:T(8,128)(2,1)S(1)}, u32[]{:S(2)}, u32[]{:S(2)}) collective-permute-start(bf16[1,9,128,128]{3,2,1,0:T(8,128)(2,1)S(1)} %copy-done.1), channel_id=1, source_target_pairs={{0,1},{1,0},{2,3},{3,2},{4,5},{5,4},{6,7},{7,6},{8,9},{9,8},{10,11... | collective-permute-start | bytes 884744 | tf_op jit(solution)/shard_map/ppermute | solution.py:211
  33.4 12.0 %collective-permute-start.6 = (f32[2,32,4,256]{3,1,2,0:T(8,128)S(1)}, f32[2,32,4,256]{3,1,2,0:T(8,128)S(1)}, u32[]{:S(2)}, u32[]{:S(2)}) collective-permute-start(f32[2,32,4,256]{3,1,2,0:T(8,128)S(1)} %add_add_fusion.1), channel_id=1, source_target_pairs={{0,32},{2,34},{4,36},{6,38},{8,40},{10,42},{12,44},{14,46},{16,48}... | collective-permute-start | bytes 786440 | tf_op jit(solution)/shard_map/ppermute | solution.py:78
  35.4 10.0 %collective-permute-start.7 = (f32[2,32,4,256]{3,1,2,0:T(8,128)S(1)}, f32[2,32,4,256]{3,1,2,0:T(8,128)S(1)}, u32[]{:S(2)}, u32[]{:S(2)}) collective-permute-start(f32[2,32,4,256]{3,1,2,0:T(8,128)S(1)} %add_add_fusion.1), channel_id=1, source_target_pairs={{0,224},{2,226},{4,228},{6,230},{8,232},{10,234},{12,236},{14,238}... | collective-permute-start | bytes 786440 | tf_op jit(solution)/shard_map/ppermute | solution.py:78
  35.5 19.4 %collective-permute-start.8 = (f32[2,32,4,256]{3,1,2,0:T(8,128)S(1)}, f32[2,32,4,256]{3,1,2,0:T(8,128)S(1)}, u32[]{:S(2)}, u32[]{:S(2)}) collective-permute-start(f32[2,32,4,256]{3,1,2,0:T(8,128)S(1)} %add_add_fusion.1), channel_id=1, source_target_pairs={{0,64},{2,66},{4,68},{6,70},{8,72},{10,74},{12,76},{14,78},{16,80}... | collective-permute-start | bytes 786440 | tf_op jit(solution)/shard_map/ppermute | solution.py:78
  55.0 7.8 %collective-permute-start.10 = (f32[2,4,256]{2,1,0:T(4,128)S(1)}, f32[2,4,256]{2,1,0:T(4,128)S(1)}, u32[]{:S(2)}, u32[]{:S(2)}) collective-permute-start(f32[2,4,256]{2,1,0:T(4,128)S(1)} %bitcast.56), channel_id=1, source_target_pairs={{0,128},{2,130},{4,132},{6,134},{8,136},{10,138},{12,140},{14,142}... | collective-permute-start | bytes 24584 | tf_op jit(solution)/shard_map/ppermute | solution.py:82

commit v5 on v4

--- a/solution.py
+++ b/solution.py
@@ -94,10 +94,20 @@
 def chain_kernel(coef_ref, state_ref, means_ref, lift_ref, embed_ref, conv_ref, gain_ref, out_ref, result_ref):
     rows, lanes = state_ref.shape
     pixel = lax.broadcasted_iota(jnp.int32, (rows, lanes), 0) % (SIDE * SIDE)
-    row = pixel // SIDE
     col = pixel % SIDE
-    row_ok = {a: (row + a >= 0) & (row + a < SIDE) for a in (-1, 1)}
     col_ok = {b: (col + b >= 0) & (col + b < SIDE) for b in (-1, 1)}
+    tiles = rows // (SIDE * SIDE)
+    zero_row = jnp.zeros((SIDE, lanes), jnp.bfloat16)
+
+    def shift_rows(moved, a):
+        parts = []
+        for t in range(tiles):
+            tile = moved[t * SIDE * SIDE : (t + 1) * SIDE * SIDE]
+            if a == 1:
+                parts += [tile[SIDE:], zero_row]
+            else:
+                parts += [zero_row, tile[:-SIDE]]
+        return jnp.concatenate(parts, axis=0)
 
     def conv(gated, index):
         columns = {}
@@ -105,18 +115,11 @@
             moved = gated
             if b:
                 moved = jnp.where(col_ok[b], pltpu.roll(gated, (-b) % rows, 0), 0.0)
-            columns[b] = moved
+            columns[b] = moved.astype(jnp.bfloat16)
         windows = []
         for a in (-1, 0, 1):
             for b in (-1, 0, 1):
-                moved = columns[b]
-                if a == 1:
-                    moved = jnp.concatenate([moved[SIDE:], moved[:SIDE]], axis=0)
-                if a == -1:
-                    moved = jnp.concatenate([moved[-SIDE:], moved[:-SIDE]], axis=0)
-                if a:
-                    moved = jnp.where(row_ok[a], moved, 0.0)
-                windows.append(moved.astype(jnp.bfloat16))
+                windows.append(columns[b] if a == 0 else shift_rows(columns[b], a))
         stacked = jnp.concatenate(windows, axis=1)
         return jnp.dot(stacked, conv_ref[index], preferred_element_type=jnp.float32)
 

time: 91.7 us -> 90.4 us (0.986)
  Pallas kernels: 25.9 us -> 24.8 us
    pallas_call x1, Pallas kernels: 25.9 us -> 24.8 us  [run_chain(): pl.pallas_call(chain_kernel, out_shape=jax.ShapeDtypeStruct(state.shape,...]
where the time goes in v5:
time: 90.4 us; the launch traced here: 90.1 us
  starting transfers between devices  27.6 us (31%)
  waiting for transfers between devices  24.9 us (28%)
  Pallas kernels  24.8 us (27%)
  local copies, waits for them, and re-layouts  7.3 us (8%)
  between operations  2.84 us (3%)
  other arithmetic  2.71 us (3%)
    pallas_call x1, Pallas kernels, run_chain(): pl.pallas_call(chain_kernel, out_shape=jax.ShapeDtypeStruct(state.shape,...  24.8 us
    ppermute x9, waiting for transfers between devices, broadcast_mean(): arrived = [lax.ppermute(block, 'member', shifts[d]) for d in stage]  22.5 us
    ppermute x9, starting transfers between devices, broadcast_mean(): arrived = [lax.ppermute(block, 'member', shifts[d]) for d in stage]  16.9 us
    ppermute x1, starting transfers between devices, broadcast_mean(): wanted = lax.ppermute(tile[None], 'member', reversed_pairs(last_pairs))[0]  6.29 us
    ppermute x1, starting transfers between devices, broadcast_mean(): arrived = lax.ppermute(sent, 'member', last_pairs)  4.36 us
    ppermute x1, waiting for transfers between devices, broadcast_mean(): arrived = lax.ppermute(sent, 'member', last_pairs)  2.4 us
    unnamed x18, local copies, waits for them, and re-layouts  2.4 us
  transfers between devices with their start and end apart: 13, of which 7 were waited for; matrix products, arithmetic and copies ran while one was open for 5% of the time, Pallas kernels for 0%

profile of v5, /device:TPU:32, one launch (start us, length us, event | category | flops | bytes accessed | tf_op | source)
XLA Modules:
  0.0 90.1 jit_solution(13514247441978023872)
XLA Ops:
  0.0 1.0 %copy-done = f32[1,4,32,4,256]{4,3,2,1,0:T(4,128)S(1)} copy-done((f32[1,4,32,4,256]{4,3,2,1,0:T(4,128)S(1)}, f32[1,4,32,4,256]{4,3,2,1,0:T(4,128)}, u32[]{:S(2)}) %copy-start) | copy-done | bytes 524312
  1.1 0.6 copy-done.7
  1.7 0.1 dynamic-slice_compare_fusion
  1.8 0.1 fusion
  1.9 1.6 %collective-permute-start = (f32[2,32,4,256]{3,1,2,0:T(8,128)S(1)}, f32[2,32,4,256]{3,1,2,0:T(8,128)S(1)}, u32[]{:S(2)}, u32[]{:S(2)}) collective-permute-start(f32[2,32,4,256]{3,1,2,0:T(8,128)S(1)} %fusion), channel_id=1, source_target_pairs={{0,8},{2,10},{4,12},{6,14},{8,16},{10,18},{12,20},{14,22},{16,24},... | collective-permute-start | bytes 786440 | tf_op jit(solution)/shard_map/ppermute | solution.py:78
  3.4 1.7 %collective-permute-start.1 = (f32[2,32,4,256]{3,1,2,0:T(8,128)S(1)}, f32[2,32,4,256]{3,1,2,0:T(8,128)S(1)}, u32[]{:S(2)}, u32[]{:S(2)}) collective-permute-start(f32[2,32,4,256]{3,1,2,0:T(8,128)S(1)} %fusion), channel_id=1, source_target_pairs={{0,24},{2,26},{4,28},{6,30},{8,0},{10,2},{12,4},{14,6},{16,8},{18,... | collective-permute-start | bytes 786440 | tf_op jit(solution)/shard_map/ppermute | solution.py:78
  5.2 1.8 %collective-permute-start.2 = (f32[2,32,4,256]{3,1,2,0:T(8,128)S(1)}, f32[2,32,4,256]{3,1,2,0:T(8,128)S(1)}, u32[]{:S(2)}, u32[]{:S(2)}) collective-permute-start(f32[2,32,4,256]{3,1,2,0:T(8,128)S(1)} %fusion), channel_id=1, source_target_pairs={{0,16},{2,18},{4,20},{6,22},{8,24},{10,26},{12,28},{14,30},{16,0},... | collective-permute-start | bytes 786440 | tf_op jit(solution)/shard_map/ppermute | solution.py:78
  7.0 6.3 %collective-permute-start.9 = (s32[1]{0:T(128)}, s32[1]{0:T(128)}, u32[]{:S(2)}, u32[]{:S(2)}) collective-permute-start(s32[1]{0:T(128)} %param.13), channel_id=1, source_target_pairs={{128,0},{130,2},{132,4},{134,6},{136,8},{138,10},{140,12},{142,14}... | collective-permute-start | bytes 20 | tf_op jit(solution)/shard_map/ppermute | solution.py:75
  13.3 0.0 collective-permute-start.12
  13.3 0.1 fusion.3
  13.4 0.0 collective-permute-done
  13.4 2.7 %collective-permute-done.1 = f32[2,32,4,256]{3,1,2,0:T(8,128)S(1)} collective-permute-done((f32[2,32,4,256]{3,1,2,0:T(8,128)S(1)}, f32[2,32,4,256]{3,1,2,0:T(8,128)S(1)}, u32[]{:S(2)}, u32[]{:S(2)}) %collective-permute-start.1) | collective-permute-done | bytes 262176 | tf_op jit(solution)/shard_map/ppermute | solution.py:78
  16.1 1.7 %collective-permute-done.2 = f32[2,32,4,256]{3,1,2,0:T(8,128)S(1)} collective-permute-done((f32[2,32,4,256]{3,1,2,0:T(8,128)S(1)}, f32[2,32,4,256]{3,1,2,0:T(8,128)S(1)}, u32[]{:S(2)}, u32[]{:S(2)}) %collective-permute-start.2) | collective-permute-done | bytes 262176 | tf_op jit(solution)/shard_map/ppermute | solution.py:78
  17.8 0.2 add_add_fusion.2
  18.0 1.7 %collective-permute-start.3 = (f32[2,32,4,256]{3,1,2,0:T(8,128)S(1)}, f32[2,32,4,256]{3,1,2,0:T(8,128)S(1)}, u32[]{:S(2)}, u32[]{:S(2)}) collective-permute-start(f32[2,32,4,256]{3,1,2,0:T(8,128)S(1)} %add_add_fusion.2), channel_id=1, source_target_pairs={{0,2},{2,4},{4,6},{6,0},{8,10},{10,12},{12,14},{14,8},{16,18},{18,... | collective-permute-start | bytes 786440 | tf_op jit(solution)/shard_map/ppermute | solution.py:78
  19.6 1.7 %collective-permute-start.4 = (f32[2,32,4,256]{3,1,2,0:T(8,128)S(1)}, f32[2,32,4,256]{3,1,2,0:T(8,128)S(1)}, u32[]{:S(2)}, u32[]{:S(2)}) collective-permute-start(f32[2,32,4,256]{3,1,2,0:T(8,128)S(1)} %add_add_fusion.2), channel_id=1, source_target_pairs={{0,6},{2,0},{4,2},{6,4},{8,14},{10,8},{12,10},{14,12},{16,22},{18,... | collective-permute-start | bytes 786440 | tf_op jit(solution)/shard_map/ppermute | solution.py:78
  21.3 2.0 %collective-permute-start.5 = (f32[2,32,4,256]{3,1,2,0:T(8,128)S(1)}, f32[2,32,4,256]{3,1,2,0:T(8,128)S(1)}, u32[]{:S(2)}, u32[]{:S(2)}) collective-permute-start(f32[2,32,4,256]{3,1,2,0:T(8,128)S(1)} %add_add_fusion.2), channel_id=1, source_target_pairs={{0,4},{2,6},{4,0},{6,2},{8,12},{10,14},{12,8},{14,10},{16,20},{18,... | collective-permute-start | bytes 786440 | tf_op jit(solution)/shard_map/ppermute | solution.py:78
  24.0 0.1 copy.17
  24.1 0.6 reshape.20.coef_ref
  24.6 0.1 copy.18
  24.8 0.5 copy-done.5
  25.3 0.1 copy.20
  25.4 0.7 pad.16.state_ref
  26.2 0.6 pad.19.out_ref
  26.8 0.1 copy-done.3
  26.9 0.6 pad.18.lift_ref
  27.5 0.0 collective-permute-done.9
  27.5 0.0 collective-permute-start.11
  29.6 0.0 collective-permute-done.12
  29.6 0.0 collective-permute-done.3
  29.6 1.9 %collective-permute-done.4 = f32[2,32,4,256]{3,1,2,0:T(8,128)S(1)} collective-permute-done((f32[2,32,4,256]{3,1,2,0:T(8,128)S(1)}, f32[2,32,4,256]{3,1,2,0:T(8,128)S(1)}, u32[]{:S(2)}, u32[]{:S(2)}) %collective-permute-start.4) | collective-permute-done | bytes 262176 | tf_op jit(solution)/shard_map/ppermute | solution.py:78
  31.5 1.8 %collective-permute-done.5 = f32[2,32,4,256]{3,1,2,0:T(8,128)S(1)} collective-permute-done((f32[2,32,4,256]{3,1,2,0:T(8,128)S(1)}, f32[2,32,4,256]{3,1,2,0:T(8,128)S(1)}, u32[]{:S(2)}, u32[]{:S(2)}) %collective-permute-start.5) | collective-permute-done | bytes 262176 | tf_op jit(solution)/shard_map/ppermute | solution.py:78
  33.3 0.1 add_add_fusion.1
  33.4 2.0 %collective-permute-start.6 = (f32[2,32,4,256]{3,1,2,0:T(8,128)S(1)}, f32[2,32,4,256]{3,1,2,0:T(8,128)S(1)}, u32[]{:S(2)}, u32[]{:S(2)}) collective-permute-start(f32[2,32,4,256]{3,1,2,0:T(8,128)S(1)} %add_add_fusion.1), channel_id=1, source_target_pairs={{0,32},{2,34},{4,36},{6,38},{8,40},{10,42},{12,44},{14,46},{16,48}... | collective-permute-start | bytes 786440 | tf_op jit(solution)/shard_map/ppermute | solution.py:78
  35.4 0.1 collective-permute-start.7
  35.5 4.4 %collective-permute-start.8 = (f32[2,32,4,256]{3,1,2,0:T(8,128)S(1)}, f32[2,32,4,256]{3,1,2,0:T(8,128)S(1)}, u32[]{:S(2)}, u32[]{:S(2)}) collective-permute-start(f32[2,32,4,256]{3,1,2,0:T(8,128)S(1)} %add_add_fusion.1), channel_id=1, source_target_pairs={{0,64},{2,66},{4,68},{6,70},{8,72},{10,74},{12,76},{14,78},{16,80}... | collective-permute-start | bytes 786440 | tf_op jit(solution)/shard_map/ppermute | solution.py:78
  39.9 0.6 maximum_convert_fusion.gain_ref
  40.5 4.9 %collective-permute-done.6 = f32[2,32,4,256]{3,1,2,0:T(8,128)S(1)} collective-permute-done((f32[2,32,4,256]{3,1,2,0:T(8,128)S(1)}, f32[2,32,4,256]{3,1,2,0:T(8,128)S(1)}, u32[]{:S(2)}, u32[]{:S(2)}) %collective-permute-start.6) | collective-permute-done | bytes 262176 | tf_op jit(solution)/shard_map/ppermute | solution.py:78
  45.3 9.5 %collective-permute-done.8 = f32[2,32,4,256]{3,1,2,0:T(8,128)S(1)} collective-permute-done((f32[2,32,4,256]{3,1,2,0:T(8,128)S(1)}, f32[2,32,4,256]{3,1,2,0:T(8,128)S(1)}, u32[]{:S(2)}, u32[]{:S(2)}) %collective-permute-start.8) | collective-permute-done | bytes 262176 | tf_op jit(solution)/shard_map/ppermute | solution.py:78
  54.9 0.1 add_add_fusion
  55.0 4.4 %collective-permute-start.10 = (f32[2,4,256]{2,1,0:T(4,128)S(1)}, f32[2,4,256]{2,1,0:T(4,128)S(1)}, u32[]{:S(2)}, u32[]{:S(2)}) collective-permute-start(f32[2,4,256]{2,1,0:T(4,128)S(1)} %bitcast.56), channel_id=1, source_target_pairs={{0,128},{2,130},{4,132},{6,134},{8,136},{10,138},{12,140},{14,142}... | collective-permute-start | bytes 24584 | tf_op jit(solution)/shard_map/ppermute | solution.py:82
  59.3 0.9 pad_maximum_fusion.conv_ref
  60.2 2.4 %collective-permute-done.10 = f32[2,4,256]{2,1,0:T(4,128)S(1)} collective-permute-done((f32[2,4,256]{2,1,0:T(4,128)S(1)}, f32[2,4,256]{2,1,0:T(4,128)S(1)}, u32[]{:S(2)}, u32[]{:S(2)}) %collective-permute-start.10) | collective-permute-done | bytes 8224 | tf_op jit(solution)/shard_map/ppermute | solution.py:82
  62.6 0.1 copy.19
  62.8 0.9 pad.17.means_ref
  63.7 24.8 %shard_map.100 = f32[512,128]{1,0:T(8,128)} custom-call(f32[40]{0:T(128)} %reshape.20.coef_ref, f32[512,128]{1,0:T(8,128)} %pad.16.state_ref, f32[512,128]{1,0:T(8,128)} %pad.17.means_ref, f32[128,128]{1,0:T(8,128)} %pad.18.lift_ref, f32[1,128]{1,0:T(1,128)} %bitcast.58, bf16[2,1152,128]{2,1,0:T(8,128)(2,1)} %pad_maximum_fusion.conv_ref, ...), custom_call_target="tpu_custom_call" | custom-call | tf_op jit(solution)/shard_map/pallas_call | solution.py:161
  88.4 1.1 %copy.21 = f32[2,256,4]{1,2,0:T(4,128)S(1)} copy(f32[2,256,4]{2,1,0:T(8,128)} %bitcast.55) | data formatting | bytes 16384 | tf_op jit(solution)/shard_map/reshape | solution.py:249
  89.5 0.6 fusion.1
  (22 shorter events, 0.2 us)
Async XLA Ops:
  0.0 1.0 %copy-start = (f32[1,4,32,4,256]{4,3,2,1,0:T(4,128)S(1)}, f32[1,4,32,4,256]{4,3,2,1,0:T(4,128)}, u32[]{:S(2)}) copy-start(f32[1,4,32,4,256]{4,3,2,1,0:T(4,128)} %param.11) | copy-start | bytes 1572868
  1.0 0.7 copy-start.7
  1.8 11.5 %copy-start.6 = (bf16[1,128]{1,0:T(2,128)(2,1)S(1)}, bf16[1,128]{1,0:T(2,128)(2,1)}, u32[]{:S(2)}) copy-start(bf16[1,128]{1,0:T(2,128)(2,1)} %param.18) | copy-start | bytes 772
  1.8 11.5 %copy-start.2 = (f32[9]{0:T(128)S(1)}, f32[9]{0:T(128)}, u32[]{:S(2)}) copy-start(f32[9]{0:T(128)} %param.14) | copy-start | bytes 112
  1.9 11.5 %collective-permute-start = (f32[2,32,4,256]{3,1,2,0:T(8,128)S(1)}, f32[2,32,4,256]{3,1,2,0:T(8,128)S(1)}, u32[]{:S(2)}, u32[]{:S(2)}) collective-permute-start(f32[2,32,4,256]{3,1,2,0:T(8,128)S(1)} %fusion), channel_id=1, source_target_pairs={{0,8},{2,10},{4,12},{6,14},{8,16},{10,18},{12,20},{14,22},{16,24},... | collective-permute-start | bytes 786440 | tf_op jit(solution)/shard_map/ppermute | solution.py:78
  3.4 12.7 %collective-permute-start.1 = (f32[2,32,4,256]{3,1,2,0:T(8,128)S(1)}, f32[2,32,4,256]{3,1,2,0:T(8,128)S(1)}, u32[]{:S(2)}, u32[]{:S(2)}) collective-permute-start(f32[2,32,4,256]{3,1,2,0:T(8,128)S(1)} %fusion), channel_id=1, source_target_pairs={{0,24},{2,26},{4,28},{6,30},{8,0},{10,2},{12,4},{14,6},{16,8},{18,... | collective-permute-start | bytes 786440 | tf_op jit(solution)/shard_map/ppermute | solution.py:78
  5.2 12.6 %collective-permute-start.2 = (f32[2,32,4,256]{3,1,2,0:T(8,128)S(1)}, f32[2,32,4,256]{3,1,2,0:T(8,128)S(1)}, u32[]{:S(2)}, u32[]{:S(2)}) collective-permute-start(f32[2,32,4,256]{3,1,2,0:T(8,128)S(1)} %fusion), channel_id=1, source_target_pairs={{0,16},{2,18},{4,20},{6,22},{8,24},{10,26},{12,28},{14,30},{16,0},... | collective-permute-start | bytes 786440 | tf_op jit(solution)/shard_map/ppermute | solution.py:78
  7.0 20.5 %collective-permute-start.9 = (s32[1]{0:T(128)}, s32[1]{0:T(128)}, u32[]{:S(2)}, u32[]{:S(2)}) collective-permute-start(s32[1]{0:T(128)} %param.13), channel_id=1, source_target_pairs={{128,0},{130,2},{132,4},{134,6},{136,8},{138,10},{140,12},{142,14}... | collective-permute-start | bytes 20 | tf_op jit(solution)/shard_map/ppermute | solution.py:75
  13.3 16.3 %collective-permute-start.12 = (bf16[1,128]{1,0:T(2,128)(2,1)S(1)}, bf16[1,128]{1,0:T(2,128)(2,1)S(1)}, u32[]{:S(2)}, u32[]{:S(2)}) collective-permute-start(bf16[1,128]{1,0:T(2,128)(2,1)S(1)} %copy-done.6), channel_id=1, source_target_pairs={{0,1},{1,0},{2,3},{3,2},{4,5},{5,4},{6,7},{7,6},{8,9},{9,8},{10,11... | collective-permute-start | bytes 776 | tf_op jit(solution)/shard_map/ppermute | solution.py:215
  13.4 9.9 %copy-start.4 = (f32[1,4,4,256]{3,2,1,0:T(4,128)S(1)}, f32[1,4,4,256]{3,2,1,0:T(4,128)}, u32[]{:S(2)}) copy-start(f32[1,4,4,256]{3,2,1,0:T(4,128)} %param.10) | copy-start | bytes 49156
  18.0 11.6 %collective-permute-start.3 = (f32[2,32,4,256]{3,1,2,0:T(8,128)S(1)}, f32[2,32,4,256]{3,1,2,0:T(8,128)S(1)}, u32[]{:S(2)}, u32[]{:S(2)}) collective-permute-start(f32[2,32,4,256]{3,1,2,0:T(8,128)S(1)} %add_add_fusion.2), channel_id=1, source_target_pairs={{0,2},{2,4},{4,6},{6,0},{8,10},{10,12},{12,14},{14,8},{16,18},{18,... | collective-permute-start | bytes 786440 | tf_op jit(solution)/shard_map/ppermute | solution.py:78
  19.6 11.9 %collective-permute-start.4 = (f32[2,32,4,256]{3,1,2,0:T(8,128)S(1)}, f32[2,32,4,256]{3,1,2,0:T(8,128)S(1)}, u32[]{:S(2)}, u32[]{:S(2)}) collective-permute-start(f32[2,32,4,256]{3,1,2,0:T(8,128)S(1)} %add_add_fusion.2), channel_id=1, source_target_pairs={{0,6},{2,0},{4,2},{6,4},{8,14},{10,8},{12,10},{14,12},{16,22},{18,... | collective-permute-start | bytes 786440 | tf_op jit(solution)/shard_map/ppermute | solution.py:78
  21.3 12.0 %collective-permute-start.5 = (f32[2,32,4,256]{3,1,2,0:T(8,128)S(1)}, f32[2,32,4,256]{3,1,2,0:T(8,128)S(1)}, u32[]{:S(2)}, u32[]{:S(2)}) collective-permute-start(f32[2,32,4,256]{3,1,2,0:T(8,128)S(1)} %add_add_fusion.2), channel_id=1, source_target_pairs={{0,4},{2,6},{4,0},{6,2},{8,12},{10,14},{12,8},{14,10},{16,20},{18,... | collective-permute-start | bytes 786440 | tf_op jit(solution)/shard_map/ppermute | solution.py:78
  24.6 0.7 copy-start.5
  25.4 2.1 %copy-start.1 = (bf16[1,9,128,128]{3,2,1,0:T(8,128)(2,1)S(1)}, bf16[1,9,128,128]{3,2,1,0:T(8,128)(2,1)}, u32[]{:S(2)}) copy-start(bf16[1,9,128,128]{3,2,1,0:T(8,128)(2,1)} %param.17) | copy-start | bytes 884740
  26.2 0.7 copy-start.3
  27.5 12.9 %collective-permute-start.11 = (bf16[1,9,128,128]{3,2,1,0:T(8,128)(2,1)S(1)}, bf16[1,9,128,128]{3,2,1,0:T(8,128)(2,1)S(1)}, u32[]{:S(2)}, u32[]{:S(2)}) collective-permute-start(bf16[1,9,128,128]{3,2,1,0:T(8,128)(2,1)S(1)} %copy-done.1), channel_id=1, source_target_pairs={{0,1},{1,0},{2,3},{3,2},{4,5},{5,4},{6,7},{7,6},{8,9},{9,8},{10,11... | collective-permute-start | bytes 884744 | tf_op jit(solution)/shard_map/ppermute | solution.py:214
  33.4 12.0 %collective-permute-start.6 = (f32[2,32,4,256]{3,1,2,0:T(8,128)S(1)}, f32[2,32,4,256]{3,1,2,0:T(8,128)S(1)}, u32[]{:S(2)}, u32[]{:S(2)}) collective-permute-start(f32[2,32,4,256]{3,1,2,0:T(8,128)S(1)} %add_add_fusion.1), channel_id=1, source_target_pairs={{0,32},{2,34},{4,36},{6,38},{8,40},{10,42},{12,44},{14,46},{16,48}... | collective-permute-start | bytes 786440 | tf_op jit(solution)/shard_map/ppermute | solution.py:78
  35.4 10.0 %collective-permute-start.7 = (f32[2,32,4,256]{3,1,2,0:T(8,128)S(1)}, f32[2,32,4,256]{3,1,2,0:T(8,128)S(1)}, u32[]{:S(2)}, u32[]{:S(2)}) collective-permute-start(f32[2,32,4,256]{3,1,2,0:T(8,128)S(1)} %add_add_fusion.1), channel_id=1, source_target_pairs={{0,224},{2,226},{4,228},{6,230},{8,232},{10,234},{12,236},{14,238}... | collective-permute-start | bytes 786440 | tf_op jit(solution)/shard_map/ppermute | solution.py:78
  35.5 19.4 %collective-permute-start.8 = (f32[2,32,4,256]{3,1,2,0:T(8,128)S(1)}, f32[2,32,4,256]{3,1,2,0:T(8,128)S(1)}, u32[]{:S(2)}, u32[]{:S(2)}) collective-permute-start(f32[2,32,4,256]{3,1,2,0:T(8,128)S(1)} %add_add_fusion.1), channel_id=1, source_target_pairs={{0,64},{2,66},{4,68},{6,70},{8,72},{10,74},{12,76},{14,78},{16,80}... | collective-permute-start | bytes 786440 | tf_op jit(solution)/shard_map/ppermute | solution.py:78
  55.0 7.6 %collective-permute-start.10 = (f32[2,4,256]{2,1,0:T(4,128)S(1)}, f32[2,4,256]{2,1,0:T(4,128)S(1)}, u32[]{:S(2)}, u32[]{:S(2)}) collective-permute-start(f32[2,4,256]{2,1,0:T(4,128)S(1)} %bitcast.56), channel_id=1, source_target_pairs={{0,128},{2,130},{4,132},{6,134},{8,136},{10,138},{12,140},{14,142}... | collective-permute-start | bytes 24584 | tf_op jit(solution)/shard_map/ppermute | solution.py:82

commit v6 on v5

--- a/solution.py
+++ b/solution.py
@@ -66,21 +66,28 @@
 
 
 def broadcast_mean(kept, tile, rings):
-    stages = [(shifts, stage) for n, shifts, _ in rings for stage in window_stages(n)]
-    last_shifts, last_stage = stages[-1]
-    if len(last_stage) != 1:
+    size_z, shifts_z, position_z = rings[-1]
+    if size_z != 8:
         block = broadcast_sum(kept, rings)
         return lax.dynamic_index_in_dim(block, tile, 1, keepdims=False)
-    last_pairs = last_shifts[last_stage[0]]
-    wanted = lax.ppermute(tile[None], "member", reversed_pairs(last_pairs))[0]
-    block = kept
-    for shifts, stage in stages[:-1]:
-        arrived = [lax.ppermute(block, "member", shifts[d]) for d in stage]
-        for part in arrived:
-            block = block + part
-    sent = lax.dynamic_index_in_dim(block, wanted, 1, keepdims=False)
-    arrived = lax.ppermute(sent, "member", last_pairs)
-    return lax.dynamic_index_in_dim(block, tile, 1, keepdims=False) + arrived
+    at_z = jnp.asarray(position_z, jnp.int32)[lax.axis_index("member")]
+    slots = jnp.arange(size_z, dtype=jnp.int32)
+    tiles_z = jnp.where(slots == at_z, tile, 0)
+    for d in (1, 2, 4):
+        tiles_z = tiles_z + lax.ppermute(tiles_z, "member", shifts_z[d])
+
+    block = broadcast_sum(kept, rings[:-1])
+
+    def served(first):
+        picked = jnp.stack([first % size_z, (first + size_z // 2) % size_z])
+        return jnp.take(block, jnp.take(tiles_z, picked), axis=1, mode="clip")
+
+    arrived = [lax.ppermute(served(at_z + d), "member", shifts_z[d]) for d in (1, -1, 2)]
+    block = served(at_z)
+    for part in arrived:
+        block = block + part
+    arrived = lax.ppermute(block[:, 1], "member", shifts_z[size_z // 2])
+    return block[:, 0] + arrived
 
 
 def rms_scale(values):

time: 90.4 us -> 104 us (1.15)
  the two profiles are of different devices: /device:TPU:32 before, /device:TPU:8 now
where the time goes in v6:
time: 104 us
  starting transfers between devices  29.3 us (28%)
  Pallas kernels  24.8 us (24%)
  waiting for transfers between devices  23.4 us (22%)
  local copies, waits for them, and re-layouts  12.4 us (12%)
  between operations  7.3 us (7%)
  other arithmetic  6.51 us (6%)
    pallas_call x1, Pallas kernels, run_chain(): pl.pallas_call(chain_kernel, out_shape=jax.ShapeDtypeStruct(state.shape,...  24.8 us
    ppermute x6, waiting for transfers between devices, broadcast_sum(): arrived = [lax.ppermute(block, 'member', shifts[d]) for d in stage]  11.1 us
    ppermute x3, starting transfers between devices, broadcast_mean(): tiles_z = tiles_z + lax.ppermute(tiles_z, 'member', shifts_z[d])  10.4 us
    ppermute x6, starting transfers between devices, broadcast_sum(): arrived = [lax.ppermute(block, 'member', shifts[d]) for d in stage]  9.53 us
    ppermute x3, waiting for transfers between devices, broadcast_mean(): tiles_z = tiles_z + lax.ppermute(tiles_z, 'member', shifts_z[d])  6.14 us
    ppermute x1, starting transfers between devices, broadcast_mean(): arrived = lax.ppermute(block[:, 1], 'member', shifts_z[size_z // 2])  5.11 us
    gather x8, local copies, waits for them, and re-layouts, served(): return jnp.take(block, jnp.take(tiles_z, picked), axis=1, mode='clip')  4.84 us
    ppermute x3, waiting for transfers between devices, broadcast_mean(): lax.ppermute(served(at_z + d), 'member', shifts_z[d])  4.52 us
  transfers between devices with their start and end apart: 15, of which 7 were waited for; matrix products, arithmetic and copies ran while one was open for 12% of the time, Pallas kernels for 0%

profile of v6, /device:TPU:8, one launch (start us, length us, event | category | flops | bytes accessed | tf_op | source)
XLA Modules:
  0.0 103.6 jit_solution(2409737281842517823)
XLA Ops:
  0.0 0.8 dynamic-slice_compare_fusion
  0.8 1.1 %bitcast_select_fusion = f32[2,32,4,256]{3,2,1,0:T(4,128)S(1)} fusion(f32[1,4,32,4,256]{4,3,2,1,0:T(4,128)} %param.14, s32[]{:T(128)S(6)} %select_n.86, pred[2]{0:T(512)(128)(4,1)S(1)} %dynamic-slice_compare_fusion), kind=kLoop, calls=%fused_computation.11 | loop fusion | flops 65536 | bytes 524294 | tf_op jit(solution)/shard_map/jit(_where)/select_n | solution.py:239
  1.9 1.6 %collective-permute-start = (f32[2,32,4,256]{3,2,1,0:T(4,128)S(1)}, f32[2,32,4,256]{3,2,1,0:T(4,128)S(1)}, u32[]{:S(2)}, u32[]{:S(2)}) collective-permute-start(f32[2,32,4,256]{3,2,1,0:T(4,128)S(1)} %bitcast_select_fusion), channel_id=1, source_target_pairs={{0,8},{2,10},{4,12},{6,14},{8,16},{10,18},{12,20},{14,22},{16,24},... | collective-permute-start | bytes 786440 | tf_op jit(solution)/shard_map/ppermute | solution.py:58
  3.4 1.7 %collective-permute-start.1 = (f32[2,32,4,256]{3,2,1,0:T(4,128)S(1)}, f32[2,32,4,256]{3,2,1,0:T(4,128)S(1)}, u32[]{:S(2)}, u32[]{:S(2)}) collective-permute-start(f32[2,32,4,256]{3,2,1,0:T(4,128)S(1)} %bitcast_select_fusion), channel_id=1, source_target_pairs={{0,24},{2,26},{4,28},{6,30},{8,0},{10,2},{12,4},{14,6},{16,8},{18,... | collective-permute-start | bytes 786440 | tf_op jit(solution)/shard_map/ppermute | solution.py:58
  5.2 1.8 %collective-permute-start.2 = (f32[2,32,4,256]{3,2,1,0:T(4,128)S(1)}, f32[2,32,4,256]{3,2,1,0:T(4,128)S(1)}, u32[]{:S(2)}, u32[]{:S(2)}) collective-permute-start(f32[2,32,4,256]{3,2,1,0:T(4,128)S(1)} %bitcast_select_fusion), channel_id=1, source_target_pairs={{0,16},{2,18},{4,20},{6,22},{8,24},{10,26},{12,28},{14,30},{16,0},... | collective-permute-start | bytes 786440 | tf_op jit(solution)/shard_map/ppermute | solution.py:58
  7.6 0.6 copy-done.7
  8.3 0.6 dynamic_slice.17
  8.9 0.6 compare_select_fusion.4
  9.5 2.0 %collective-permute-start.6 = (s32[8]{0:T(128)S(1)}, s32[8]{0:T(128)S(1)}, u32[]{:S(2)}, u32[]{:S(2)}) collective-permute-start(s32[8]{0:T(128)S(1)} %compare_select_fusion.4), channel_id=1, source_target_pairs={{0,32},{2,34},{4,36},{6,38},{8,40},{10,42},{12,44},{14,46},{16,48}... | collective-permute-start | bytes 104 | tf_op jit(solution)/shard_map/ppermute | solution.py:77
  18.2 0.6 copy-done.2
  19.0 0.6 reshape.25.coef_ref
  19.8 0.5 copy-done.5
  20.5 0.7 pad.16.state_ref
  21.2 0.6 pad.19.out_ref
  21.9 0.6 pad.18.lift_ref
  22.5 0.6 fusion.6
  23.2 3.3 %collective-permute-start.7 = (s32[8]{0:T(128)S(1)}, s32[8]{0:T(128)S(1)}, u32[]{:S(2)}, u32[]{:S(2)}) collective-permute-start(s32[8]{0:T(128)S(1)} %fusion.6), channel_id=1, source_target_pairs={{0,64},{2,66},{4,68},{6,70},{8,72},{10,74},{12,76},{14,78},{16,80}... | collective-permute-start | bytes 104 | tf_op jit(solution)/shard_map/ppermute | solution.py:77
  26.5 3.7 %collective-permute-done.7 = s32[8]{0:T(128)S(1)} collective-permute-done((s32[8]{0:T(128)S(1)}, s32[8]{0:T(128)S(1)}, u32[]{:S(2)}, u32[]{:S(2)}) %collective-permute-start.7) | collective-permute-done | bytes 64 | tf_op jit(solution)/shard_map/ppermute | solution.py:77
  30.2 0.6 fusion.7
  30.8 5.1 %collective-permute-start.8 = (s32[8]{0:T(128)S(1)}, s32[8]{0:T(128)S(1)}, u32[]{:S(2)}, u32[]{:S(2)}) collective-permute-start(s32[8]{0:T(128)S(1)} %fusion.7), channel_id=1, source_target_pairs={{0,128},{2,130},{4,132},{6,134},{8,136},{10,138},{12,140},{14,142}... | collective-permute-start | bytes 104 | tf_op jit(solution)/shard_map/ppermute | solution.py:77
  36.0 2.5 %collective-permute-done.8 = s32[8]{0:T(128)S(1)} collective-permute-done((s32[8]{0:T(128)S(1)}, s32[8]{0:T(128)S(1)}, u32[]{:S(2)}, u32[]{:S(2)}) %collective-permute-start.8) | collective-permute-done | bytes 64 | tf_op jit(solution)/shard_map/ppermute | solution.py:77
  38.4 0.6 gather_fusion.4
  39.1 0.6 gather_fusion.5
  39.7 0.6 gather_fusion.6
  40.4 0.6 gather_fusion.7
  41.1 0.2 add_add_fusion.1
  41.3 2.4 %collective-permute-start.5 = (f32[2,32,4,256]{3,2,1,0:T(4,128)S(1)}, f32[2,32,4,256]{3,2,1,0:T(4,128)S(1)}, u32[]{:S(2)}, u32[]{:S(2)}) collective-permute-start(f32[2,32,4,256]{3,2,1,0:T(4,128)S(1)} %add_add_fusion.1), channel_id=1, source_target_pairs={{0,4},{2,6},{4,0},{6,2},{8,12},{10,14},{12,8},{14,10},{16,20},{18,... | collective-permute-start | bytes 786440 | tf_op jit(solution)/shard_map/ppermute | solution.py:58
  43.7 1.3 %collective-permute-start.4 = (f32[2,32,4,256]{3,2,1,0:T(4,128)S(1)}, f32[2,32,4,256]{3,2,1,0:T(4,128)S(1)}, u32[]{:S(2)}, u32[]{:S(2)}) collective-permute-start(f32[2,32,4,256]{3,2,1,0:T(4,128)S(1)} %add_add_fusion.1), channel_id=1, source_target_pairs={{0,6},{2,0},{4,2},{6,4},{8,14},{10,8},{12,10},{14,12},{16,22},{18,... | collective-permute-start | bytes 786440 | tf_op jit(solution)/shard_map/ppermute | solution.py:58
  45.0 0.7 collective-permute-start.3
  45.7 0.6 maximum_convert_fusion.gain_ref
  46.3 5.8 %collective-permute-done.5 = f32[2,32,4,256]{3,2,1,0:T(4,128)S(1)} collective-permute-done((f32[2,32,4,256]{3,2,1,0:T(4,128)S(1)}, f32[2,32,4,256]{3,2,1,0:T(4,128)S(1)}, u32[]{:S(2)}, u32[]{:S(2)}) %collective-permute-start.5) | collective-permute-done | bytes 262176 | tf_op jit(solution)/shard_map/ppermute | solution.py:58
  52.1 5.1 %collective-permute-done.4 = f32[2,32,4,256]{3,2,1,0:T(4,128)S(1)} collective-permute-done((f32[2,32,4,256]{3,2,1,0:T(4,128)S(1)}, f32[2,32,4,256]{3,2,1,0:T(4,128)S(1)}, u32[]{:S(2)}, u32[]{:S(2)}) %collective-permute-start.4) | collective-permute-done | bytes 262176 | tf_op jit(solution)/shard_map/ppermute | solution.py:58
  57.2 0.2 collective-permute-done.3
  57.4 0.6 gather_fusion.1
  58.0 0.8 collective-permute-start.9
  58.8 0.6 gather_fusion.2
  59.4 2.6 %collective-permute-start.10 = (f32[2,2,4,256]{3,2,0,1:T(4,128)S(1)}, f32[2,2,4,256]{3,2,0,1:T(4,128)S(1)}, u32[]{:S(2)}, u32[]{:S(2)}) collective-permute-start(f32[2,2,4,256]{3,2,0,1:T(4,128)S(1)} %bitcast.86), channel_id=1, source_target_pairs={{0,224},{2,226},{4,228},{6,230},{8,232},{10,234},{12,236},{14,238}... | collective-permute-start | bytes 49160 | tf_op jit(solution)/shard_map/ppermute | solution.py:85
  62.0 0.6 gather_fusion.3
  62.5 0.8 collective-permute-start.11
  63.4 0.6 gather_fusion
  64.0 4.5 %collective-permute-done.11 = f32[2,2,4,256]{3,2,0,1:T(4,128)S(1)} collective-permute-done((f32[2,2,4,256]{3,2,0,1:T(4,128)S(1)}, f32[2,2,4,256]{3,2,0,1:T(4,128)S(1)}, u32[]{:S(2)}, u32[]{:S(2)}) %collective-permute-start.11) | collective-permute-done | bytes 16416 | tf_op jit(solution)/shard_map/ppermute | solution.py:85
  68.5 5.1 %collective-permute-start.12 = (f32[2,4,256]{2,1,0:T(4,128)S(1)}, f32[2,4,256]{2,1,0:T(4,128)S(1)}, u32[]{:S(2)}, u32[]{:S(2)}) collective-permute-start(f32[2,4,256]{2,1,0:T(4,128)S(1)} %slice_bitcast_fusion), channel_id=1, source_target_pairs={{0,128},{2,130},{4,132},{6,134},{8,136},{10,138},{12,140},{14,142}... | collective-permute-start | bytes 24584 | tf_op jit(solution)/shard_map/ppermute | solution.py:89
  73.6 0.9 pad_maximum_fusion.conv_ref
  74.5 1.6 %collective-permute-done.12 = f32[2,4,256]{2,1,0:T(4,128)S(1)} collective-permute-done((f32[2,4,256]{2,1,0:T(4,128)S(1)}, f32[2,4,256]{2,1,0:T(4,128)S(1)}, u32[]{:S(2)}, u32[]{:S(2)}) %collective-permute-start.12) | collective-permute-done | bytes 8224 | tf_op jit(solution)/shard_map/ppermute | solution.py:89
  76.3 0.9 pad.17.means_ref
  77.2 24.8 %shard_map.109 = f32[512,128]{1,0:T(8,128)} custom-call(f32[40]{0:T(128)} %reshape.25.coef_ref, f32[512,128]{1,0:T(8,128)} %pad.16.state_ref, f32[512,128]{1,0:T(8,128)} %pad.17.means_ref, f32[128,128]{1,0:T(8,128)} %pad.18.lift_ref, f32[1,128]{1,0:T(1,128)} %bitcast.89, bf16[2,1152,128]{2,1,0:T(8,128)(2,1)} %pad_maximum_fusion.conv_ref, ...), custom_call_target="tpu_custom_call" | custom-call | tf_op jit(solution)/shard_map/pallas_call | solution.py:168
  101.9 1.1 %copy.21 = f32[2,256,4]{1,2,0:T(4,128)S(1)} copy(f32[2,256,4]{2,1,0:T(8,128)} %bitcast.77) | data formatting | bytes 16384 | tf_op jit(solution)/shard_map/reshape | solution.py:256
  103.0 0.6 fusion.3
  (51 shorter events, 1.1 us)
Async XLA Ops:
  0.0 11.5 %copy-start.1 = (bf16[1,9,128,128]{3,2,1,0:T(8,128)(2,1)S(1)}, bf16[1,9,128,128]{3,2,1,0:T(8,128)(2,1)}, u32[]{:S(2)}) copy-start(bf16[1,9,128,128]{3,2,1,0:T(8,128)(2,1)} %param.20) | copy-start | bytes 884740
  1.9 39.2 %collective-permute-start = (f32[2,32,4,256]{3,2,1,0:T(4,128)S(1)}, f32[2,32,4,256]{3,2,1,0:T(4,128)S(1)}, u32[]{:S(2)}, u32[]{:S(2)}) collective-permute-start(f32[2,32,4,256]{3,2,1,0:T(4,128)S(1)} %bitcast_select_fusion), channel_id=1, source_target_pairs={{0,8},{2,10},{4,12},{6,14},{8,16},{10,18},{12,20},{14,22},{16,24},... | collective-permute-start | bytes 786440 | tf_op jit(solution)/shard_map/ppermute | solution.py:58
  3.4 37.6 %collective-permute-start.1 = (f32[2,32,4,256]{3,2,1,0:T(4,128)S(1)}, f32[2,32,4,256]{3,2,1,0:T(4,128)S(1)}, u32[]{:S(2)}, u32[]{:S(2)}) collective-permute-start(f32[2,32,4,256]{3,2,1,0:T(4,128)S(1)} %bitcast_select_fusion), channel_id=1, source_target_pairs={{0,24},{2,26},{4,28},{6,30},{8,0},{10,2},{12,4},{14,6},{16,8},{18,... | collective-permute-start | bytes 786440 | tf_op jit(solution)/shard_map/ppermute | solution.py:58
  5.2 35.9 %collective-permute-start.2 = (f32[2,32,4,256]{3,2,1,0:T(4,128)S(1)}, f32[2,32,4,256]{3,2,1,0:T(4,128)S(1)}, u32[]{:S(2)}, u32[]{:S(2)}) collective-permute-start(f32[2,32,4,256]{3,2,1,0:T(4,128)S(1)} %bitcast_select_fusion), channel_id=1, source_target_pairs={{0,16},{2,18},{4,20},{6,22},{8,24},{10,26},{12,28},{14,30},{16,0},... | collective-permute-start | bytes 786440 | tf_op jit(solution)/shard_map/ppermute | solution.py:58
  7.6 0.7 copy-start.7
  9.5 13.0 %collective-permute-start.6 = (s32[8]{0:T(128)S(1)}, s32[8]{0:T(128)S(1)}, u32[]{:S(2)}, u32[]{:S(2)}) collective-permute-start(s32[8]{0:T(128)S(1)} %compare_select_fusion.4), channel_id=1, source_target_pairs={{0,32},{2,34},{4,36},{6,38},{8,40},{10,42},{12,44},{14,46},{16,48}... | collective-permute-start | bytes 104 | tf_op jit(solution)/shard_map/ppermute | solution.py:77
  11.5 51.8 %collective-permute-start.13 = (bf16[1,9,128,128]{3,2,1,0:T(8,128)(2,1)S(1)}, bf16[1,9,128,128]{3,2,1,0:T(8,128)(2,1)S(1)}, u32[]{:S(2)}, u32[]{:S(2)}) collective-permute-start(bf16[1,9,128,128]{3,2,1,0:T(8,128)(2,1)S(1)} %copy-done.1), channel_id=1, source_target_pairs={{0,1},{1,0},{2,3},{3,2},{4,5},{5,4},{6,7},{7,6},{8,9},{9,8},{10,11... | collective-permute-start | bytes 884744 | tf_op jit(solution)/shard_map/ppermute | solution.py:221
  18.2 0.7 copy-start.2
  18.9 0.7 copy-start.4
  19.7 0.7 copy-start.5
  21.2 0.7 copy-start.3
  23.2 7.0 %collective-permute-start.7 = (s32[8]{0:T(128)S(1)}, s32[8]{0:T(128)S(1)}, u32[]{:S(2)}, u32[]{:S(2)}) collective-permute-start(s32[8]{0:T(128)S(1)} %fusion.6), channel_id=1, source_target_pairs={{0,64},{2,66},{4,68},{6,70},{8,72},{10,74},{12,76},{14,78},{16,80}... | collective-permute-start | bytes 104 | tf_op jit(solution)/shard_map/ppermute | solution.py:77
  30.2 8.2 %copy-start.6 = (bf16[1,128]{1,0:T(2,128)(2,1)S(1)}, bf16[1,128]{1,0:T(2,128)(2,1)}, u32[]{:S(2)}) copy-start(bf16[1,128]{1,0:T(2,128)(2,1)} %param.21) | copy-start | bytes 772
  30.8 7.6 %collective-permute-start.8 = (s32[8]{0:T(128)S(1)}, s32[8]{0:T(128)S(1)}, u32[]{:S(2)}, u32[]{:S(2)}) collective-permute-start(s32[8]{0:T(128)S(1)} %fusion.7), channel_id=1, source_target_pairs={{0,128},{2,130},{4,132},{6,134},{8,136},{10,138},{12,140},{14,142}... | collective-permute-start | bytes 104 | tf_op jit(solution)/shard_map/ppermute | solution.py:77
  38.4 7.3 %collective-permute-start.14 = (bf16[1,128]{1,0:T(2,128)(2,1)S(1)}, bf16[1,128]{1,0:T(2,128)(2,1)S(1)}, u32[]{:S(2)}, u32[]{:S(2)}) collective-permute-start(bf16[1,128]{1,0:T(2,128)(2,1)S(1)} %copy-done.6), channel_id=1, source_target_pairs={{0,1},{1,0},{2,3},{3,2},{4,5},{5,4},{6,7},{7,6},{8,9},{9,8},{10,11... | collective-permute-start | bytes 776 | tf_op jit(solution)/shard_map/ppermute | solution.py:222
  39.7 1.4 %copy-start = (f32[1,4,32,4,256]{4,3,2,1,0:T(4,128)S(1)}, f32[1,4,32,4,256]{4,3,2,1,0:T(4,128)}, u32[]{:S(2)}) copy-start(f32[1,4,32,4,256]{4,3,2,1,0:T(4,128)} %param.14) | copy-start | bytes 1572868
  41.3 10.8 %collective-permute-start.5 = (f32[2,32,4,256]{3,2,1,0:T(4,128)S(1)}, f32[2,32,4,256]{3,2,1,0:T(4,128)S(1)}, u32[]{:S(2)}, u32[]{:S(2)}) collective-permute-start(f32[2,32,4,256]{3,2,1,0:T(4,128)S(1)} %add_add_fusion.1), channel_id=1, source_target_pairs={{0,4},{2,6},{4,0},{6,2},{8,12},{10,14},{12,8},{14,10},{16,20},{18,... | collective-permute-start | bytes 786440 | tf_op jit(solution)/shard_map/ppermute | solution.py:58
  43.7 13.5 %collective-permute-start.4 = (f32[2,32,4,256]{3,2,1,0:T(4,128)S(1)}, f32[2,32,4,256]{3,2,1,0:T(4,128)S(1)}, u32[]{:S(2)}, u32[]{:S(2)}) collective-permute-start(f32[2,32,4,256]{3,2,1,0:T(4,128)S(1)} %add_add_fusion.1), channel_id=1, source_target_pairs={{0,6},{2,0},{4,2},{6,4},{8,14},{10,8},{12,10},{14,12},{16,22},{18,... | collective-permute-start | bytes 786440 | tf_op jit(solution)/shard_map/ppermute | solution.py:58
  45.0 12.3 %collective-permute-start.3 = (f32[2,32,4,256]{3,2,1,0:T(4,128)S(1)}, f32[2,32,4,256]{3,2,1,0:T(4,128)S(1)}, u32[]{:S(2)}, u32[]{:S(2)}) collective-permute-start(f32[2,32,4,256]{3,2,1,0:T(4,128)S(1)} %add_add_fusion.1), channel_id=1, source_target_pairs={{0,2},{2,4},{4,6},{6,0},{8,10},{10,12},{12,14},{14,8},{16,18},{18,... | collective-permute-start | bytes 786440 | tf_op jit(solution)/shard_map/ppermute | solution.py:58
  58.0 5.9 %collective-permute-start.9 = (f32[2,2,4,256]{3,2,0,1:T(4,128)S(1)}, f32[2,2,4,256]{3,2,0,1:T(4,128)S(1)}, u32[]{:S(2)}, u32[]{:S(2)}) collective-permute-start(f32[2,2,4,256]{3,2,0,1:T(4,128)S(1)} %bitcast.85), channel_id=1, source_target_pairs={{0,32},{2,34},{4,36},{6,38},{8,40},{10,42},{12,44},{14,46},{16,48}... | collective-permute-start | bytes 49160 | tf_op jit(solution)/shard_map/ppermute | solution.py:85
  59.4 4.5 %collective-permute-start.10 = (f32[2,2,4,256]{3,2,0,1:T(4,128)S(1)}, f32[2,2,4,256]{3,2,0,1:T(4,128)S(1)}, u32[]{:S(2)}, u32[]{:S(2)}) collective-permute-start(f32[2,2,4,256]{3,2,0,1:T(4,128)S(1)} %bitcast.86), channel_id=1, source_target_pairs={{0,224},{2,226},{4,228},{6,230},{8,232},{10,234},{12,236},{14,238}... | collective-permute-start | bytes 49160 | tf_op jit(solution)/shard_map/ppermute | solution.py:85
  62.5 5.9 %collective-permute-start.11 = (f32[2,2,4,256]{3,2,0,1:T(4,128)S(1)}, f32[2,2,4,256]{3,2,0,1:T(4,128)S(1)}, u32[]{:S(2)}, u32[]{:S(2)}) collective-permute-start(f32[2,2,4,256]{3,2,0,1:T(4,128)S(1)} %bitcast.87), channel_id=1, source_target_pairs={{0,64},{2,66},{4,68},{6,70},{8,72},{10,74},{12,76},{14,78},{16,80}... | collective-permute-start | bytes 49160 | tf_op jit(solution)/shard_map/ppermute | solution.py:85
  68.5 7.6 %collective-permute-start.12 = (f32[2,4,256]{2,1,0:T(4,128)S(1)}, f32[2,4,256]{2,1,0:T(4,128)S(1)}, u32[]{:S(2)}, u32[]{:S(2)}) collective-permute-start(f32[2,4,256]{2,1,0:T(4,128)S(1)} %slice_bitcast_fusion), channel_id=1, source_target_pairs={{0,128},{2,130},{4,132},{6,134},{8,136},{10,138},{12,140},{14,142}... | collective-permute-start | bytes 24584 | tf_op jit(solution)/shard_map/ppermute | solution.py:89

commit v7 on v6

--- a/solution.py
+++ b/solution.py
@@ -66,28 +66,26 @@
 
 
 def broadcast_mean(kept, tile, rings):
-    size_z, shifts_z, position_z = rings[-1]
-    if size_z != 8:
+    size_z, shifts_z, _ = rings[-1]
+    if size_z < 4 or size_z % 2:
         block = broadcast_sum(kept, rings)
         return lax.dynamic_index_in_dim(block, tile, 1, keepdims=False)
-    at_z = jnp.asarray(position_z, jnp.int32)[lax.axis_index("member")]
-    slots = jnp.arange(size_z, dtype=jnp.int32)
-    tiles_z = jnp.where(slots == at_z, tile, 0)
-    for d in (1, 2, 4):
-        tiles_z = tiles_z + lax.ppermute(tiles_z, "member", shifts_z[d])
-
+    far = range(2, size_z, 2)
+    wanted = {
+        d: lax.ppermute(tile[None], "member", reversed_pairs(shifts_z[d]))[0] for d in far
+    }
     block = broadcast_sum(kept, rings[:-1])
-
-    def served(first):
-        picked = jnp.stack([first % size_z, (first + size_z // 2) % size_z])
-        return jnp.take(block, jnp.take(tiles_z, picked), axis=1, mode="clip")
-
-    arrived = [lax.ppermute(served(at_z + d), "member", shifts_z[d]) for d in (1, -1, 2)]
-    block = served(at_z)
+    block = block + lax.ppermute(block, "member", shifts_z[1])
+    arrived = [
+        lax.ppermute(
+            lax.dynamic_index_in_dim(block, wanted[d], 1, keepdims=False), "member", shifts_z[d]
+        )
+        for d in far
+    ]
+    mean = lax.dynamic_index_in_dim(block, tile, 1, keepdims=False)
     for part in arrived:
-        block = block + part
-    arrived = lax.ppermute(block[:, 1], "member", shifts_z[size_z // 2])
-    return block[:, 0] + arrived
+        mean = mean + part
+    return mean
 
 
 def rms_scale(values):

time: 104 us -> 87.6 us (0.84)
  the two profiles are of different devices: /device:TPU:8 before, /device:TPU:32 now
where the time goes in v7:
time: 87.6 us; the launch traced here: 86.6 us
  starting transfers between devices  31.3 us (36%)
  Pallas kernels  24.8 us (28%)
  waiting for transfers between devices  13.6 us (16%)
  local copies, waits for them, and re-layouts  7.45 us (9%)
  between operations  6.68 us (8%)
  other arithmetic  2.7 us (3%)
    pallas_call x1, Pallas kernels, run_chain(): pl.pallas_call(chain_kernel, out_shape=jax.ShapeDtypeStruct(state.shape,...  24.8 us
    ppermute x6, starting transfers between devices, broadcast_sum(): arrived = [lax.ppermute(block, 'member', shifts[d]) for d in stage]  10.4 us
    ppermute x3, starting transfers between devices, broadcast_mean(): lax.ppermute(tile[None], 'member', reversed_pairs(shifts_z[d]))[0]  10.1 us
    ppermute x3, starting transfers between devices, broadcast_mean(): lax.ppermute(lax.dynamic_index_in_dim(block, wanted[d], 1, keepdims=False...  8.03 us
    ppermute x1, waiting for transfers between devices, broadcast_mean(): block = block + lax.ppermute(block, 'member', shifts_z[1])  5.49 us
    ppermute x6, waiting for transfers between devices, broadcast_sum(): arrived = [lax.ppermute(block, 'member', shifts[d]) for d in stage]  3.89 us
    ppermute x3, waiting for transfers between devices, broadcast_mean(): lax.ppermute(lax.dynamic_index_in_dim(block, wanted[d], 1, keepdims=False...  3.13 us
    ppermute x1, starting transfers between devices, broadcast_mean(): block = block + lax.ppermute(block, 'member', shifts_z[1])  2.68 us
  transfers between devices with their start and end apart: 15, of which 6 were waited for; matrix products, arithmetic and copies ran while one was open for 6% of the time, Pallas kernels for 0%

profile of v7, /device:TPU:32, one launch (start us, length us, event | category | flops | bytes accessed | tf_op | source)
XLA Modules:
  0.0 86.6 jit_solution(4740993869608914032)
XLA Ops:
  0.0 1.0 %copy-done = f32[1,4,32,4,256]{4,3,2,1,0:T(4,128)S(1)} copy-done((f32[1,4,32,4,256]{4,3,2,1,0:T(4,128)S(1)}, f32[1,4,32,4,256]{4,3,2,1,0:T(4,128)}, u32[]{:S(2)}) %copy-start) | copy-done | bytes 524312
  1.1 0.6 copy-done.7
  1.7 0.1 dynamic-slice_compare_fusion
  1.8 0.1 fusion
  1.9 1.6 %collective-permute-start = (f32[2,32,4,256]{3,1,2,0:T(8,128)S(1)}, f32[2,32,4,256]{3,1,2,0:T(8,128)S(1)}, u32[]{:S(2)}, u32[]{:S(2)}) collective-permute-start(f32[2,32,4,256]{3,1,2,0:T(8,128)S(1)} %fusion), channel_id=1, source_target_pairs={{0,8},{2,10},{4,12},{6,14},{8,16},{10,18},{12,20},{14,22},{16,24},... | collective-permute-start | bytes 786440 | tf_op jit(solution)/shard_map/ppermute | solution.py:58
  3.4 1.7 %collective-permute-start.1 = (f32[2,32,4,256]{3,1,2,0:T(8,128)S(1)}, f32[2,32,4,256]{3,1,2,0:T(8,128)S(1)}, u32[]{:S(2)}, u32[]{:S(2)}) collective-permute-start(f32[2,32,4,256]{3,1,2,0:T(8,128)S(1)} %fusion), channel_id=1, source_target_pairs={{0,24},{2,26},{4,28},{6,30},{8,0},{10,2},{12,4},{14,6},{16,8},{18,... | collective-permute-start | bytes 786440 | tf_op jit(solution)/shard_map/ppermute | solution.py:58
  5.2 1.8 %collective-permute-start.2 = (f32[2,32,4,256]{3,1,2,0:T(8,128)S(1)}, f32[2,32,4,256]{3,1,2,0:T(8,128)S(1)}, u32[]{:S(2)}, u32[]{:S(2)}) collective-permute-start(f32[2,32,4,256]{3,1,2,0:T(8,128)S(1)} %fusion), channel_id=1, source_target_pairs={{0,16},{2,18},{4,20},{6,22},{8,24},{10,26},{12,28},{14,30},{16,0},... | collective-permute-start | bytes 786440 | tf_op jit(solution)/shard_map/ppermute | solution.py:58
  7.0 5.4 %collective-permute-start.7 = (s32[1]{0:T(128)}, s32[1]{0:T(128)}, u32[]{:S(2)}, u32[]{:S(2)}) collective-permute-start(s32[1]{0:T(128)} %param.13), channel_id=1, source_target_pairs={{64,0},{66,2},{68,4},{70,6},{72,8},{74,10},{76,12},{78,14},{80,16}... | collective-permute-start | bytes 20 | tf_op jit(solution)/shard_map/ppermute | solution.py:75
  12.4 1.4 %collective-permute-start.9 = (s32[1]{0:T(128)}, s32[1]{0:T(128)}, u32[]{:S(2)}, u32[]{:S(2)}) collective-permute-start(s32[1]{0:T(128)} %param.13), channel_id=1, source_target_pairs={{128,0},{130,2},{132,4},{134,6},{136,8},{138,10},{140,12},{142,14}... | collective-permute-start | bytes 20 | tf_op jit(solution)/shard_map/ppermute | solution.py:75
  13.8 0.1 fusion.4
  13.9 0.0 collective-permute-done
  13.9 2.2 %collective-permute-done.1 = f32[2,32,4,256]{3,1,2,0:T(8,128)S(1)} collective-permute-done((f32[2,32,4,256]{3,1,2,0:T(8,128)S(1)}, f32[2,32,4,256]{3,1,2,0:T(8,128)S(1)}, u32[]{:S(2)}, u32[]{:S(2)}) %collective-permute-start.1) | collective-permute-done | bytes 262176 | tf_op jit(solution)/shard_map/ppermute | solution.py:58
  16.1 1.7 %collective-permute-done.2 = f32[2,32,4,256]{3,1,2,0:T(8,128)S(1)} collective-permute-done((f32[2,32,4,256]{3,1,2,0:T(8,128)S(1)}, f32[2,32,4,256]{3,1,2,0:T(8,128)S(1)}, u32[]{:S(2)}, u32[]{:S(2)}) %collective-permute-start.2) | collective-permute-done | bytes 262176 | tf_op jit(solution)/shard_map/ppermute | solution.py:58
  17.8 0.2 add_add_fusion.1
  18.0 1.7 %collective-permute-start.3 = (f32[2,32,4,256]{3,1,2,0:T(8,128)S(1)}, f32[2,32,4,256]{3,1,2,0:T(8,128)S(1)}, u32[]{:S(2)}, u32[]{:S(2)}) collective-permute-start(f32[2,32,4,256]{3,1,2,0:T(8,128)S(1)} %add_add_fusion.1), channel_id=1, source_target_pairs={{0,2},{2,4},{4,6},{6,0},{8,10},{10,12},{12,14},{14,8},{16,18},{18,... | collective-permute-start | bytes 786440 | tf_op jit(solution)/shard_map/ppermute | solution.py:58
  19.6 1.7 %collective-permute-start.4 = (f32[2,32,4,256]{3,1,2,0:T(8,128)S(1)}, f32[2,32,4,256]{3,1,2,0:T(8,128)S(1)}, u32[]{:S(2)}, u32[]{:S(2)}) collective-permute-start(f32[2,32,4,256]{3,1,2,0:T(8,128)S(1)} %add_add_fusion.1), channel_id=1, source_target_pairs={{0,6},{2,0},{4,2},{6,4},{8,14},{10,8},{12,10},{14,12},{16,22},{18,... | collective-permute-start | bytes 786440 | tf_op jit(solution)/shard_map/ppermute | solution.py:58
  21.3 2.0 %collective-permute-start.5 = (f32[2,32,4,256]{3,1,2,0:T(8,128)S(1)}, f32[2,32,4,256]{3,1,2,0:T(8,128)S(1)}, u32[]{:S(2)}, u32[]{:S(2)}) collective-permute-start(f32[2,32,4,256]{3,1,2,0:T(8,128)S(1)} %add_add_fusion.1), channel_id=1, source_target_pairs={{0,4},{2,6},{4,0},{6,2},{8,12},{10,14},{12,8},{14,10},{16,20},{18,... | collective-permute-start | bytes 786440 | tf_op jit(solution)/shard_map/ppermute | solution.py:58
  24.0 0.1 copy.17
  24.1 0.7 reshape.20.coef_ref
  24.7 0.1 copy.18
  24.9 0.5 copy-done.5
  25.4 0.1 copy.20
  25.5 0.7 pad.16.state_ref
  26.3 0.6 pad.19.out_ref
  26.9 0.1 copy-done.3
  27.0 0.6 pad.18.lift_ref
  27.6 0.0 collective-permute-done.7
  27.6 3.3 %collective-permute-start.11 = (s32[1]{0:T(128)}, s32[1]{0:T(128)}, u32[]{:S(2)}, u32[]{:S(2)}) collective-permute-start(s32[1]{0:T(128)} %param.13), channel_id=1, source_target_pairs={{192,0},{194,2},{196,4},{198,6},{200,8},{202,10},{204,12},{206,14}... | collective-permute-start | bytes 20 | tf_op jit(solution)/shard_map/ppermute | solution.py:75
  32.2 0.0 collective-permute-done.9
  32.2 0.1 collective-permute-start.13
  33.0 0.0 copy-start.6
  33.7 1.1 %collective-permute-done.11 = s32[1]{0:T(128)} collective-permute-done((s32[1]{0:T(128)}, s32[1]{0:T(128)}, u32[]{:S(2)}, u32[]{:S(2)}) %collective-permute-start.11) | collective-permute-done | bytes 36 | tf_op jit(solution)/shard_map/ppermute | solution.py:75
  38.0 0.0 collective-permute-done.14
  38.1 0.1 add_add_fusion
  38.1 2.7 %collective-permute-start.6 = (f32[2,32,4,256]{3,1,2,0:T(8,128)S(1)}, f32[2,32,4,256]{3,1,2,0:T(8,128)S(1)}, u32[]{:S(2)}, u32[]{:S(2)}) collective-permute-start(f32[2,32,4,256]{3,1,2,0:T(8,128)S(1)} %add_add_fusion), channel_id=1, source_target_pairs={{0,32},{2,34},{4,36},{6,38},{8,40},{10,42},{12,44},{14,46},{16,48}... | collective-permute-start | bytes 786440 | tf_op jit(solution)/shard_map/ppermute | solution.py:78
  40.8 0.6 maximum_convert_fusion.gain_ref
  41.5 5.5 %collective-permute-done.6 = f32[2,32,4,256]{3,1,2,0:T(8,128)S(1)} collective-permute-done((f32[2,32,4,256]{3,1,2,0:T(8,128)S(1)}, f32[2,32,4,256]{3,1,2,0:T(8,128)S(1)}, u32[]{:S(2)}, u32[]{:S(2)}) %collective-permute-start.6) | collective-permute-done | bytes 262176 | tf_op jit(solution)/shard_map/ppermute | solution.py:78
  47.0 5.1 %collective-permute-start.10 = (f32[2,4,256]{2,1,0:T(4,128)S(1)}, f32[2,4,256]{2,1,0:T(4,128)S(1)}, u32[]{:S(2)}, u32[]{:S(2)}) collective-permute-start(f32[2,4,256]{2,1,0:T(4,128)S(1)} %bitcast.64), channel_id=1, source_target_pairs={{0,128},{2,130},{4,132},{6,134},{8,136},{10,138},{12,140},{14,142}... | collective-permute-start | bytes 24584 | tf_op jit(solution)/shard_map/ppermute | solution.py:80
  52.2 1.2 %collective-permute-start.12 = (f32[2,4,256]{2,1,0:T(4,128)S(1)}, f32[2,4,256]{2,1,0:T(4,128)S(1)}, u32[]{:S(2)}, u32[]{:S(2)}) collective-permute-start(f32[2,4,256]{2,1,0:T(4,128)S(1)} %bitcast.65), channel_id=1, source_target_pairs={{0,192},{2,194},{4,196},{6,198},{8,200},{10,202},{12,204},{14,206}... | collective-permute-start | bytes 24584 | tf_op jit(solution)/shard_map/ppermute | solution.py:80
  53.4 1.7 %collective-permute-start.8 = (f32[2,4,256]{2,1,0:T(4,128)S(1)}, f32[2,4,256]{2,1,0:T(4,128)S(1)}, u32[]{:S(2)}, u32[]{:S(2)}) collective-permute-start(f32[2,4,256]{2,1,0:T(4,128)S(1)} %bitcast.66), channel_id=1, source_target_pairs={{0,64},{2,66},{4,68},{6,70},{8,72},{10,74},{12,76},{14,78},{16,80}... | collective-permute-start | bytes 24584 | tf_op jit(solution)/shard_map/ppermute | solution.py:80
  55.1 0.9 %pad_maximum_fusion.conv_ref = bf16[2,1152,128]{2,1,0:T(8,128)(2,1)} fusion(bf16[1,1152,128]{2,1,0:T(8,128)(2,1)S(1)} %bitcast.59, bf16[1,1152,128]{2,1,0:T(8,128)(2,1)S(1)} %bitcast.58), kind=kLoop, calls=%fused_computation | loop fusion | flops 294912 | bytes 1179648 | tf_op jit(solution)/shard_map/stack | solution.py:221
  56.0 0.7 collective-permute-done.12
  56.7 2.4 %collective-permute-done.8 = f32[2,4,256]{2,1,0:T(4,128)S(1)} collective-permute-done((f32[2,4,256]{2,1,0:T(4,128)S(1)}, f32[2,4,256]{2,1,0:T(4,128)S(1)}, u32[]{:S(2)}, u32[]{:S(2)}) %collective-permute-start.8) | collective-permute-done | bytes 8224 | tf_op jit(solution)/shard_map/ppermute | solution.py:80
  59.1 0.1 copy.19
  59.3 0.9 %pad.17.means_ref = f32[512,128]{1,0:T(8,128)} pad(f32[512,4]{1,0:T(8,128)S(1)} %bitcast.61, f32[]{:T(128)} %constant.31.clone.1), padding=0_0x4_120 | pad | bytes 270340 | tf_op jit(solution)/shard_map/jit(_pad)/pad | solution.py:194
  60.2 24.8 %shard_map.100 = f32[512,128]{1,0:T(8,128)} custom-call(f32[40]{0:T(128)} %reshape.20.coef_ref, f32[512,128]{1,0:T(8,128)} %pad.16.state_ref, f32[512,128]{1,0:T(8,128)} %pad.17.means_ref, f32[128,128]{1,0:T(8,128)} %pad.18.lift_ref, f32[1,128]{1,0:T(1,128)} %bitcast.68, bf16[2,1152,128]{2,1,0:T(8,128)(2,1)} %pad_maximum_fusion.conv_ref, ...), custom_call_target="tpu_custom_call" | custom-call | tf_op jit(solution)/shard_map/pallas_call | solution.py:166
  84.9 1.1 %copy.21 = f32[2,256,4]{1,2,0:T(4,128)S(1)} copy(f32[2,256,4]{2,1,0:T(8,128)} %bitcast.62) | data formatting | bytes 16384 | tf_op jit(solution)/shard_map/reshape | solution.py:254
  86.0 0.6 fusion.3
  (28 shorter events, 0.3 us)
Async XLA Ops:
  0.0 1.0 %copy-start = (f32[1,4,32,4,256]{4,3,2,1,0:T(4,128)S(1)}, f32[1,4,32,4,256]{4,3,2,1,0:T(4,128)}, u32[]{:S(2)}) copy-start(f32[1,4,32,4,256]{4,3,2,1,0:T(4,128)} %param.11) | copy-start | bytes 1572868
  1.0 0.7 copy-start.7
  1.8 12.1 %copy-start.2 = (f32[9]{0:T(128)S(1)}, f32[9]{0:T(128)}, u32[]{:S(2)}) copy-start(f32[9]{0:T(128)} %param.14) | copy-start | bytes 112
  1.9 12.1 %collective-permute-start = (f32[2,32,4,256]{3,1,2,0:T(8,128)S(1)}, f32[2,32,4,256]{3,1,2,0:T(8,128)S(1)}, u32[]{:S(2)}, u32[]{:S(2)}) collective-permute-start(f32[2,32,4,256]{3,1,2,0:T(8,128)S(1)} %fusion), channel_id=1, source_target_pairs={{0,8},{2,10},{4,12},{6,14},{8,16},{10,18},{12,20},{14,22},{16,24},... | collective-permute-start | bytes 786440 | tf_op jit(solution)/shard_map/ppermute | solution.py:58
  3.4 12.7 %collective-permute-start.1 = (f32[2,32,4,256]{3,1,2,0:T(8,128)S(1)}, f32[2,32,4,256]{3,1,2,0:T(8,128)S(1)}, u32[]{:S(2)}, u32[]{:S(2)}) collective-permute-start(f32[2,32,4,256]{3,1,2,0:T(8,128)S(1)} %fusion), channel_id=1, source_target_pairs={{0,24},{2,26},{4,28},{6,30},{8,0},{10,2},{12,4},{14,6},{16,8},{18,... | collective-permute-start | bytes 786440 | tf_op jit(solution)/shard_map/ppermute | solution.py:58
  5.2 12.6 %collective-permute-start.2 = (f32[2,32,4,256]{3,1,2,0:T(8,128)S(1)}, f32[2,32,4,256]{3,1,2,0:T(8,128)S(1)}, u32[]{:S(2)}, u32[]{:S(2)}) collective-permute-start(f32[2,32,4,256]{3,1,2,0:T(8,128)S(1)} %fusion), channel_id=1, source_target_pairs={{0,16},{2,18},{4,20},{6,22},{8,24},{10,26},{12,28},{14,30},{16,0},... | collective-permute-start | bytes 786440 | tf_op jit(solution)/shard_map/ppermute | solution.py:58
  7.0 20.6 %collective-permute-start.7 = (s32[1]{0:T(128)}, s32[1]{0:T(128)}, u32[]{:S(2)}, u32[]{:S(2)}) collective-permute-start(s32[1]{0:T(128)} %param.13), channel_id=1, source_target_pairs={{64,0},{66,2},{68,4},{70,6},{72,8},{74,10},{76,12},{78,14},{80,16}... | collective-permute-start | bytes 20 | tf_op jit(solution)/shard_map/ppermute | solution.py:75
  12.4 19.8 %collective-permute-start.9 = (s32[1]{0:T(128)}, s32[1]{0:T(128)}, u32[]{:S(2)}, u32[]{:S(2)}) collective-permute-start(s32[1]{0:T(128)} %param.13), channel_id=1, source_target_pairs={{128,0},{130,2},{132,4},{134,6},{136,8},{138,10},{140,12},{142,14}... | collective-permute-start | bytes 20 | tf_op jit(solution)/shard_map/ppermute | solution.py:75
  13.9 9.3 %copy-start.4 = (f32[1,4,4,256]{3,2,1,0:T(4,128)S(1)}, f32[1,4,4,256]{3,2,1,0:T(4,128)}, u32[]{:S(2)}) copy-start(f32[1,4,4,256]{3,2,1,0:T(4,128)} %param.10) | copy-start | bytes 49156
  18.0 20.1 %collective-permute-start.3 = (f32[2,32,4,256]{3,1,2,0:T(8,128)S(1)}, f32[2,32,4,256]{3,1,2,0:T(8,128)S(1)}, u32[]{:S(2)}, u32[]{:S(2)}) collective-permute-start(f32[2,32,4,256]{3,1,2,0:T(8,128)S(1)} %add_add_fusion.1), channel_id=1, source_target_pairs={{0,2},{2,4},{4,6},{6,0},{8,10},{10,12},{12,14},{14,8},{16,18},{18,... | collective-permute-start | bytes 786440 | tf_op jit(solution)/shard_map/ppermute | solution.py:58
  19.6 18.4 %collective-permute-start.4 = (f32[2,32,4,256]{3,1,2,0:T(8,128)S(1)}, f32[2,32,4,256]{3,1,2,0:T(8,128)S(1)}, u32[]{:S(2)}, u32[]{:S(2)}) collective-permute-start(f32[2,32,4,256]{3,1,2,0:T(8,128)S(1)} %add_add_fusion.1), channel_id=1, source_target_pairs={{0,6},{2,0},{4,2},{6,4},{8,14},{10,8},{12,10},{14,12},{16,22},{18,... | collective-permute-start | bytes 786440 | tf_op jit(solution)/shard_map/ppermute | solution.py:58
  21.3 16.8 %collective-permute-start.5 = (f32[2,32,4,256]{3,1,2,0:T(8,128)S(1)}, f32[2,32,4,256]{3,1,2,0:T(8,128)S(1)}, u32[]{:S(2)}, u32[]{:S(2)}) collective-permute-start(f32[2,32,4,256]{3,1,2,0:T(8,128)S(1)} %add_add_fusion.1), channel_id=1, source_target_pairs={{0,4},{2,6},{4,0},{6,2},{8,12},{10,14},{12,8},{14,10},{16,20},{18,... | collective-permute-start | bytes 786440 | tf_op jit(solution)/shard_map/ppermute | solution.py:58
  24.7 0.7 copy-start.5
  25.5 6.6 %copy-start.1 = (bf16[1,9,128,128]{3,2,1,0:T(8,128)(2,1)S(1)}, bf16[1,9,128,128]{3,2,1,0:T(8,128)(2,1)}, u32[]{:S(2)}) copy-start(bf16[1,9,128,128]{3,2,1,0:T(8,128)(2,1)} %param.17) | copy-start | bytes 884740
  26.3 0.7 copy-start.3
  27.6 7.2 %collective-permute-start.11 = (s32[1]{0:T(128)}, s32[1]{0:T(128)}, u32[]{:S(2)}, u32[]{:S(2)}) collective-permute-start(s32[1]{0:T(128)} %param.13), channel_id=1, source_target_pairs={{192,0},{194,2},{196,4},{198,6},{200,8},{202,10},{204,12},{206,14}... | collective-permute-start | bytes 20 | tf_op jit(solution)/shard_map/ppermute | solution.py:75
  32.2 9.2 %collective-permute-start.13 = (bf16[1,9,128,128]{3,2,1,0:T(8,128)(2,1)S(1)}, bf16[1,9,128,128]{3,2,1,0:T(8,128)(2,1)S(1)}, u32[]{:S(2)}, u32[]{:S(2)}) collective-permute-start(bf16[1,9,128,128]{3,2,1,0:T(8,128)(2,1)S(1)} %copy-done.1), channel_id=1, source_target_pairs={{0,1},{1,0},{2,3},{3,2},{4,5},{5,4},{6,7},{7,6},{8,9},{9,8},{10,11... | collective-permute-start | bytes 884744 | tf_op jit(solution)/shard_map/ppermute | solution.py:219
  33.0 1.8 %copy-start.6 = (bf16[1,128]{1,0:T(2,128)(2,1)S(1)}, bf16[1,128]{1,0:T(2,128)(2,1)}, u32[]{:S(2)}) copy-start(bf16[1,128]{1,0:T(2,128)(2,1)} %param.18) | copy-start | bytes 772
  34.8 3.2 %collective-permute-start.14 = (bf16[1,128]{1,0:T(2,128)(2,1)S(1)}, bf16[1,128]{1,0:T(2,128)(2,1)S(1)}, u32[]{:S(2)}, u32[]{:S(2)}) collective-permute-start(bf16[1,128]{1,0:T(2,128)(2,1)S(1)} %copy-done.6), channel_id=1, source_target_pairs={{0,1},{1,0},{2,3},{3,2},{4,5},{5,4},{6,7},{7,6},{8,9},{9,8},{10,11... | collective-permute-start | bytes 776 | tf_op jit(solution)/shard_map/ppermute | solution.py:220
  38.1 8.8 %collective-permute-start.6 = (f32[2,32,4,256]{3,1,2,0:T(8,128)S(1)}, f32[2,32,4,256]{3,1,2,0:T(8,128)S(1)}, u32[]{:S(2)}, u32[]{:S(2)}) collective-permute-start(f32[2,32,4,256]{3,1,2,0:T(8,128)S(1)} %add_add_fusion), channel_id=1, source_target_pairs={{0,32},{2,34},{4,36},{6,38},{8,40},{10,42},{12,44},{14,46},{16,48}... | collective-permute-start | bytes 786440 | tf_op jit(solution)/shard_map/ppermute | solution.py:78
  47.0 8.9 %collective-permute-start.10 = (f32[2,4,256]{2,1,0:T(4,128)S(1)}, f32[2,4,256]{2,1,0:T(4,128)S(1)}, u32[]{:S(2)}, u32[]{:S(2)}) collective-permute-start(f32[2,4,256]{2,1,0:T(4,128)S(1)} %bitcast.64), channel_id=1, source_target_pairs={{0,128},{2,130},{4,132},{6,134},{8,136},{10,138},{12,140},{14,142}... | collective-permute-start | bytes 24584 | tf_op jit(solution)/shard_map/ppermute | solution.py:80
  52.2 4.5 %collective-permute-start.12 = (f32[2,4,256]{2,1,0:T(4,128)S(1)}, f32[2,4,256]{2,1,0:T(4,128)S(1)}, u32[]{:S(2)}, u32[]{:S(2)}) collective-permute-start(f32[2,4,256]{2,1,0:T(4,128)S(1)} %bitcast.65), channel_id=1, source_target_pairs={{0,192},{2,194},{4,196},{6,198},{8,200},{10,202},{12,204},{14,206}... | collective-permute-start | bytes 24584 | tf_op jit(solution)/shard_map/ppermute | solution.py:80
  53.4 5.8 %collective-permute-start.8 = (f32[2,4,256]{2,1,0:T(4,128)S(1)}, f32[2,4,256]{2,1,0:T(4,128)S(1)}, u32[]{:S(2)}, u32[]{:S(2)}) collective-permute-start(f32[2,4,256]{2,1,0:T(4,128)S(1)} %bitcast.66), channel_id=1, source_target_pairs={{0,64},{2,66},{4,68},{6,70},{8,72},{10,74},{12,76},{14,78},{16,80}... | collective-permute-start | bytes 24584 | tf_op jit(solution)/shard_map/ppermute | solution.py:80

commit v8 on v7

--- a/solution.py
+++ b/solution.py
@@ -75,7 +75,13 @@
         d: lax.ppermute(tile[None], "member", reversed_pairs(shifts_z[d]))[0] for d in far
     }
     block = broadcast_sum(kept, rings[:-1])
-    block = block + lax.ppermute(block, "member", shifts_z[1])
+    half = block.shape[0] // 2
+    if half:
+        up = lax.ppermute(block[:half], "member", shifts_z[1])
+        down = lax.ppermute(block[half:], "member", shifts_z[-1])
+        block = block + jnp.concatenate([up, down], axis=0)
+    else:
+        block = block + lax.ppermute(block, "member", shifts_z[1])
     arrived = [
         lax.ppermute(
             lax.dynamic_index_in_dim(block, wanted[d], 1, keepdims=False), "member", shifts_z[d]

time: 87.6 us -> 93.2 us (1.064)
  waiting for transfers between devices: 13.6 us -> 21.1 us
  starting transfers between devices: 31.3 us -> 29.8 us
    ppermute x6, waiting for transfers between devices: 3.89 us -> 11 us  [broadcast_sum(): arrived = [lax.ppermute(block, 'member', shifts[d]) for d in stage]]
    ppermute x3, waiting for transfers between devices: 3.13 us -> 4.86 us  [broadcast_mean(): lax.ppermute(lax.dynamic_index_in_dim(block, wanted[d], 1, keepdims=False...]
    ppermute x1 -> x2, waiting for transfers between devices: 5.49 us -> 4.43 us  [the longest x1 2.97 us: broadcast_mean(): up = lax.ppermute(block[:half], 'member', shifts_z[1])]
    ppermute x1 -> x2, starting transfers between devices: 2.68 us -> 2.1 us  [the longest x1 1.62 us: broadcast_mean(): up = lax.ppermute(block[:half], 'member', shifts_z[1])]
  transfers between devices with their start and end apart: 15 -> 16, of which waited for: 6 -> 8; matrix products, arithmetic and copies ran while one was open for 6% -> 5% of each run, Pallas kernels for 0% -> 0%
where the time goes in v8:
time: 93.2 us; the launch traced here: 92.9 us
  starting transfers between devices  29.8 us (32%)
  Pallas kernels  24.8 us (27%)
  waiting for transfers between devices  21.1 us (23%)
  local copies, waits for them, and re-layouts  8.08 us (9%)
  between operations  6.52 us (7%)
  other arithmetic  2.69 us (3%)
    pallas_call x1, Pallas kernels, run_chain(): pl.pallas_call(chain_kernel, out_shape=jax.ShapeDtypeStruct(state.shape,...  24.8 us
    ppermute x6, waiting for transfers between devices, broadcast_sum(): arrived = [lax.ppermute(block, 'member', shifts[d]) for d in stage]  11 us
    ppermute x6, starting transfers between devices, broadcast_sum(): arrived = [lax.ppermute(block, 'member', shifts[d]) for d in stage]  10.4 us
    ppermute x3, starting transfers between devices, broadcast_mean(): lax.ppermute(tile[None], 'member', reversed_pairs(shifts_z[d]))[0]  9.22 us
    ppermute x3, starting transfers between devices, broadcast_mean(): lax.ppermute(lax.dynamic_index_in_dim(block, wanted[d], 1, keepdims=False...  7.93 us
    ppermute x3, waiting for transfers between devices, broadcast_mean(): lax.ppermute(lax.dynamic_index_in_dim(block, wanted[d], 1, keepdims=False...  4.86 us
    unnamed x20, local copies, waits for them, and re-layouts  3.03 us
    ppermute x1, waiting for transfers between devices, broadcast_mean(): up = lax.ppermute(block[:half], 'member', shifts_z[1])  2.97 us
  transfers between devices with their start and end apart: 16, of which 8 were waited for; matrix products, arithmetic and copies ran while one was open for 5% of the time, Pallas kernels for 0%

profile of v8, /device:TPU:32, one launch (start us, length us, event | category | flops | bytes accessed | tf_op | source)
XLA Modules:
  0.0 92.9 jit_solution(13705986879797631365)
XLA Ops:
  0.0 1.0 %copy-done = f32[1,4,32,4,256]{4,3,2,1,0:T(4,128)S(1)} copy-done((f32[1,4,32,4,256]{4,3,2,1,0:T(4,128)S(1)}, f32[1,4,32,4,256]{4,3,2,1,0:T(4,128)}, u32[]{:S(2)}) %copy-start) | copy-done | bytes 524312
  1.1 0.6 copy-done.7
  1.7 0.1 dynamic-slice_compare_fusion
  1.8 0.1 fusion
  1.9 1.6 %collective-permute-start = (f32[2,32,4,256]{3,1,2,0:T(8,128)S(1)}, f32[2,32,4,256]{3,1,2,0:T(8,128)S(1)}, u32[]{:S(2)}, u32[]{:S(2)}) collective-permute-start(f32[2,32,4,256]{3,1,2,0:T(8,128)S(1)} %fusion), channel_id=1, source_target_pairs={{0,8},{2,10},{4,12},{6,14},{8,16},{10,18},{12,20},{14,22},{16,24},... | collective-permute-start | bytes 786440 | tf_op jit(solution)/shard_map/ppermute | solution.py:58
  3.4 1.7 %collective-permute-start.1 = (f32[2,32,4,256]{3,1,2,0:T(8,128)S(1)}, f32[2,32,4,256]{3,1,2,0:T(8,128)S(1)}, u32[]{:S(2)}, u32[]{:S(2)}) collective-permute-start(f32[2,32,4,256]{3,1,2,0:T(8,128)S(1)} %fusion), channel_id=1, source_target_pairs={{0,24},{2,26},{4,28},{6,30},{8,0},{10,2},{12,4},{14,6},{16,8},{18,... | collective-permute-start | bytes 786440 | tf_op jit(solution)/shard_map/ppermute | solution.py:58
  5.2 1.8 %collective-permute-start.2 = (f32[2,32,4,256]{3,1,2,0:T(8,128)S(1)}, f32[2,32,4,256]{3,1,2,0:T(8,128)S(1)}, u32[]{:S(2)}, u32[]{:S(2)}) collective-permute-start(f32[2,32,4,256]{3,1,2,0:T(8,128)S(1)} %fusion), channel_id=1, source_target_pairs={{0,16},{2,18},{4,20},{6,22},{8,24},{10,26},{12,28},{14,30},{16,0},... | collective-permute-start | bytes 786440 | tf_op jit(solution)/shard_map/ppermute | solution.py:58
  7.0 5.4 %collective-permute-start.8 = (s32[1]{0:T(128)}, s32[1]{0:T(128)}, u32[]{:S(2)}, u32[]{:S(2)}) collective-permute-start(s32[1]{0:T(128)} %param.13), channel_id=1, source_target_pairs={{64,0},{66,2},{68,4},{70,6},{72,8},{74,10},{76,12},{78,14},{80,16}... | collective-permute-start | bytes 20 | tf_op jit(solution)/shard_map/ppermute | solution.py:75
  12.4 1.4 %collective-permute-start.10 = (s32[1]{0:T(128)}, s32[1]{0:T(128)}, u32[]{:S(2)}, u32[]{:S(2)}) collective-permute-start(s32[1]{0:T(128)} %param.13), channel_id=1, source_target_pairs={{128,0},{130,2},{132,4},{134,6},{136,8},{138,10},{140,12},{142,14}... | collective-permute-start | bytes 20 | tf_op jit(solution)/shard_map/ppermute | solution.py:75
  14.5 0.0 copy-start.2
  14.6 0.6 copy-done.2
  15.2 0.1 fusion.4
  15.3 0.1 copy.17
  15.4 0.7 reshape.20.coef_ref
  16.1 0.0 copy-start.5
  16.1 0.1 copy.18
  16.3 0.5 copy-done.5
  16.8 0.1 copy.20
  16.9 0.7 pad.16.state_ref
  17.6 0.6 pad.19.out_ref
  18.3 0.0 copy-done.3
  18.3 0.6 pad.18.lift_ref
  18.9 2.4 %collective-permute-start.12 = (s32[1]{0:T(128)}, s32[1]{0:T(128)}, u32[]{:S(2)}, u32[]{:S(2)}) collective-permute-start(s32[1]{0:T(128)} %param.13), channel_id=1, source_target_pairs={{192,0},{194,2},{196,4},{198,6},{200,8},{202,10},{204,12},{206,14}... | collective-permute-start | bytes 20 | tf_op jit(solution)/shard_map/ppermute | solution.py:75
  22.7 0.1 collective-permute-start.14
  24.1 0.8 collective-permute-done.12
  27.9 0.1 add_add_fusion.1
  28.1 1.7 %collective-permute-start.3 = (f32[2,32,4,256]{3,1,2,0:T(8,128)S(1)}, f32[2,32,4,256]{3,1,2,0:T(8,128)S(1)}, u32[]{:S(2)}, u32[]{:S(2)}) collective-permute-start(f32[2,32,4,256]{3,1,2,0:T(8,128)S(1)} %add_add_fusion.1), channel_id=1, source_target_pairs={{0,2},{2,4},{4,6},{6,0},{8,10},{10,12},{12,14},{14,8},{16,18},{18,... | collective-permute-start | bytes 786440 | tf_op jit(solution)/shard_map/ppermute | solution.py:58
  29.7 1.7 %collective-permute-start.4 = (f32[2,32,4,256]{3,1,2,0:T(8,128)S(1)}, f32[2,32,4,256]{3,1,2,0:T(8,128)S(1)}, u32[]{:S(2)}, u32[]{:S(2)}) collective-permute-start(f32[2,32,4,256]{3,1,2,0:T(8,128)S(1)} %add_add_fusion.1), channel_id=1, source_target_pairs={{0,6},{2,0},{4,2},{6,4},{8,14},{10,8},{12,10},{14,12},{16,22},{18,... | collective-permute-start | bytes 786440 | tf_op jit(solution)/shard_map/ppermute | solution.py:58
  31.4 2.0 %collective-permute-start.5 = (f32[2,32,4,256]{3,1,2,0:T(8,128)S(1)}, f32[2,32,4,256]{3,1,2,0:T(8,128)S(1)}, u32[]{:S(2)}, u32[]{:S(2)}) collective-permute-start(f32[2,32,4,256]{3,1,2,0:T(8,128)S(1)} %add_add_fusion.1), channel_id=1, source_target_pairs={{0,4},{2,6},{4,0},{6,2},{8,12},{10,14},{12,8},{14,10},{16,20},{18,... | collective-permute-start | bytes 786440 | tf_op jit(solution)/shard_map/ppermute | solution.py:58
  33.4 0.6 maximum_convert_fusion.gain_ref
  33.9 4.2 %collective-permute-done.3 = f32[2,32,4,256]{3,1,2,0:T(8,128)S(1)} collective-permute-done((f32[2,32,4,256]{3,1,2,0:T(8,128)S(1)}, f32[2,32,4,256]{3,1,2,0:T(8,128)S(1)}, u32[]{:S(2)}, u32[]{:S(2)}) %collective-permute-start.3) | collective-permute-done | bytes 262176 | tf_op jit(solution)/shard_map/ppermute | solution.py:58
  38.1 5.0 %collective-permute-done.4 = f32[2,32,4,256]{3,1,2,0:T(8,128)S(1)} collective-permute-done((f32[2,32,4,256]{3,1,2,0:T(8,128)S(1)}, f32[2,32,4,256]{3,1,2,0:T(8,128)S(1)}, u32[]{:S(2)}, u32[]{:S(2)}) %collective-permute-start.4) | collective-permute-done | bytes 262176 | tf_op jit(solution)/shard_map/ppermute | solution.py:58
  43.1 1.8 %collective-permute-done.5 = f32[2,32,4,256]{3,1,2,0:T(8,128)S(1)} collective-permute-done((f32[2,32,4,256]{3,1,2,0:T(8,128)S(1)}, f32[2,32,4,256]{3,1,2,0:T(8,128)S(1)}, u32[]{:S(2)}, u32[]{:S(2)}) %collective-permute-start.5) | collective-permute-done | bytes 262176 | tf_op jit(solution)/shard_map/ppermute | solution.py:58
  44.9 0.1 add_add_fusion
  45.0 1.6 %collective-permute-start.6 = (f32[1,32,4,256]{3,1,2,0:T(8,128)S(1)}, f32[1,32,4,256]{3,1,2,0:T(8,128)S(1)}, u32[]{:S(2)}, u32[]{:S(2)}) collective-permute-start(f32[1,32,4,256]{3,1,2,0:T(8,128)S(1)} %get-tuple-element.11), channel_id=1, source_target_pairs={{0,32},{2,34},{4,36},{6,38},{8,40},{10,42},{12,44},{14,46},{16,48}... | collective-permute-start | bytes 393224 | tf_op jit(solution)/shard_map/ppermute | solution.py:80
  46.7 0.5 collective-permute-start.7
  47.2 3.0 %collective-permute-done.6 = f32[1,32,4,256]{3,1,2,0:T(8,128)S(1)} collective-permute-done((f32[1,32,4,256]{3,1,2,0:T(8,128)S(1)}, f32[1,32,4,256]{3,1,2,0:T(8,128)S(1)}, u32[]{:S(2)}, u32[]{:S(2)}) %collective-permute-start.6) | collective-permute-done | bytes 131104 | tf_op jit(solution)/shard_map/ppermute | solution.py:80
  50.2 1.5 %collective-permute-done.7 = f32[1,32,4,256]{3,1,2,0:T(8,128)S(1)} collective-permute-done((f32[1,32,4,256]{3,1,2,0:T(8,128)S(1)}, f32[1,32,4,256]{3,1,2,0:T(8,128)S(1)}, u32[]{:S(2)}, u32[]{:S(2)}) %collective-permute-start.7) | collective-permute-done | bytes 131104 | tf_op jit(solution)/shard_map/ppermute | solution.py:81
  51.7 3.2 %collective-permute-start.11 = (f32[2,4,256]{2,1,0:T(4,128)S(1)}, f32[2,4,256]{2,1,0:T(4,128)S(1)}, u32[]{:S(2)}, u32[]{:S(2)}) collective-permute-start(f32[2,4,256]{2,1,0:T(4,128)S(1)} %bitcast.64), channel_id=1, source_target_pairs={{0,128},{2,130},{4,132},{6,134},{8,136},{10,138},{12,140},{14,142}... | collective-permute-start | bytes 24584 | tf_op jit(solution)/shard_map/ppermute | solution.py:86
  54.9 4.7 %collective-permute-start.13 = (f32[2,4,256]{2,1,0:T(4,128)S(1)}, f32[2,4,256]{2,1,0:T(4,128)S(1)}, u32[]{:S(2)}, u32[]{:S(2)}) collective-permute-start(f32[2,4,256]{2,1,0:T(4,128)S(1)} %bitcast.65), channel_id=1, source_target_pairs={{0,192},{2,194},{4,196},{6,198},{8,200},{10,202},{12,204},{14,206}... | collective-permute-start | bytes 24584 | tf_op jit(solution)/shard_map/ppermute | solution.py:86
  59.7 0.9 pad_maximum_fusion.conv_ref
  60.6 0.5 collective-permute-done.13
  61.0 4.4 %collective-permute-done.9 = f32[2,4,256]{2,1,0:T(4,128)S(1)} collective-permute-done((f32[2,4,256]{2,1,0:T(4,128)S(1)}, f32[2,4,256]{2,1,0:T(4,128)S(1)}, u32[]{:S(2)}, u32[]{:S(2)}) %collective-permute-start.9) | collective-permute-done | bytes 8224 | tf_op jit(solution)/shard_map/ppermute | solution.py:86
  65.4 0.1 copy.19
  65.6 0.9 pad.17.means_ref
  66.5 24.8 %shard_map.100 = f32[512,128]{1,0:T(8,128)} custom-call(f32[40]{0:T(128)} %reshape.20.coef_ref, f32[512,128]{1,0:T(8,128)} %pad.16.state_ref, f32[512,128]{1,0:T(8,128)} %pad.17.means_ref, f32[128,128]{1,0:T(8,128)} %pad.18.lift_ref, f32[1,128]{1,0:T(1,128)} %bitcast.68, bf16[2,1152,128]{2,1,0:T(8,128)(2,1)} %pad_maximum_fusion.conv_ref, ...), custom_call_target="tpu_custom_call" | custom-call | tf_op jit(solution)/shard_map/pallas_call | solution.py:172
  91.2 1.1 %copy.21 = f32[2,256,4]{1,2,0:T(4,128)S(1)} copy(f32[2,256,4]{2,1,0:T(8,128)} %bitcast.62) | data formatting | bytes 16384 | tf_op jit(solution)/shard_map/reshape | solution.py:260
  92.3 0.6 fusion.3
  (31 shorter events, 0.3 us)
Async XLA Ops:
  0.0 1.0 %copy-start = (f32[1,4,32,4,256]{4,3,2,1,0:T(4,128)S(1)}, f32[1,4,32,4,256]{4,3,2,1,0:T(4,128)}, u32[]{:S(2)}) copy-start(f32[1,4,32,4,256]{4,3,2,1,0:T(4,128)} %param.11) | copy-start | bytes 1572868
  1.0 0.7 copy-start.7
  1.9 26.0 %collective-permute-start = (f32[2,32,4,256]{3,1,2,0:T(8,128)S(1)}, f32[2,32,4,256]{3,1,2,0:T(8,128)S(1)}, u32[]{:S(2)}, u32[]{:S(2)}) collective-permute-start(f32[2,32,4,256]{3,1,2,0:T(8,128)S(1)} %fusion), channel_id=1, source_target_pairs={{0,8},{2,10},{4,12},{6,14},{8,16},{10,18},{12,20},{14,22},{16,24},... | collective-permute-start | bytes 786440 | tf_op jit(solution)/shard_map/ppermute | solution.py:58
  3.4 24.5 %collective-permute-start.1 = (f32[2,32,4,256]{3,1,2,0:T(8,128)S(1)}, f32[2,32,4,256]{3,1,2,0:T(8,128)S(1)}, u32[]{:S(2)}, u32[]{:S(2)}) collective-permute-start(f32[2,32,4,256]{3,1,2,0:T(8,128)S(1)} %fusion), channel_id=1, source_target_pairs={{0,24},{2,26},{4,28},{6,30},{8,0},{10,2},{12,4},{14,6},{16,8},{18,... | collective-permute-start | bytes 786440 | tf_op jit(solution)/shard_map/ppermute | solution.py:58
  5.2 22.7 %collective-permute-start.2 = (f32[2,32,4,256]{3,1,2,0:T(8,128)S(1)}, f32[2,32,4,256]{3,1,2,0:T(8,128)S(1)}, u32[]{:S(2)}, u32[]{:S(2)}) collective-permute-start(f32[2,32,4,256]{3,1,2,0:T(8,128)S(1)} %fusion), channel_id=1, source_target_pairs={{0,16},{2,18},{4,20},{6,22},{8,24},{10,26},{12,28},{14,30},{16,0},... | collective-permute-start | bytes 786440 | tf_op jit(solution)/shard_map/ppermute | solution.py:58
  7.0 11.9 %collective-permute-start.8 = (s32[1]{0:T(128)}, s32[1]{0:T(128)}, u32[]{:S(2)}, u32[]{:S(2)}) collective-permute-start(s32[1]{0:T(128)} %param.13), channel_id=1, source_target_pairs={{64,0},{66,2},{68,4},{70,6},{72,8},{74,10},{76,12},{78,14},{80,16}... | collective-permute-start | bytes 20 | tf_op jit(solution)/shard_map/ppermute | solution.py:75
  12.4 10.3 %collective-permute-start.10 = (s32[1]{0:T(128)}, s32[1]{0:T(128)}, u32[]{:S(2)}, u32[]{:S(2)}) collective-permute-start(s32[1]{0:T(128)} %param.13), channel_id=1, source_target_pairs={{128,0},{130,2},{132,4},{134,6},{136,8},{138,10},{140,12},{142,14}... | collective-permute-start | bytes 20 | tf_op jit(solution)/shard_map/ppermute | solution.py:75
  14.5 0.7 copy-start.2
  15.3 0.8 copy-start.4
  16.1 0.7 copy-start.5
  16.9 5.8 %copy-start.1 = (bf16[1,9,128,128]{3,2,1,0:T(8,128)(2,1)S(1)}, bf16[1,9,128,128]{3,2,1,0:T(8,128)(2,1)}, u32[]{:S(2)}) copy-start(bf16[1,9,128,128]{3,2,1,0:T(8,128)(2,1)} %param.17) | copy-start | bytes 884740
  17.6 0.7 copy-start.3
  18.9 5.9 %collective-permute-start.12 = (s32[1]{0:T(128)}, s32[1]{0:T(128)}, u32[]{:S(2)}, u32[]{:S(2)}) collective-permute-start(s32[1]{0:T(128)} %param.13), channel_id=1, source_target_pairs={{192,0},{194,2},{196,4},{198,6},{200,8},{202,10},{204,12},{206,14}... | collective-permute-start | bytes 20 | tf_op jit(solution)/shard_map/ppermute | solution.py:75
  22.7 24.5 %collective-permute-start.14 = (bf16[1,9,128,128]{3,2,1,0:T(8,128)(2,1)S(1)}, bf16[1,9,128,128]{3,2,1,0:T(8,128)(2,1)S(1)}, u32[]{:S(2)}, u32[]{:S(2)}) collective-permute-start(bf16[1,9,128,128]{3,2,1,0:T(8,128)(2,1)S(1)} %copy-done.1), channel_id=1, source_target_pairs={{0,1},{1,0},{2,3},{3,2},{4,5},{5,4},{6,7},{7,6},{8,9},{9,8},{10,11... | collective-permute-start | bytes 884744 | tf_op jit(solution)/shard_map/ppermute | solution.py:225
  23.4 1.4 %copy-start.6 = (bf16[1,128]{1,0:T(2,128)(2,1)S(1)}, bf16[1,128]{1,0:T(2,128)(2,1)}, u32[]{:S(2)}) copy-start(bf16[1,128]{1,0:T(2,128)(2,1)} %param.18) | copy-start | bytes 772
  24.9 8.5 %collective-permute-start.15 = (bf16[1,128]{1,0:T(2,128)(2,1)S(1)}, bf16[1,128]{1,0:T(2,128)(2,1)S(1)}, u32[]{:S(2)}, u32[]{:S(2)}) collective-permute-start(bf16[1,128]{1,0:T(2,128)(2,1)S(1)} %copy-done.6), channel_id=1, source_target_pairs={{0,1},{1,0},{2,3},{3,2},{4,5},{5,4},{6,7},{7,6},{8,9},{9,8},{10,11... | collective-permute-start | bytes 776 | tf_op jit(solution)/shard_map/ppermute | solution.py:226
  28.1 10.1 %collective-permute-start.3 = (f32[2,32,4,256]{3,1,2,0:T(8,128)S(1)}, f32[2,32,4,256]{3,1,2,0:T(8,128)S(1)}, u32[]{:S(2)}, u32[]{:S(2)}) collective-permute-start(f32[2,32,4,256]{3,1,2,0:T(8,128)S(1)} %add_add_fusion.1), channel_id=1, source_target_pairs={{0,2},{2,4},{4,6},{6,0},{8,10},{10,12},{12,14},{14,8},{16,18},{18,... | collective-permute-start | bytes 786440 | tf_op jit(solution)/shard_map/ppermute | solution.py:58
  29.7 13.4 %collective-permute-start.4 = (f32[2,32,4,256]{3,1,2,0:T(8,128)S(1)}, f32[2,32,4,256]{3,1,2,0:T(8,128)S(1)}, u32[]{:S(2)}, u32[]{:S(2)}) collective-permute-start(f32[2,32,4,256]{3,1,2,0:T(8,128)S(1)} %add_add_fusion.1), channel_id=1, source_target_pairs={{0,6},{2,0},{4,2},{6,4},{8,14},{10,8},{12,10},{14,12},{16,22},{18,... | collective-permute-start | bytes 786440 | tf_op jit(solution)/shard_map/ppermute | solution.py:58
  31.4 13.5 %collective-permute-start.5 = (f32[2,32,4,256]{3,1,2,0:T(8,128)S(1)}, f32[2,32,4,256]{3,1,2,0:T(8,128)S(1)}, u32[]{:S(2)}, u32[]{:S(2)}) collective-permute-start(f32[2,32,4,256]{3,1,2,0:T(8,128)S(1)} %add_add_fusion.1), channel_id=1, source_target_pairs={{0,4},{2,6},{4,0},{6,2},{8,12},{10,14},{12,8},{14,10},{16,20},{18,... | collective-permute-start | bytes 786440 | tf_op jit(solution)/shard_map/ppermute | solution.py:58
  45.0 5.1 %collective-permute-start.6 = (f32[1,32,4,256]{3,1,2,0:T(8,128)S(1)}, f32[1,32,4,256]{3,1,2,0:T(8,128)S(1)}, u32[]{:S(2)}, u32[]{:S(2)}) collective-permute-start(f32[1,32,4,256]{3,1,2,0:T(8,128)S(1)} %get-tuple-element.11), channel_id=1, source_target_pairs={{0,32},{2,34},{4,36},{6,38},{8,40},{10,42},{12,44},{14,46},{16,48}... | collective-permute-start | bytes 393224 | tf_op jit(solution)/shard_map/ppermute | solution.py:80
  46.7 5.0 %collective-permute-start.7 = (f32[1,32,4,256]{3,1,2,0:T(8,128)S(1)}, f32[1,32,4,256]{3,1,2,0:T(8,128)S(1)}, u32[]{:S(2)}, u32[]{:S(2)}) collective-permute-start(f32[1,32,4,256]{3,1,2,0:T(8,128)S(1)} %get-tuple-element.12), channel_id=1, source_target_pairs={{0,224},{2,226},{4,228},{6,230},{8,232},{10,234},{12,236},{14,238}... | collective-permute-start | bytes 393224 | tf_op jit(solution)/shard_map/ppermute | solution.py:81
  51.7 8.8 %collective-permute-start.11 = (f32[2,4,256]{2,1,0:T(4,128)S(1)}, f32[2,4,256]{2,1,0:T(4,128)S(1)}, u32[]{:S(2)}, u32[]{:S(2)}) collective-permute-start(f32[2,4,256]{2,1,0:T(4,128)S(1)} %bitcast.64), channel_id=1, source_target_pairs={{0,128},{2,130},{4,132},{6,134},{8,136},{10,138},{12,140},{14,142}... | collective-permute-start | bytes 24584 | tf_op jit(solution)/shard_map/ppermute | solution.py:86
  54.9 6.1 %collective-permute-start.13 = (f32[2,4,256]{2,1,0:T(4,128)S(1)}, f32[2,4,256]{2,1,0:T(4,128)S(1)}, u32[]{:S(2)}, u32[]{:S(2)}) collective-permute-start(f32[2,4,256]{2,1,0:T(4,128)S(1)} %bitcast.65), channel_id=1, source_target_pairs={{0,192},{2,194},{4,196},{6,198},{8,200},{10,202},{12,204},{14,206}... | collective-permute-start | bytes 24584 | tf_op jit(solution)/shard_map/ppermute | solution.py:86
  59.7 5.8 %collective-permute-start.9 = (f32[2,4,256]{2,1,0:T(4,128)S(1)}, f32[2,4,256]{2,1,0:T(4,128)S(1)}, u32[]{:S(2)}, u32[]{:S(2)}) collective-permute-start(f32[2,4,256]{2,1,0:T(4,128)S(1)} %bitcast.66), channel_id=1, source_target_pairs={{0,64},{2,66},{4,68},{6,70},{8,72},{10,74},{12,76},{14,78},{16,80}... | collective-permute-start | bytes 24584 | tf_op jit(solution)/shard_map/ppermute | solution.py:86

commit v9 on v7

--- a/solution.py
+++ b/solution.py
@@ -158,7 +158,7 @@
         denoised = keep_state * state + keep_net * net_out
         return state + move * (state - denoised)
 
-    result_ref[...] = lax.fori_loop(0, STEPS, one_step, state_ref[...])
+    result_ref[...] = lax.fori_loop(0, STEPS, one_step, state_ref[...], unroll=True)
 
 
 def run_chain(coefs, state, means, lift, embed, kernels, gains, out_weight):

time: 87.6 us -> 86.5 us (0.987)
  Pallas kernels: 24.8 us -> 23.5 us
    pallas_call x1, Pallas kernels: 24.8 us -> 23.5 us  [run_chain(): pl.pallas_call(chain_kernel, out_shape=jax.ShapeDtypeStruct(state.shape,...]
where the time goes in v9:
time: 86.5 us; the launch traced here: 85.4 us
  starting transfers between devices  31.4 us (36%)
  Pallas kernels  23.5 us (27%)
  waiting for transfers between devices  13.6 us (16%)
  local copies, waits for them, and re-layouts  7.45 us (9%)
  between operations  6.68 us (8%)
  other arithmetic  2.7 us (3%)
    pallas_call x1, Pallas kernels, run_chain(): pl.pallas_call(chain_kernel, out_shape=jax.ShapeDtypeStruct(state.shape,...  23.5 us
    ppermute x6, starting transfers between devices, broadcast_sum(): arrived = [lax.ppermute(block, 'member', shifts[d]) for d in stage]  10.4 us
    ppermute x3, starting transfers between devices, broadcast_mean(): lax.ppermute(tile[None], 'member', reversed_pairs(shifts_z[d]))[0]  10.1 us
    ppermute x3, starting transfers between devices, broadcast_mean(): lax.ppermute(lax.dynamic_index_in_dim(block, wanted[d], 1, keepdims=False...  8.03 us
    ppermute x1, waiting for transfers between devices, broadcast_mean(): block = block + lax.ppermute(block, 'member', shifts_z[1])  5.49 us
    ppermute x6, waiting for transfers between devices, broadcast_sum(): arrived = [lax.ppermute(block, 'member', shifts[d]) for d in stage]  3.89 us
    ppermute x3, waiting for transfers between devices, broadcast_mean(): lax.ppermute(lax.dynamic_index_in_dim(block, wanted[d], 1, keepdims=False...  3.13 us
    ppermute x1, starting transfers between devices, broadcast_mean(): block = block + lax.ppermute(block, 'member', shifts_z[1])  2.68 us
  transfers between devices with their start and end apart: 15, of which 6 were waited for; matrix products, arithmetic and copies ran while one was open for 6% of the time, Pallas kernels for 0%

profile of v9, /device:TPU:32, one launch (start us, length us, event | category | flops | bytes accessed | tf_op | source)
XLA Modules:
  0.0 85.4 jit_solution(9646733204792346520)
XLA Ops:
  0.0 1.0 %copy-done = f32[1,4,32,4,256]{4,3,2,1,0:T(4,128)S(1)} copy-done((f32[1,4,32,4,256]{4,3,2,1,0:T(4,128)S(1)}, f32[1,4,32,4,256]{4,3,2,1,0:T(4,128)}, u32[]{:S(2)}) %copy-start) | copy-done | bytes 524312
  1.1 0.6 copy-done.7
  1.7 0.1 dynamic-slice_compare_fusion
  1.8 0.1 fusion
  1.9 1.6 %collective-permute-start = (f32[2,32,4,256]{3,1,2,0:T(8,128)S(1)}, f32[2,32,4,256]{3,1,2,0:T(8,128)S(1)}, u32[]{:S(2)}, u32[]{:S(2)}) collective-permute-start(f32[2,32,4,256]{3,1,2,0:T(8,128)S(1)} %fusion), channel_id=1, source_target_pairs={{0,8},{2,10},{4,12},{6,14},{8,16},{10,18},{12,20},{14,22},{16,24},... | collective-permute-start | bytes 786440 | tf_op jit(solution)/shard_map/ppermute | solution.py:58
  3.4 1.7 %collective-permute-start.1 = (f32[2,32,4,256]{3,1,2,0:T(8,128)S(1)}, f32[2,32,4,256]{3,1,2,0:T(8,128)S(1)}, u32[]{:S(2)}, u32[]{:S(2)}) collective-permute-start(f32[2,32,4,256]{3,1,2,0:T(8,128)S(1)} %fusion), channel_id=1, source_target_pairs={{0,24},{2,26},{4,28},{6,30},{8,0},{10,2},{12,4},{14,6},{16,8},{18,... | collective-permute-start | bytes 786440 | tf_op jit(solution)/shard_map/ppermute | solution.py:58
  5.2 1.8 %collective-permute-start.2 = (f32[2,32,4,256]{3,1,2,0:T(8,128)S(1)}, f32[2,32,4,256]{3,1,2,0:T(8,128)S(1)}, u32[]{:S(2)}, u32[]{:S(2)}) collective-permute-start(f32[2,32,4,256]{3,1,2,0:T(8,128)S(1)} %fusion), channel_id=1, source_target_pairs={{0,16},{2,18},{4,20},{6,22},{8,24},{10,26},{12,28},{14,30},{16,0},... | collective-permute-start | bytes 786440 | tf_op jit(solution)/shard_map/ppermute | solution.py:58
  7.0 5.4 %collective-permute-start.7 = (s32[1]{0:T(128)}, s32[1]{0:T(128)}, u32[]{:S(2)}, u32[]{:S(2)}) collective-permute-start(s32[1]{0:T(128)} %param.13), channel_id=1, source_target_pairs={{64,0},{66,2},{68,4},{70,6},{72,8},{74,10},{76,12},{78,14},{80,16}... | collective-permute-start | bytes 20 | tf_op jit(solution)/shard_map/ppermute | solution.py:75
  12.4 1.4 %collective-permute-start.9 = (s32[1]{0:T(128)}, s32[1]{0:T(128)}, u32[]{:S(2)}, u32[]{:S(2)}) collective-permute-start(s32[1]{0:T(128)} %param.13), channel_id=1, source_target_pairs={{128,0},{130,2},{132,4},{134,6},{136,8},{138,10},{140,12},{142,14}... | collective-permute-start | bytes 20 | tf_op jit(solution)/shard_map/ppermute | solution.py:75
  13.8 0.1 fusion.4
  13.9 0.0 collective-permute-done
  13.9 2.2 %collective-permute-done.1 = f32[2,32,4,256]{3,1,2,0:T(8,128)S(1)} collective-permute-done((f32[2,32,4,256]{3,1,2,0:T(8,128)S(1)}, f32[2,32,4,256]{3,1,2,0:T(8,128)S(1)}, u32[]{:S(2)}, u32[]{:S(2)}) %collective-permute-start.1) | collective-permute-done | bytes 262176 | tf_op jit(solution)/shard_map/ppermute | solution.py:58
  16.1 1.7 %collective-permute-done.2 = f32[2,32,4,256]{3,1,2,0:T(8,128)S(1)} collective-permute-done((f32[2,32,4,256]{3,1,2,0:T(8,128)S(1)}, f32[2,32,4,256]{3,1,2,0:T(8,128)S(1)}, u32[]{:S(2)}, u32[]{:S(2)}) %collective-permute-start.2) | collective-permute-done | bytes 262176 | tf_op jit(solution)/shard_map/ppermute | solution.py:58
  17.8 0.2 add_add_fusion.1
  18.0 1.7 %collective-permute-start.3 = (f32[2,32,4,256]{3,1,2,0:T(8,128)S(1)}, f32[2,32,4,256]{3,1,2,0:T(8,128)S(1)}, u32[]{:S(2)}, u32[]{:S(2)}) collective-permute-start(f32[2,32,4,256]{3,1,2,0:T(8,128)S(1)} %add_add_fusion.1), channel_id=1, source_target_pairs={{0,2},{2,4},{4,6},{6,0},{8,10},{10,12},{12,14},{14,8},{16,18},{18,... | collective-permute-start | bytes 786440 | tf_op jit(solution)/shard_map/ppermute | solution.py:58
  19.6 1.7 %collective-permute-start.4 = (f32[2,32,4,256]{3,1,2,0:T(8,128)S(1)}, f32[2,32,4,256]{3,1,2,0:T(8,128)S(1)}, u32[]{:S(2)}, u32[]{:S(2)}) collective-permute-start(f32[2,32,4,256]{3,1,2,0:T(8,128)S(1)} %add_add_fusion.1), channel_id=1, source_target_pairs={{0,6},{2,0},{4,2},{6,4},{8,14},{10,8},{12,10},{14,12},{16,22},{18,... | collective-permute-start | bytes 786440 | tf_op jit(solution)/shard_map/ppermute | solution.py:58
  21.3 2.0 %collective-permute-start.5 = (f32[2,32,4,256]{3,1,2,0:T(8,128)S(1)}, f32[2,32,4,256]{3,1,2,0:T(8,128)S(1)}, u32[]{:S(2)}, u32[]{:S(2)}) collective-permute-start(f32[2,32,4,256]{3,1,2,0:T(8,128)S(1)} %add_add_fusion.1), channel_id=1, source_target_pairs={{0,4},{2,6},{4,0},{6,2},{8,12},{10,14},{12,8},{14,10},{16,20},{18,... | collective-permute-start | bytes 786440 | tf_op jit(solution)/shard_map/ppermute | solution.py:58
  24.0 0.1 copy.17
  24.1 0.7 reshape.20.coef_ref
  24.7 0.1 copy.18
  24.9 0.5 copy-done.5
  25.4 0.1 copy.20
  25.5 0.7 pad.16.state_ref
  26.3 0.6 pad.19.out_ref
  26.9 0.1 copy-done.3
  27.0 0.6 pad.18.lift_ref
  27.6 0.0 collective-permute-done.7
  27.6 3.3 %collective-permute-start.11 = (s32[1]{0:T(128)}, s32[1]{0:T(128)}, u32[]{:S(2)}, u32[]{:S(2)}) collective-permute-start(s32[1]{0:T(128)} %param.13), channel_id=1, source_target_pairs={{192,0},{194,2},{196,4},{198,6},{200,8},{202,10},{204,12},{206,14}... | collective-permute-start | bytes 20 | tf_op jit(solution)/shard_map/ppermute | solution.py:75
  32.2 0.1 collective-permute-start.13
  33.0 0.0 copy-start.6
  33.7 1.1 %collective-permute-done.11 = s32[1]{0:T(128)} collective-permute-done((s32[1]{0:T(128)}, s32[1]{0:T(128)}, u32[]{:S(2)}, u32[]{:S(2)}) %collective-permute-start.11) | collective-permute-done | bytes 36 | tf_op jit(solution)/shard_map/ppermute | solution.py:75
  34.8 0.0 collective-permute-start.14
  38.0 0.0 collective-permute-done.3
  38.1 0.1 add_add_fusion
  38.1 2.7 %collective-permute-start.6 = (f32[2,32,4,256]{3,1,2,0:T(8,128)S(1)}, f32[2,32,4,256]{3,1,2,0:T(8,128)S(1)}, u32[]{:S(2)}, u32[]{:S(2)}) collective-permute-start(f32[2,32,4,256]{3,1,2,0:T(8,128)S(1)} %add_add_fusion), channel_id=1, source_target_pairs={{0,32},{2,34},{4,36},{6,38},{8,40},{10,42},{12,44},{14,46},{16,48}... | collective-permute-start | bytes 786440 | tf_op jit(solution)/shard_map/ppermute | solution.py:78
  40.8 0.6 maximum_convert_fusion.gain_ref
  41.5 5.5 %collective-permute-done.6 = f32[2,32,4,256]{3,1,2,0:T(8,128)S(1)} collective-permute-done((f32[2,32,4,256]{3,1,2,0:T(8,128)S(1)}, f32[2,32,4,256]{3,1,2,0:T(8,128)S(1)}, u32[]{:S(2)}, u32[]{:S(2)}) %collective-permute-start.6) | collective-permute-done | bytes 262176 | tf_op jit(solution)/shard_map/ppermute | solution.py:78
  47.0 5.1 %collective-permute-start.10 = (f32[2,4,256]{2,1,0:T(4,128)S(1)}, f32[2,4,256]{2,1,0:T(4,128)S(1)}, u32[]{:S(2)}, u32[]{:S(2)}) collective-permute-start(f32[2,4,256]{2,1,0:T(4,128)S(1)} %bitcast.64), channel_id=1, source_target_pairs={{0,128},{2,130},{4,132},{6,134},{8,136},{10,138},{12,140},{14,142}... | collective-permute-start | bytes 24584 | tf_op jit(solution)/shard_map/ppermute | solution.py:80
  52.2 1.2 %collective-permute-start.12 = (f32[2,4,256]{2,1,0:T(4,128)S(1)}, f32[2,4,256]{2,1,0:T(4,128)S(1)}, u32[]{:S(2)}, u32[]{:S(2)}) collective-permute-start(f32[2,4,256]{2,1,0:T(4,128)S(1)} %bitcast.65), channel_id=1, source_target_pairs={{0,192},{2,194},{4,196},{6,198},{8,200},{10,202},{12,204},{14,206}... | collective-permute-start | bytes 24584 | tf_op jit(solution)/shard_map/ppermute | solution.py:80
  53.4 1.7 %collective-permute-start.8 = (f32[2,4,256]{2,1,0:T(4,128)S(1)}, f32[2,4,256]{2,1,0:T(4,128)S(1)}, u32[]{:S(2)}, u32[]{:S(2)}) collective-permute-start(f32[2,4,256]{2,1,0:T(4,128)S(1)} %bitcast.66), channel_id=1, source_target_pairs={{0,64},{2,66},{4,68},{6,70},{8,72},{10,74},{12,76},{14,78},{16,80}... | collective-permute-start | bytes 24584 | tf_op jit(solution)/shard_map/ppermute | solution.py:80
  55.1 0.9 %pad_maximum_fusion.conv_ref = bf16[2,1152,128]{2,1,0:T(8,128)(2,1)} fusion(bf16[1,1152,128]{2,1,0:T(8,128)(2,1)S(1)} %bitcast.59, bf16[1,1152,128]{2,1,0:T(8,128)(2,1)S(1)} %bitcast.58), kind=kLoop, calls=%fused_computation | loop fusion | flops 294912 | bytes 1179648 | tf_op jit(solution)/shard_map/stack | solution.py:221
  56.0 0.7 collective-permute-done.12
  56.7 2.4 %collective-permute-done.8 = f32[2,4,256]{2,1,0:T(4,128)S(1)} collective-permute-done((f32[2,4,256]{2,1,0:T(4,128)S(1)}, f32[2,4,256]{2,1,0:T(4,128)S(1)}, u32[]{:S(2)}, u32[]{:S(2)}) %collective-permute-start.8) | collective-permute-done | bytes 8224 | tf_op jit(solution)/shard_map/ppermute | solution.py:80
  59.1 0.1 copy.19
  59.3 0.9 %pad.17.means_ref = f32[512,128]{1,0:T(8,128)} pad(f32[512,4]{1,0:T(8,128)S(1)} %bitcast.61, f32[]{:T(128)} %constant.31.clone.1), padding=0_0x4_120 | pad | bytes 270340 | tf_op jit(solution)/shard_map/jit(_pad)/pad | solution.py:194
  60.2 23.5 %shard_map.100 = f32[512,128]{1,0:T(8,128)} custom-call(f32[40]{0:T(128)} %reshape.20.coef_ref, f32[512,128]{1,0:T(8,128)} %pad.16.state_ref, f32[512,128]{1,0:T(8,128)} %pad.17.means_ref, f32[128,128]{1,0:T(8,128)} %pad.18.lift_ref, f32[1,128]{1,0:T(1,128)} %bitcast.68, bf16[2,1152,128]{2,1,0:T(8,128)(2,1)} %pad_maximum_fusion.conv_ref, ...), custom_call_target="tpu_custom_call" | custom-call | tf_op jit(solution)/shard_map/pallas_call | solution.py:166
  83.7 1.1 %copy.21 = f32[2,256,4]{1,2,0:T(4,128)S(1)} copy(f32[2,256,4]{2,1,0:T(8,128)} %bitcast.62) | data formatting | bytes 16384 | tf_op jit(solution)/shard_map/reshape | solution.py:254
  84.7 0.6 fusion.3
  (28 shorter events, 0.3 us)
Async XLA Ops:
  0.0 1.0 %copy-start = (f32[1,4,32,4,256]{4,3,2,1,0:T(4,128)S(1)}, f32[1,4,32,4,256]{4,3,2,1,0:T(4,128)}, u32[]{:S(2)}) copy-start(f32[1,4,32,4,256]{4,3,2,1,0:T(4,128)} %param.11) | copy-start | bytes 1572868
  1.0 0.7 copy-start.7
  1.8 12.1 %copy-start.2 = (f32[9]{0:T(128)S(1)}, f32[9]{0:T(128)}, u32[]{:S(2)}) copy-start(f32[9]{0:T(128)} %param.14) | copy-start | bytes 112
  1.9 12.1 %collective-permute-start = (f32[2,32,4,256]{3,1,2,0:T(8,128)S(1)}, f32[2,32,4,256]{3,1,2,0:T(8,128)S(1)}, u32[]{:S(2)}, u32[]{:S(2)}) collective-permute-start(f32[2,32,4,256]{3,1,2,0:T(8,128)S(1)} %fusion), channel_id=1, source_target_pairs={{0,8},{2,10},{4,12},{6,14},{8,16},{10,18},{12,20},{14,22},{16,24},... | collective-permute-start | bytes 786440 | tf_op jit(solution)/shard_map/ppermute | solution.py:58
  3.4 12.7 %collective-permute-start.1 = (f32[2,32,4,256]{3,1,2,0:T(8,128)S(1)}, f32[2,32,4,256]{3,1,2,0:T(8,128)S(1)}, u32[]{:S(2)}, u32[]{:S(2)}) collective-permute-start(f32[2,32,4,256]{3,1,2,0:T(8,128)S(1)} %fusion), channel_id=1, source_target_pairs={{0,24},{2,26},{4,28},{6,30},{8,0},{10,2},{12,4},{14,6},{16,8},{18,... | collective-permute-start | bytes 786440 | tf_op jit(solution)/shard_map/ppermute | solution.py:58
  5.2 12.6 %collective-permute-start.2 = (f32[2,32,4,256]{3,1,2,0:T(8,128)S(1)}, f32[2,32,4,256]{3,1,2,0:T(8,128)S(1)}, u32[]{:S(2)}, u32[]{:S(2)}) collective-permute-start(f32[2,32,4,256]{3,1,2,0:T(8,128)S(1)} %fusion), channel_id=1, source_target_pairs={{0,16},{2,18},{4,20},{6,22},{8,24},{10,26},{12,28},{14,30},{16,0},... | collective-permute-start | bytes 786440 | tf_op jit(solution)/shard_map/ppermute | solution.py:58
  7.0 20.6 %collective-permute-start.7 = (s32[1]{0:T(128)}, s32[1]{0:T(128)}, u32[]{:S(2)}, u32[]{:S(2)}) collective-permute-start(s32[1]{0:T(128)} %param.13), channel_id=1, source_target_pairs={{64,0},{66,2},{68,4},{70,6},{72,8},{74,10},{76,12},{78,14},{80,16}... | collective-permute-start | bytes 20 | tf_op jit(solution)/shard_map/ppermute | solution.py:75
  12.4 19.8 %collective-permute-start.9 = (s32[1]{0:T(128)}, s32[1]{0:T(128)}, u32[]{:S(2)}, u32[]{:S(2)}) collective-permute-start(s32[1]{0:T(128)} %param.13), channel_id=1, source_target_pairs={{128,0},{130,2},{132,4},{134,6},{136,8},{138,10},{140,12},{142,14}... | collective-permute-start | bytes 20 | tf_op jit(solution)/shard_map/ppermute | solution.py:75
  13.9 9.3 %copy-start.4 = (f32[1,4,4,256]{3,2,1,0:T(4,128)S(1)}, f32[1,4,4,256]{3,2,1,0:T(4,128)}, u32[]{:S(2)}) copy-start(f32[1,4,4,256]{3,2,1,0:T(4,128)} %param.10) | copy-start | bytes 49156
  18.0 20.1 %collective-permute-start.3 = (f32[2,32,4,256]{3,1,2,0:T(8,128)S(1)}, f32[2,32,4,256]{3,1,2,0:T(8,128)S(1)}, u32[]{:S(2)}, u32[]{:S(2)}) collective-permute-start(f32[2,32,4,256]{3,1,2,0:T(8,128)S(1)} %add_add_fusion.1), channel_id=1, source_target_pairs={{0,2},{2,4},{4,6},{6,0},{8,10},{10,12},{12,14},{14,8},{16,18},{18,... | collective-permute-start | bytes 786440 | tf_op jit(solution)/shard_map/ppermute | solution.py:58
  19.6 18.4 %collective-permute-start.4 = (f32[2,32,4,256]{3,1,2,0:T(8,128)S(1)}, f32[2,32,4,256]{3,1,2,0:T(8,128)S(1)}, u32[]{:S(2)}, u32[]{:S(2)}) collective-permute-start(f32[2,32,4,256]{3,1,2,0:T(8,128)S(1)} %add_add_fusion.1), channel_id=1, source_target_pairs={{0,6},{2,0},{4,2},{6,4},{8,14},{10,8},{12,10},{14,12},{16,22},{18,... | collective-permute-start | bytes 786440 | tf_op jit(solution)/shard_map/ppermute | solution.py:58
  21.3 16.8 %collective-permute-start.5 = (f32[2,32,4,256]{3,1,2,0:T(8,128)S(1)}, f32[2,32,4,256]{3,1,2,0:T(8,128)S(1)}, u32[]{:S(2)}, u32[]{:S(2)}) collective-permute-start(f32[2,32,4,256]{3,1,2,0:T(8,128)S(1)} %add_add_fusion.1), channel_id=1, source_target_pairs={{0,4},{2,6},{4,0},{6,2},{8,12},{10,14},{12,8},{14,10},{16,20},{18,... | collective-permute-start | bytes 786440 | tf_op jit(solution)/shard_map/ppermute | solution.py:58
  24.7 0.7 copy-start.5
  25.5 6.6 %copy-start.1 = (bf16[1,9,128,128]{3,2,1,0:T(8,128)(2,1)S(1)}, bf16[1,9,128,128]{3,2,1,0:T(8,128)(2,1)}, u32[]{:S(2)}) copy-start(bf16[1,9,128,128]{3,2,1,0:T(8,128)(2,1)} %param.17) | copy-start | bytes 884740
  26.3 0.7 copy-start.3
  27.6 7.2 %collective-permute-start.11 = (s32[1]{0:T(128)}, s32[1]{0:T(128)}, u32[]{:S(2)}, u32[]{:S(2)}) collective-permute-start(s32[1]{0:T(128)} %param.13), channel_id=1, source_target_pairs={{192,0},{194,2},{196,4},{198,6},{200,8},{202,10},{204,12},{206,14}... | collective-permute-start | bytes 20 | tf_op jit(solution)/shard_map/ppermute | solution.py:75
  32.2 9.2 %collective-permute-start.13 = (bf16[1,9,128,128]{3,2,1,0:T(8,128)(2,1)S(1)}, bf16[1,9,128,128]{3,2,1,0:T(8,128)(2,1)S(1)}, u32[]{:S(2)}, u32[]{:S(2)}) collective-permute-start(bf16[1,9,128,128]{3,2,1,0:T(8,128)(2,1)S(1)} %copy-done.1), channel_id=1, source_target_pairs={{0,1},{1,0},{2,3},{3,2},{4,5},{5,4},{6,7},{7,6},{8,9},{9,8},{10,11... | collective-permute-start | bytes 884744 | tf_op jit(solution)/shard_map/ppermute | solution.py:219
  33.0 1.8 %copy-start.6 = (bf16[1,128]{1,0:T(2,128)(2,1)S(1)}, bf16[1,128]{1,0:T(2,128)(2,1)}, u32[]{:S(2)}) copy-start(bf16[1,128]{1,0:T(2,128)(2,1)} %param.18) | copy-start | bytes 772
  34.8 3.2 %collective-permute-start.14 = (bf16[1,128]{1,0:T(2,128)(2,1)S(1)}, bf16[1,128]{1,0:T(2,128)(2,1)S(1)}, u32[]{:S(2)}, u32[]{:S(2)}) collective-permute-start(bf16[1,128]{1,0:T(2,128)(2,1)S(1)} %copy-done.6), channel_id=1, source_target_pairs={{0,1},{1,0},{2,3},{3,2},{4,5},{5,4},{6,7},{7,6},{8,9},{9,8},{10,11... | collective-permute-start | bytes 776 | tf_op jit(solution)/shard_map/ppermute | solution.py:220
  38.1 8.8 %collective-permute-start.6 = (f32[2,32,4,256]{3,1,2,0:T(8,128)S(1)}, f32[2,32,4,256]{3,1,2,0:T(8,128)S(1)}, u32[]{:S(2)}, u32[]{:S(2)}) collective-permute-start(f32[2,32,4,256]{3,1,2,0:T(8,128)S(1)} %add_add_fusion), channel_id=1, source_target_pairs={{0,32},{2,34},{4,36},{6,38},{8,40},{10,42},{12,44},{14,46},{16,48}... | collective-permute-start | bytes 786440 | tf_op jit(solution)/shard_map/ppermute | solution.py:78
  47.0 8.9 %collective-permute-start.10 = (f32[2,4,256]{2,1,0:T(4,128)S(1)}, f32[2,4,256]{2,1,0:T(4,128)S(1)}, u32[]{:S(2)}, u32[]{:S(2)}) collective-permute-start(f32[2,4,256]{2,1,0:T(4,128)S(1)} %bitcast.64), channel_id=1, source_target_pairs={{0,128},{2,130},{4,132},{6,134},{8,136},{10,138},{12,140},{14,142}... | collective-permute-start | bytes 24584 | tf_op jit(solution)/shard_map/ppermute | solution.py:80
  52.2 4.5 %collective-permute-start.12 = (f32[2,4,256]{2,1,0:T(4,128)S(1)}, f32[2,4,256]{2,1,0:T(4,128)S(1)}, u32[]{:S(2)}, u32[]{:S(2)}) collective-permute-start(f32[2,4,256]{2,1,0:T(4,128)S(1)} %bitcast.65), channel_id=1, source_target_pairs={{0,192},{2,194},{4,196},{6,198},{8,200},{10,202},{12,204},{14,206}... | collective-permute-start | bytes 24584 | tf_op jit(solution)/shard_map/ppermute | solution.py:80
  53.4 5.8 %collective-permute-start.8 = (f32[2,4,256]{2,1,0:T(4,128)S(1)}, f32[2,4,256]{2,1,0:T(4,128)S(1)}, u32[]{:S(2)}, u32[]{:S(2)}) collective-permute-start(f32[2,4,256]{2,1,0:T(4,128)S(1)} %bitcast.66), channel_id=1, source_target_pairs={{0,64},{2,66},{4,68},{6,70},{8,72},{10,74},{12,76},{14,78},{16,80}... | collective-permute-start | bytes 24584 | tf_op jit(solution)/shard_map/ppermute | solution.py:80

commit v10 on v9

--- a/solution.py
+++ b/solution.py
@@ -1,3 +1,5 @@
+import functools
+
 import numpy as np
 import jax
 import jax.numpy as jnp
@@ -96,7 +98,9 @@
     return values / (1.0 + jnp.exp(-values))
 
 
-def chain_kernel(coef_ref, state_ref, means_ref, lift_ref, embed_ref, conv_ref, gain_ref, out_ref, result_ref):
+def chain_kernel(
+    variables, coef_ref, state_ref, means_ref, lift_ref, embed_ref, conv_ref, gain_ref, out_ref, result_ref
+):
     rows, lanes = state_ref.shape
     pixel = lax.broadcasted_iota(jnp.int32, (rows, lanes), 0) % (SIDE * SIDE)
     col = pixel % SIDE
@@ -158,13 +162,14 @@
         denoised = keep_state * state + keep_net * net_out
         return state + move * (state - denoised)
 
-    result_ref[...] = lax.fori_loop(0, STEPS, one_step, state_ref[...], unroll=True)
-
-
-def run_chain(coefs, state, means, lift, embed, kernels, gains, out_weight):
+    finished = lax.fori_loop(0, STEPS, one_step, state_ref[...], unroll=True)
+    result_ref[...] = finished + pltpu.roll(means, lanes - variables, 1)
+
+
+def run_chain(variables, coefs, state, means, lift, embed, kernels, gains, out_weight):
     vmem = pltpu.MemorySpace.VMEM
     return pl.pallas_call(
-        chain_kernel,
+        functools.partial(chain_kernel, variables),
         out_shape=jax.ShapeDtypeStruct(state.shape, jnp.float32),
         in_specs=[pl.BlockSpec(memory_space=pltpu.MemorySpace.SMEM)]
         + [pl.BlockSpec(memory_space=vmem)] * 7,
@@ -242,6 +247,7 @@
         lift = jnp.pad(lift_weight, ((0, channels - 2 * variables), (0, 0)))
         out_pad = jnp.pad(out_weight, ((0, 0), (0, channels - variables)))
         finished = run_chain(
+            variables,
             step_coefficients(sigmas),
             to_lanes(states, 0, channels),
             to_lanes(means, variables, channels),
@@ -252,7 +258,7 @@
             out_pad,
         )
         finished = finished[:, :variables].reshape(half_hours, pixels, variables)
-        return (means + jnp.transpose(finished, (0, 2, 1)))[:, None]
+        return jnp.transpose(finished, (0, 2, 1))[:, None]
 
     return body
 

time: 86.5 us -> 104 us (1.20)
  waiting for transfers between devices: 13.6 us -> 29.7 us
  other arithmetic: 2.7 us -> 3.91 us
    ppermute x3, waiting for transfers between devices: 3.13 us -> 19.3 us  [broadcast_mean(): lax.ppermute(lax.dynamic_index_in_dim(block, wanted[d], 1, keepdims=False...]
    unnamed x20 -> x15, local copies, waits for them, and re-layouts: 2.4 us -> 0.73 us
  transfers between devices with their start and end apart: 15 -> 15, of which waited for: 6 -> 7; matrix products, arithmetic and copies ran while one was open for 6% -> 5% of each run, Pallas kernels for 0% -> 0%
where the time goes in v10:
time: 104 us; the launch traced here: 102 us
  starting transfers between devices  31.7 us (30%)
  waiting for transfers between devices  29.7 us (29%)
  Pallas kernels  23.5 us (23%)
  local copies, waits for them, and re-layouts  6.67 us (6%)
  between operations  6.52 us (6%)
  other arithmetic  3.91 us (4%)
    pallas_call x1, Pallas kernels, run_chain(): pl.pallas_call(functools.partial(chain_kernel, variables), out_shape=jax....  23.5 us
    ppermute x3, waiting for transfers between devices, broadcast_mean(): lax.ppermute(lax.dynamic_index_in_dim(block, wanted[d], 1, keepdims=False...  19.3 us
    ppermute x6, starting transfers between devices, broadcast_sum(): arrived = [lax.ppermute(block, 'member', shifts[d]) for d in stage]  10.4 us
    ppermute x3, starting transfers between devices, broadcast_mean(): lax.ppermute(tile[None], 'member', reversed_pairs(shifts_z[d]))[0]  10.1 us
    ppermute x3, starting transfers between devices, broadcast_mean(): lax.ppermute(lax.dynamic_index_in_dim(block, wanted[d], 1, keepdims=False...  8.37 us
    ppermute x1, waiting for transfers between devices, broadcast_mean(): block = block + lax.ppermute(block, 'member', shifts_z[1])  5.46 us
    ppermute x6, waiting for transfers between devices, broadcast_sum(): arrived = [lax.ppermute(block, 'member', shifts[d]) for d in stage]  3.89 us
    ppermute x1, starting transfers between devices, broadcast_mean(): block = block + lax.ppermute(block, 'member', shifts_z[1])  2.72 us
  transfers between devices with their start and end apart: 15, of which 7 were waited for; matrix products, arithmetic and copies ran while one was open for 5% of the time, Pallas kernels for 0%

profile of v10, /device:TPU:32, one launch (start us, length us, event | category | flops | bytes accessed | tf_op | source)
XLA Modules:
  0.0 102.1 jit_solution(12940233823122084077)
XLA Ops:
  0.0 0.8 dynamic-slice_compare_fusion
  0.8 1.1 %bitcast_select_fusion = f32[2,32,4,256]{3,2,1,0:T(4,128)S(1)} fusion(f32[1,4,32,4,256]{4,3,2,1,0:T(4,128)} %param.11, s32[]{:T(128)S(6)} %select_n.50, pred[2]{0:T(512)(128)(4,1)S(1)} %dynamic-slice_compare_fusion), kind=kLoop, calls=%fused_computation.6 | loop fusion | flops 65536 | bytes 524294 | tf_op jit(solution)/shard_map/jit(_where)/select_n | solution.py:242
  1.9 1.6 %collective-permute-start = (f32[2,32,4,256]{3,2,1,0:T(4,128)S(1)}, f32[2,32,4,256]{3,2,1,0:T(4,128)S(1)}, u32[]{:S(2)}, u32[]{:S(2)}) collective-permute-start(f32[2,32,4,256]{3,2,1,0:T(4,128)S(1)} %bitcast_select_fusion), channel_id=1, source_target_pairs={{0,8},{2,10},{4,12},{6,14},{8,16},{10,18},{12,20},{14,22},{16,24},... | collective-permute-start | bytes 786440 | tf_op jit(solution)/shard_map/ppermute | solution.py:60
  3.5 1.7 %collective-permute-start.1 = (f32[2,32,4,256]{3,2,1,0:T(4,128)S(1)}, f32[2,32,4,256]{3,2,1,0:T(4,128)S(1)}, u32[]{:S(2)}, u32[]{:S(2)}) collective-permute-start(f32[2,32,4,256]{3,2,1,0:T(4,128)S(1)} %bitcast_select_fusion), channel_id=1, source_target_pairs={{0,24},{2,26},{4,28},{6,30},{8,0},{10,2},{12,4},{14,6},{16,8},{18,... | collective-permute-start | bytes 786440 | tf_op jit(solution)/shard_map/ppermute | solution.py:60
  5.2 1.8 %collective-permute-start.2 = (f32[2,32,4,256]{3,2,1,0:T(4,128)S(1)}, f32[2,32,4,256]{3,2,1,0:T(4,128)S(1)}, u32[]{:S(2)}, u32[]{:S(2)}) collective-permute-start(f32[2,32,4,256]{3,2,1,0:T(4,128)S(1)} %bitcast_select_fusion), channel_id=1, source_target_pairs={{0,16},{2,18},{4,20},{6,22},{8,24},{10,26},{12,28},{14,30},{16,0},... | collective-permute-start | bytes 786440 | tf_op jit(solution)/shard_map/ppermute | solution.py:60
  7.0 5.4 %collective-permute-start.7 = (s32[1]{0:T(128)}, s32[1]{0:T(128)}, u32[]{:S(2)}, u32[]{:S(2)}) collective-permute-start(s32[1]{0:T(128)} %param.13), channel_id=1, source_target_pairs={{64,0},{66,2},{68,4},{70,6},{72,8},{74,10},{76,12},{78,14},{80,16}... | collective-permute-start | bytes 20 | tf_op jit(solution)/shard_map/ppermute | solution.py:77
  12.4 1.4 %collective-permute-start.9 = (s32[1]{0:T(128)}, s32[1]{0:T(128)}, u32[]{:S(2)}, u32[]{:S(2)}) collective-permute-start(s32[1]{0:T(128)} %param.13), channel_id=1, source_target_pairs={{128,0},{130,2},{132,4},{134,6},{136,8},{138,10},{140,12},{142,14}... | collective-permute-start | bytes 20 | tf_op jit(solution)/shard_map/ppermute | solution.py:77
  13.9 0.1 fusion.2
  13.9 2.2 %collective-permute-done.1 = f32[2,32,4,256]{3,2,1,0:T(4,128)S(1)} collective-permute-done((f32[2,32,4,256]{3,2,1,0:T(4,128)S(1)}, f32[2,32,4,256]{3,2,1,0:T(4,128)S(1)}, u32[]{:S(2)}, u32[]{:S(2)}) %collective-permute-start.1) | collective-permute-done | bytes 262176 | tf_op jit(solution)/shard_map/ppermute | solution.py:60
  16.1 1.7 %collective-permute-done.2 = f32[2,32,4,256]{3,2,1,0:T(4,128)S(1)} collective-permute-done((f32[2,32,4,256]{3,2,1,0:T(4,128)S(1)}, f32[2,32,4,256]{3,2,1,0:T(4,128)S(1)}, u32[]{:S(2)}, u32[]{:S(2)}) %collective-permute-start.2) | collective-permute-done | bytes 262176 | tf_op jit(solution)/shard_map/ppermute | solution.py:60
  17.8 0.2 add_add_fusion.1
  18.0 3.3 %collective-permute-start.5 = (f32[2,32,4,256]{3,2,1,0:T(4,128)S(1)}, f32[2,32,4,256]{3,2,1,0:T(4,128)S(1)}, u32[]{:S(2)}, u32[]{:S(2)}) collective-permute-start(f32[2,32,4,256]{3,2,1,0:T(4,128)S(1)} %add_add_fusion.1), channel_id=1, source_target_pairs={{0,4},{2,6},{4,0},{6,2},{8,12},{10,14},{12,8},{14,10},{16,20},{18,... | collective-permute-start | bytes 786440 | tf_op jit(solution)/shard_map/ppermute | solution.py:60
  21.3 1.1 %collective-permute-start.4 = (f32[2,32,4,256]{3,2,1,0:T(4,128)S(1)}, f32[2,32,4,256]{3,2,1,0:T(4,128)S(1)}, u32[]{:S(2)}, u32[]{:S(2)}) collective-permute-start(f32[2,32,4,256]{3,2,1,0:T(4,128)S(1)} %add_add_fusion.1), channel_id=1, source_target_pairs={{0,6},{2,0},{4,2},{6,4},{8,14},{10,8},{12,10},{14,12},{16,22},{18,... | collective-permute-start | bytes 786440 | tf_op jit(solution)/shard_map/ppermute | solution.py:60
  22.4 1.0 collective-permute-start.3
  24.1 0.1 copy.11
  24.2 0.6 reshape.20.coef_ref
  24.8 0.1 copy.12
  24.9 0.5 copy-done.5
  25.5 0.1 copy.17
  25.6 0.7 pad.16.state_ref
  26.3 0.6 pad.19.out_ref
  26.9 0.1 copy-done.3
  27.0 0.6 pad.18.lift_ref
  27.6 0.0 collective-permute-done.7
  27.6 3.3 %collective-permute-start.11 = (s32[1]{0:T(128)}, s32[1]{0:T(128)}, u32[]{:S(2)}, u32[]{:S(2)}) collective-permute-start(s32[1]{0:T(128)} %param.13), channel_id=1, source_target_pairs={{192,0},{194,2},{196,4},{198,6},{200,8},{202,10},{204,12},{206,14}... | collective-permute-start | bytes 20 | tf_op jit(solution)/shard_map/ppermute | solution.py:77
  32.3 0.1 collective-permute-start.13
  33.0 0.0 copy-start.6
  33.6 1.1 %collective-permute-done.11 = s32[1]{0:T(128)} collective-permute-done((s32[1]{0:T(128)}, s32[1]{0:T(128)}, u32[]{:S(2)}, u32[]{:S(2)}) %collective-permute-start.11) | collective-permute-done | bytes 36 | tf_op jit(solution)/shard_map/ppermute | solution.py:77
  37.9 0.1 add_add_fusion
  37.9 2.7 %collective-permute-start.6 = (f32[2,32,4,256]{3,2,1,0:T(4,128)S(1)}, f32[2,32,4,256]{3,2,1,0:T(4,128)S(1)}, u32[]{:S(2)}, u32[]{:S(2)}) collective-permute-start(f32[2,32,4,256]{3,2,1,0:T(4,128)S(1)} %bitcast.55), channel_id=1, source_target_pairs={{0,32},{2,34},{4,36},{6,38},{8,40},{10,42},{12,44},{14,46},{16,48}... | collective-permute-start | bytes 786440 | tf_op jit(solution)/shard_map/ppermute | solution.py:80
  40.7 0.6 maximum_convert_fusion.gain_ref
  41.3 5.5 %collective-permute-done.6 = f32[2,32,4,256]{3,2,1,0:T(4,128)S(1)} collective-permute-done((f32[2,32,4,256]{3,2,1,0:T(4,128)S(1)}, f32[2,32,4,256]{3,2,1,0:T(4,128)S(1)}, u32[]{:S(2)}, u32[]{:S(2)}) %collective-permute-start.6) | collective-permute-done | bytes 262176 | tf_op jit(solution)/shard_map/ppermute | solution.py:80
  46.7 0.1 add.67
  46.8 0.1 copy.15
  47.0 5.1 %collective-permute-start.10 = (f32[2,4,256]{1,2,0:T(8,128)S(1)}, f32[2,4,256]{1,2,0:T(8,128)S(1)}, u32[]{:S(2)}, u32[]{:S(2)}) collective-permute-start(f32[2,4,256]{1,2,0:T(8,128)S(1)} %bitcast.64), channel_id=1, source_target_pairs={{0,128},{2,130},{4,132},{6,134},{8,136},{10,138},{12,140},{14,142}... | collective-permute-start | bytes 24584 | tf_op jit(solution)/shard_map/ppermute | solution.py:82
  52.1 0.1 copy.16
  52.2 1.3 %collective-permute-start.12 = (f32[2,4,256]{1,2,0:T(8,128)S(1)}, f32[2,4,256]{1,2,0:T(8,128)S(1)}, u32[]{:S(2)}, u32[]{:S(2)}) collective-permute-start(f32[2,4,256]{1,2,0:T(8,128)S(1)} %bitcast.65), channel_id=1, source_target_pairs={{0,192},{2,194},{4,196},{6,198},{8,200},{10,202},{12,204},{14,206}... | collective-permute-start | bytes 24584 | tf_op jit(solution)/shard_map/ppermute | solution.py:82
  53.5 0.1 copy.14
  53.7 2.0 %collective-permute-start.8 = (f32[2,4,256]{1,2,0:T(8,128)S(1)}, f32[2,4,256]{1,2,0:T(8,128)S(1)}, u32[]{:S(2)}, u32[]{:S(2)}) collective-permute-start(f32[2,4,256]{1,2,0:T(8,128)S(1)} %bitcast.66), channel_id=1, source_target_pairs={{0,64},{2,66},{4,68},{6,70},{8,72},{10,74},{12,76},{14,78},{16,80}... | collective-permute-start | bytes 24584 | tf_op jit(solution)/shard_map/ppermute | solution.py:82
  55.7 0.9 pad_maximum_fusion.conv_ref
  56.6 0.1 copy.13
  56.7 8.7 %collective-permute-done.10 = f32[2,4,256]{1,2,0:T(8,128)S(1)} collective-permute-done((f32[2,4,256]{1,2,0:T(8,128)S(1)}, f32[2,4,256]{1,2,0:T(8,128)S(1)}, u32[]{:S(2)}, u32[]{:S(2)}) %collective-permute-start.10) | collective-permute-done | bytes 8224 | tf_op jit(solution)/shard_map/ppermute | solution.py:82
  65.4 4.3 %collective-permute-done.12 = f32[2,4,256]{1,2,0:T(8,128)S(1)} collective-permute-done((f32[2,4,256]{1,2,0:T(8,128)S(1)}, f32[2,4,256]{1,2,0:T(8,128)S(1)}, u32[]{:S(2)}, u32[]{:S(2)}) %collective-permute-start.12) | collective-permute-done | bytes 8224 | tf_op jit(solution)/shard_map/ppermute | solution.py:82
  69.7 6.3 %collective-permute-done.8 = f32[2,4,256]{1,2,0:T(8,128)S(1)} collective-permute-done((f32[2,4,256]{1,2,0:T(8,128)S(1)}, f32[2,4,256]{1,2,0:T(8,128)S(1)}, u32[]{:S(2)}, u32[]{:S(2)}) %collective-permute-start.8) | collective-permute-done | bytes 8224 | tf_op jit(solution)/shard_map/ppermute | solution.py:82
  76.0 0.1 fusion.1
  76.0 0.9 pad.17.means_ref
  76.9 23.5 %shard_map.100 = f32[512,128]{1,0:T(8,128)} custom-call(f32[40]{0:T(128)} %reshape.20.coef_ref, f32[512,128]{1,0:T(8,128)} %pad.16.state_ref, f32[512,128]{1,0:T(8,128)} %pad.17.means_ref, f32[128,128]{1,0:T(8,128)} %pad.18.lift_ref, f32[1,128]{1,0:T(1,128)} %bitcast.68, bf16[2,1152,128]{2,1,0:T(8,128)(2,1)} %pad_maximum_fusion.conv_ref, ...), custom_call_target="tpu_custom_call" | custom-call | tf_op jit(solution)/shard_map/pallas_call | solution.py:171
  100.4 1.7 %copy.18 = f32[2,256,4]{1,2,0:T(4,128)} copy(f32[2,256,4]{2,1,0:T(8,128)} %bitcast.60) | data formatting | bytes 16384 | tf_op jit(solution)/shard_map/reshape | solution.py:260
  (24 shorter events, 0.2 us)
Async XLA Ops:
  0.0 17.8 %copy-start = (f32[1,4,32,4,256]{4,3,2,1,0:T(4,128)S(1)}, f32[1,4,32,4,256]{4,3,2,1,0:T(4,128)}, u32[]{:S(2)}) copy-start(f32[1,4,32,4,256]{4,3,2,1,0:T(4,128)} %param.11) | copy-start | bytes 1572868
  0.8 13.1 %copy-start.2 = (f32[9]{0:T(128)S(1)}, f32[9]{0:T(128)}, u32[]{:S(2)}) copy-start(f32[9]{0:T(128)} %param.14) | copy-start | bytes 112
  1.9 12.1 %collective-permute-start = (f32[2,32,4,256]{3,2,1,0:T(4,128)S(1)}, f32[2,32,4,256]{3,2,1,0:T(4,128)S(1)}, u32[]{:S(2)}, u32[]{:S(2)}) collective-permute-start(f32[2,32,4,256]{3,2,1,0:T(4,128)S(1)} %bitcast_select_fusion), channel_id=1, source_target_pairs={{0,8},{2,10},{4,12},{6,14},{8,16},{10,18},{12,20},{14,22},{16,24},... | collective-permute-start | bytes 786440 | tf_op jit(solution)/shard_map/ppermute | solution.py:60
  3.5 12.7 %collective-permute-start.1 = (f32[2,32,4,256]{3,2,1,0:T(4,128)S(1)}, f32[2,32,4,256]{3,2,1,0:T(4,128)S(1)}, u32[]{:S(2)}, u32[]{:S(2)}) collective-permute-start(f32[2,32,4,256]{3,2,1,0:T(4,128)S(1)} %bitcast_select_fusion), channel_id=1, source_target_pairs={{0,24},{2,26},{4,28},{6,30},{8,0},{10,2},{12,4},{14,6},{16,8},{18,... | collective-permute-start | bytes 786440 | tf_op jit(solution)/shard_map/ppermute | solution.py:60
  5.2 12.6 %collective-permute-start.2 = (f32[2,32,4,256]{3,2,1,0:T(4,128)S(1)}, f32[2,32,4,256]{3,2,1,0:T(4,128)S(1)}, u32[]{:S(2)}, u32[]{:S(2)}) collective-permute-start(f32[2,32,4,256]{3,2,1,0:T(4,128)S(1)} %bitcast_select_fusion), channel_id=1, source_target_pairs={{0,16},{2,18},{4,20},{6,22},{8,24},{10,26},{12,28},{14,30},{16,0},... | collective-permute-start | bytes 786440 | tf_op jit(solution)/shard_map/ppermute | solution.py:60
  7.0 20.6 %collective-permute-start.7 = (s32[1]{0:T(128)}, s32[1]{0:T(128)}, u32[]{:S(2)}, u32[]{:S(2)}) collective-permute-start(s32[1]{0:T(128)} %param.13), channel_id=1, source_target_pairs={{64,0},{66,2},{68,4},{70,6},{72,8},{74,10},{76,12},{78,14},{80,16}... | collective-permute-start | bytes 20 | tf_op jit(solution)/shard_map/ppermute | solution.py:77
  12.4 19.9 %collective-permute-start.9 = (s32[1]{0:T(128)}, s32[1]{0:T(128)}, u32[]{:S(2)}, u32[]{:S(2)}) collective-permute-start(s32[1]{0:T(128)} %param.13), channel_id=1, source_target_pairs={{128,0},{130,2},{132,4},{134,6},{136,8},{138,10},{140,12},{142,14}... | collective-permute-start | bytes 20 | tf_op jit(solution)/shard_map/ppermute | solution.py:77
  13.9 9.4 %copy-start.4 = (f32[1,4,4,256]{3,2,1,0:T(4,128)S(1)}, f32[1,4,4,256]{3,2,1,0:T(4,128)}, u32[]{:S(2)}) copy-start(f32[1,4,4,256]{3,2,1,0:T(4,128)} %param.10) | copy-start | bytes 49156
  18.0 19.8 %collective-permute-start.5 = (f32[2,32,4,256]{3,2,1,0:T(4,128)S(1)}, f32[2,32,4,256]{3,2,1,0:T(4,128)S(1)}, u32[]{:S(2)}, u32[]{:S(2)}) collective-permute-start(f32[2,32,4,256]{3,2,1,0:T(4,128)S(1)} %add_add_fusion.1), channel_id=1, source_target_pairs={{0,4},{2,6},{4,0},{6,2},{8,12},{10,14},{12,8},{14,10},{16,20},{18,... | collective-permute-start | bytes 786440 | tf_op jit(solution)/shard_map/ppermute | solution.py:60
  21.3 16.5 %collective-permute-start.4 = (f32[2,32,4,256]{3,2,1,0:T(4,128)S(1)}, f32[2,32,4,256]{3,2,1,0:T(4,128)S(1)}, u32[]{:S(2)}, u32[]{:S(2)}) collective-permute-start(f32[2,32,4,256]{3,2,1,0:T(4,128)S(1)} %add_add_fusion.1), channel_id=1, source_target_pairs={{0,6},{2,0},{4,2},{6,4},{8,14},{10,8},{12,10},{14,12},{16,22},{18,... | collective-permute-start | bytes 786440 | tf_op jit(solution)/shard_map/ppermute | solution.py:60
  22.4 15.5 %collective-permute-start.3 = (f32[2,32,4,256]{3,2,1,0:T(4,128)S(1)}, f32[2,32,4,256]{3,2,1,0:T(4,128)S(1)}, u32[]{:S(2)}, u32[]{:S(2)}) collective-permute-start(f32[2,32,4,256]{3,2,1,0:T(4,128)S(1)} %add_add_fusion.1), channel_id=1, source_target_pairs={{0,2},{2,4},{4,6},{6,0},{8,10},{10,12},{12,14},{14,8},{16,18},{18,... | collective-permute-start | bytes 786440 | tf_op jit(solution)/shard_map/ppermute | solution.py:60
  24.8 0.7 copy-start.5
  25.6 6.7 %copy-start.1 = (bf16[1,9,128,128]{3,2,1,0:T(8,128)(2,1)S(1)}, bf16[1,9,128,128]{3,2,1,0:T(8,128)(2,1)}, u32[]{:S(2)}) copy-start(bf16[1,9,128,128]{3,2,1,0:T(8,128)(2,1)} %param.17) | copy-start | bytes 884740
  26.3 0.7 copy-start.3
  27.6 7.0 %collective-permute-start.11 = (s32[1]{0:T(128)}, s32[1]{0:T(128)}, u32[]{:S(2)}, u32[]{:S(2)}) collective-permute-start(s32[1]{0:T(128)} %param.13), channel_id=1, source_target_pairs={{192,0},{194,2},{196,4},{198,6},{200,8},{202,10},{204,12},{206,14}... | collective-permute-start | bytes 20 | tf_op jit(solution)/shard_map/ppermute | solution.py:77
  32.3 8.9 %collective-permute-start.13 = (bf16[1,9,128,128]{3,2,1,0:T(8,128)(2,1)S(1)}, bf16[1,9,128,128]{3,2,1,0:T(8,128)(2,1)S(1)}, u32[]{:S(2)}, u32[]{:S(2)}) collective-permute-start(bf16[1,9,128,128]{3,2,1,0:T(8,128)(2,1)S(1)} %copy-done.1), channel_id=1, source_target_pairs={{0,1},{1,0},{2,3},{3,2},{4,5},{5,4},{6,7},{7,6},{8,9},{9,8},{10,11... | collective-permute-start | bytes 884744 | tf_op jit(solution)/shard_map/ppermute | solution.py:224
  33.0 1.7 %copy-start.6 = (bf16[1,128]{1,0:T(2,128)(2,1)S(1)}, bf16[1,128]{1,0:T(2,128)(2,1)}, u32[]{:S(2)}) copy-start(bf16[1,128]{1,0:T(2,128)(2,1)} %param.18) | copy-start | bytes 772
  34.7 3.2 %collective-permute-start.14 = (bf16[1,128]{1,0:T(2,128)(2,1)S(1)}, bf16[1,128]{1,0:T(2,128)(2,1)S(1)}, u32[]{:S(2)}, u32[]{:S(2)}) collective-permute-start(bf16[1,128]{1,0:T(2,128)(2,1)S(1)} %copy-done.6), channel_id=1, source_target_pairs={{0,1},{1,0},{2,3},{3,2},{4,5},{5,4},{6,7},{7,6},{8,9},{9,8},{10,11... | collective-permute-start | bytes 776 | tf_op jit(solution)/shard_map/ppermute | solution.py:225
  37.9 8.8 %collective-permute-start.6 = (f32[2,32,4,256]{3,2,1,0:T(4,128)S(1)}, f32[2,32,4,256]{3,2,1,0:T(4,128)S(1)}, u32[]{:S(2)}, u32[]{:S(2)}) collective-permute-start(f32[2,32,4,256]{3,2,1,0:T(4,128)S(1)} %bitcast.55), channel_id=1, source_target_pairs={{0,32},{2,34},{4,36},{6,38},{8,40},{10,42},{12,44},{14,46},{16,48}... | collective-permute-start | bytes 786440 | tf_op jit(solution)/shard_map/ppermute | solution.py:80
  47.0 18.4 %collective-permute-start.10 = (f32[2,4,256]{1,2,0:T(8,128)S(1)}, f32[2,4,256]{1,2,0:T(8,128)S(1)}, u32[]{:S(2)}, u32[]{:S(2)}) collective-permute-start(f32[2,4,256]{1,2,0:T(8,128)S(1)} %bitcast.64), channel_id=1, source_target_pairs={{0,128},{2,130},{4,132},{6,134},{8,136},{10,138},{12,140},{14,142}... | collective-permute-start | bytes 24584 | tf_op jit(solution)/shard_map/ppermute | solution.py:82
  52.2 17.4 %collective-permute-start.12 = (f32[2,4,256]{1,2,0:T(8,128)S(1)}, f32[2,4,256]{1,2,0:T(8,128)S(1)}, u32[]{:S(2)}, u32[]{:S(2)}) collective-permute-start(f32[2,4,256]{1,2,0:T(8,128)S(1)} %bitcast.65), channel_id=1, source_target_pairs={{0,192},{2,194},{4,196},{6,198},{8,200},{10,202},{12,204},{14,206}... | collective-permute-start | bytes 24584 | tf_op jit(solution)/shard_map/ppermute | solution.py:82
  53.7 22.3 %collective-permute-start.8 = (f32[2,4,256]{1,2,0:T(8,128)S(1)}, f32[2,4,256]{1,2,0:T(8,128)S(1)}, u32[]{:S(2)}, u32[]{:S(2)}) collective-permute-start(f32[2,4,256]{1,2,0:T(8,128)S(1)} %bitcast.66), channel_id=1, source_target_pairs={{0,64},{2,66},{4,68},{6,70},{8,72},{10,74},{12,76},{14,78},{16,80}... | collective-permute-start | bytes 24584 | tf_op jit(solution)/shard_map/ppermute | solution.py:82

commit v11 on v9

--- a/solution.py
+++ b/solution.py
@@ -70,19 +70,20 @@
     if size_z < 4 or size_z % 2:
         block = broadcast_sum(kept, rings)
         return lax.dynamic_index_in_dim(block, tile, 1, keepdims=False)
-    far = range(2, size_z, 2)
-    wanted = {
-        d: lax.ppermute(tile[None], "member", reversed_pairs(shifts_z[d]))[0] for d in far
+    known = {
+        d: lax.ppermute(tile[None], "member", reversed_pairs(shifts_z[d]))[0]
+        for d in range(1, size_z)
     }
+    known[0] = tile
+    evens = range(0, size_z, 2)
     block = broadcast_sum(kept, rings[:-1])
-    block = block + lax.ppermute(block, "member", shifts_z[1])
+    sent = jnp.take(block, jnp.stack([known[1 + e] for e in evens]), axis=1, mode="clip")
+    block = jnp.take(block, jnp.stack([known[e] for e in evens]), axis=1, mode="clip")
+    block = block + lax.ppermute(sent, "member", shifts_z[1])
     arrived = [
-        lax.ppermute(
-            lax.dynamic_index_in_dim(block, wanted[d], 1, keepdims=False), "member", shifts_z[d]
-        )
-        for d in far
+        lax.ppermute(block[:, slot], "member", shifts_z[e]) for slot, e in enumerate(evens) if e
     ]
-    mean = lax.dynamic_index_in_dim(block, tile, 1, keepdims=False)
+    mean = block[:, 0]
     for part in arrived:
         mean = mean + part
     return mean

time: 86.5 us -> 97.8 us (1.13)
  the two profiles are of different devices: /device:TPU:32 before, /device:TPU:8 now
where the time goes in v11:
time: 97.8 us; the launch traced here: 97.5 us
  starting transfers between devices  35.4 us (36%)
  Pallas kernels  23.5 us (24%)
  waiting for transfers between devices  21.5 us (22%)
  local copies, waits for them, and re-layouts  8.07 us (8%)
  other arithmetic  8.07 us (8%)
    pallas_call x1, Pallas kernels, run_chain(): pl.pallas_call(chain_kernel, out_shape=jax.ShapeDtypeStruct(state.shape,...  23.5 us
    ppermute x7, starting transfers between devices, broadcast_mean(): lax.ppermute(tile[None], 'member', reversed_pairs(shifts_z[d]))[0]  16.5 us
    ppermute x6, waiting for transfers between devices, broadcast_sum(): arrived = [lax.ppermute(block, 'member', shifts[d]) for d in stage]  11.1 us
    ppermute x6, starting transfers between devices, broadcast_sum(): arrived = [lax.ppermute(block, 'member', shifts[d]) for d in stage]  9.53 us
    ppermute x3, starting transfers between devices, broadcast_mean(): lax.ppermute(block[:, slot], 'member', shifts_z[e])  8.26 us
    ppermute x7, waiting for transfers between devices, broadcast_mean(): lax.ppermute(tile[None], 'member', reversed_pairs(shifts_z[d]))[0]  6.43 us
    ppermute x1, waiting for transfers between devices, broadcast_mean(): block = block + lax.ppermute(sent, 'member', shifts_z[1])  3.48 us
    another operation x1, other arithmetic, broadcast_mean(): jnp.stack([known[1 + e] for e in evens])  2.58 us
  transfers between devices with their start and end apart: 19, of which 9 were waited for; matrix products, arithmetic and copies ran while one was open for 11% of the time, Pallas kernels for 0%

profile of v11, /device:TPU:8, one launch (start us, length us, event | category | flops | bytes accessed | tf_op | source)
XLA Modules:
  0.0 97.5 jit_solution(11036023161560368518)
XLA Ops:
  0.0 0.7 copy-done.7
  0.7 1.1 %bitcast_select_fusion = f32[2,32,4,256]{3,2,1,0:T(4,128)S(1)} fusion(f32[1,4,32,4,256]{4,3,2,1,0:T(4,128)} %param.11, s32[]{:T(128)S(6)} %select_n.37, pred[2]{0:T(512)(128)(4,1)S(1)} %dynamic-slice_compare_fusion), kind=kLoop, calls=%fused_computation.5 | loop fusion | flops 65536 | bytes 524294 | tf_op jit(solution)/shard_map/jit(_where)/select_n | solution.py:238
  1.8 1.6 %collective-permute-start = (f32[2,32,4,256]{3,2,1,0:T(4,128)S(1)}, f32[2,32,4,256]{3,2,1,0:T(4,128)S(1)}, u32[]{:S(2)}, u32[]{:S(2)}) collective-permute-start(f32[2,32,4,256]{3,2,1,0:T(4,128)S(1)} %bitcast_select_fusion), channel_id=1, source_target_pairs={{0,8},{2,10},{4,12},{6,14},{8,16},{10,18},{12,20},{14,22},{16,24},... | collective-permute-start | bytes 786440 | tf_op jit(solution)/shard_map/ppermute | solution.py:58
  3.4 1.7 %collective-permute-start.1 = (f32[2,32,4,256]{3,2,1,0:T(4,128)S(1)}, f32[2,32,4,256]{3,2,1,0:T(4,128)S(1)}, u32[]{:S(2)}, u32[]{:S(2)}) collective-permute-start(f32[2,32,4,256]{3,2,1,0:T(4,128)S(1)} %bitcast_select_fusion), channel_id=1, source_target_pairs={{0,24},{2,26},{4,28},{6,30},{8,0},{10,2},{12,4},{14,6},{16,8},{18,... | collective-permute-start | bytes 786440 | tf_op jit(solution)/shard_map/ppermute | solution.py:58
  5.1 1.8 %collective-permute-start.2 = (f32[2,32,4,256]{3,2,1,0:T(4,128)S(1)}, f32[2,32,4,256]{3,2,1,0:T(4,128)S(1)}, u32[]{:S(2)}, u32[]{:S(2)}) collective-permute-start(f32[2,32,4,256]{3,2,1,0:T(4,128)S(1)} %bitcast_select_fusion), channel_id=1, source_target_pairs={{0,16},{2,18},{4,20},{6,22},{8,24},{10,26},{12,28},{14,30},{16,0},... | collective-permute-start | bytes 786440 | tf_op jit(solution)/shard_map/ppermute | solution.py:58
  6.9 6.7 %collective-permute-start.10 = (s32[1]{0:T(128)}, s32[1]{0:T(128)}, u32[]{:S(2)}, u32[]{:S(2)}) collective-permute-start(s32[1]{0:T(128)} %param.13), channel_id=1, source_target_pairs={{96,0},{98,2},{100,4},{102,6},{104,8},{106,10},{108,12},{110,14},{... | collective-permute-start | bytes 20 | tf_op jit(solution)/shard_map/ppermute | solution.py:74
  14.4 0.6 copy-done.2
  15.2 0.1 copy.11
  15.2 0.7 reshape.20.coef_ref
  16.0 0.1 copy.12
  16.1 0.5 copy-done.5
  16.6 0.1 copy.14
  16.7 0.7 pad.16.state_ref
  17.4 0.6 pad.19.out_ref
  18.1 0.6 pad.18.lift_ref
  18.8 1.0 %collective-permute-start.12 = (s32[1]{0:T(128)}, s32[1]{0:T(128)}, u32[]{:S(2)}, u32[]{:S(2)}) collective-permute-start(s32[1]{0:T(128)} %param.13), channel_id=1, source_target_pairs={{224,0},{226,2},{228,4},{230,6},{232,8},{234,10},{236,12},{238,14}... | collective-permute-start | bytes 20 | tf_op jit(solution)/shard_map/ppermute | solution.py:74
  19.8 0.7 collective-permute-done.11
  20.5 2.5 %collective-permute-start.9 = (s32[1]{0:T(128)}, s32[1]{0:T(128)}, u32[]{:S(2)}, u32[]{:S(2)}) collective-permute-start(s32[1]{0:T(128)} %param.13), channel_id=1, source_target_pairs={{32,0},{34,2},{36,4},{38,6},{40,8},{42,10},{44,12},{46,14},{48,16}... | collective-permute-start | bytes 20 | tf_op jit(solution)/shard_map/ppermute | solution.py:74
  23.0 1.5 %collective-permute-done.12 = s32[1]{0:T(128)} collective-permute-done((s32[1]{0:T(128)}, s32[1]{0:T(128)}, u32[]{:S(2)}, u32[]{:S(2)}) %collective-permute-start.12) | collective-permute-done | bytes 36 | tf_op jit(solution)/shard_map/ppermute | solution.py:74
  24.5 2.5 %collective-permute-start.6 = (s32[1]{0:T(128)}, s32[1]{0:T(128)}, u32[]{:S(2)}, u32[]{:S(2)}) collective-permute-start(s32[1]{0:T(128)} %param.13), channel_id=1, source_target_pairs={{64,0},{66,2},{68,4},{70,6},{72,8},{74,10},{76,12},{78,14},{80,16}... | collective-permute-start | bytes 20 | tf_op jit(solution)/shard_map/ppermute | solution.py:74
  27.0 2.1 %collective-permute-start.7 = (s32[1]{0:T(128)}, s32[1]{0:T(128)}, u32[]{:S(2)}, u32[]{:S(2)}) collective-permute-start(s32[1]{0:T(128)} %param.13), channel_id=1, source_target_pairs={{128,0},{130,2},{132,4},{134,6},{136,8},{138,10},{140,12},{142,14}... | collective-permute-start | bytes 20 | tf_op jit(solution)/shard_map/ppermute | solution.py:74
  29.0 2.6 %pad_add_fusion.1 = s32[4]{0:T(128)S(1)} fusion(s32[1]{0:T(128)} %collective-permute-done.12, s32[1]{0:T(128)} %collective-permute-done.11, s32[1]{0:T(128)} %collective-permute-done.10, s32[1]{0:T(128)} %collective-permute-done.9), kind=kLoop, calls=%fused_computation.25 | loop fusion | flops 12 | bytes 32 | tf_op jit(solution)/shard_map/stack | solution.py:80
  31.6 1.8 %collective-permute-start.8 = (s32[1]{0:T(128)}, s32[1]{0:T(128)}, u32[]{:S(2)}, u32[]{:S(2)}) collective-permute-start(s32[1]{0:T(128)} %param.13), channel_id=1, source_target_pairs={{192,0},{194,2},{196,4},{198,6},{200,8},{202,10},{204,12},{206,14}... | collective-permute-start | bytes 20 | tf_op jit(solution)/shard_map/ppermute | solution.py:74
  33.4 1.1 %collective-permute-done.7 = s32[1]{0:T(128)} collective-permute-done((s32[1]{0:T(128)}, s32[1]{0:T(128)}, u32[]{:S(2)}, u32[]{:S(2)}) %collective-permute-start.7) | collective-permute-done | bytes 36 | tf_op jit(solution)/shard_map/ppermute | solution.py:74
  34.5 3.0 %collective-permute-done.8 = s32[1]{0:T(128)} collective-permute-done((s32[1]{0:T(128)}, s32[1]{0:T(128)}, u32[]{:S(2)}, u32[]{:S(2)}) %collective-permute-start.8) | collective-permute-done | bytes 36 | tf_op jit(solution)/shard_map/ppermute | solution.py:74
  37.6 1.8 %pad_add_fusion = s32[4]{0:T(128)S(1)} fusion(s32[1]{0:T(128)} %collective-permute-done.8, s32[1]{0:T(128)} %collective-permute-done.7, s32[1]{0:T(128)} %collective-permute-done.6, s32[1]{0:T(128)S(6)} %copy.16), kind=kLoop, calls=%fused_computation.24 | loop fusion | flops 12 | bytes 32 | tf_op jit(solution)/shard_map/stack | solution.py:81
  39.5 0.2 add_add_fusion.1
  39.7 2.4 %collective-permute-start.5 = (f32[2,32,4,256]{3,2,1,0:T(4,128)S(1)}, f32[2,32,4,256]{3,2,1,0:T(4,128)S(1)}, u32[]{:S(2)}, u32[]{:S(2)}) collective-permute-start(f32[2,32,4,256]{3,2,1,0:T(4,128)S(1)} %add_add_fusion.1), channel_id=1, source_target_pairs={{0,4},{2,6},{4,0},{6,2},{8,12},{10,14},{12,8},{14,10},{16,20},{18,... | collective-permute-start | bytes 786440 | tf_op jit(solution)/shard_map/ppermute | solution.py:58
  42.0 1.3 %collective-permute-start.4 = (f32[2,32,4,256]{3,2,1,0:T(4,128)S(1)}, f32[2,32,4,256]{3,2,1,0:T(4,128)S(1)}, u32[]{:S(2)}, u32[]{:S(2)}) collective-permute-start(f32[2,32,4,256]{3,2,1,0:T(4,128)S(1)} %add_add_fusion.1), channel_id=1, source_target_pairs={{0,6},{2,0},{4,2},{6,4},{8,14},{10,8},{12,10},{14,12},{16,22},{18,... | collective-permute-start | bytes 786440 | tf_op jit(solution)/shard_map/ppermute | solution.py:58
  43.4 0.7 collective-permute-start.3
  44.1 0.6 maximum_convert_fusion.gain_ref
  44.6 5.8 %collective-permute-done.5 = f32[2,32,4,256]{3,2,1,0:T(4,128)S(1)} collective-permute-done((f32[2,32,4,256]{3,2,1,0:T(4,128)S(1)}, f32[2,32,4,256]{3,2,1,0:T(4,128)S(1)}, u32[]{:S(2)}, u32[]{:S(2)}) %collective-permute-start.5) | collective-permute-done | bytes 262176 | tf_op jit(solution)/shard_map/ppermute | solution.py:58
  50.5 5.1 %collective-permute-done.4 = f32[2,32,4,256]{3,2,1,0:T(4,128)S(1)} collective-permute-done((f32[2,32,4,256]{3,2,1,0:T(4,128)S(1)}, f32[2,32,4,256]{3,2,1,0:T(4,128)S(1)}, u32[]{:S(2)}, u32[]{:S(2)}) %collective-permute-start.4) | collective-permute-done | bytes 262176 | tf_op jit(solution)/shard_map/ppermute | solution.py:58
  55.6 0.2 collective-permute-done.3
  55.8 0.6 gather_fusion.1
  56.4 1.1 %collective-permute-start.13 = (f32[2,4,4,256]{3,2,0,1:T(4,128)S(1)}, f32[2,4,4,256]{3,2,0,1:T(4,128)S(1)}, u32[]{:S(2)}, u32[]{:S(2)}) collective-permute-start(f32[2,4,4,256]{3,2,0,1:T(4,128)S(1)} %bitcast.68), channel_id=1, source_target_pairs={{0,32},{2,34},{4,36},{6,38},{8,40},{10,42},{12,44},{14,46},{16,48}... | collective-permute-start | bytes 98312 | tf_op jit(solution)/shard_map/ppermute | solution.py:82
  57.5 0.6 gather_fusion
  58.1 3.5 %collective-permute-done.13 = f32[2,4,4,256]{3,2,0,1:T(4,128)S(1)} collective-permute-done((f32[2,4,4,256]{3,2,0,1:T(4,128)S(1)}, f32[2,4,4,256]{3,2,0,1:T(4,128)S(1)}, u32[]{:S(2)}, u32[]{:S(2)}) %collective-permute-start.13) | collective-permute-done | bytes 32800 | tf_op jit(solution)/shard_map/ppermute | solution.py:82
  61.6 0.3 collective-permute-start.14
  61.9 4.0 %collective-permute-start.15 = (f32[2,4,256]{2,1,0:T(4,128)S(1)}, f32[2,4,256]{2,1,0:T(4,128)S(1)}, u32[]{:S(2)}, u32[]{:S(2)}) collective-permute-start(f32[2,4,256]{2,1,0:T(4,128)S(1)} %get-tuple-element.9), channel_id=1, source_target_pairs={{0,128},{2,130},{4,132},{6,134},{8,136},{10,138},{12,140},{14,142}... | collective-permute-start | bytes 24584 | tf_op jit(solution)/shard_map/ppermute | solution.py:84
  65.8 4.0 %collective-permute-start.16 = (f32[2,4,256]{2,1,0:T(4,128)S(1)}, f32[2,4,256]{2,1,0:T(4,128)S(1)}, u32[]{:S(2)}, u32[]{:S(2)}) collective-permute-start(f32[2,4,256]{2,1,0:T(4,128)S(1)} %get-tuple-element.8), channel_id=1, source_target_pairs={{0,192},{2,194},{4,196},{6,198},{8,200},{10,202},{12,204},{14,206}... | collective-permute-start | bytes 24584 | tf_op jit(solution)/shard_map/ppermute | solution.py:84
  69.9 0.9 pad_maximum_fusion.conv_ref
  70.8 0.5 collective-permute-done.16
  71.3 0.1 copy.13
  71.4 0.9 pad.17.means_ref
  72.3 23.5 %shard_map.100 = f32[512,128]{1,0:T(8,128)} custom-call(f32[40]{0:T(128)} %reshape.20.coef_ref, f32[512,128]{1,0:T(8,128)} %pad.16.state_ref, f32[512,128]{1,0:T(8,128)} %pad.17.means_ref, f32[128,128]{1,0:T(8,128)} %pad.18.lift_ref, f32[1,128]{1,0:T(1,128)} %bitcast.70, bf16[2,1152,128]{2,1,0:T(8,128)(2,1)} %pad_maximum_fusion.conv_ref, ...), custom_call_target="tpu_custom_call" | custom-call | tf_op jit(solution)/shard_map/pallas_call | solution.py:167
  95.8 1.1 %copy.15 = f32[2,256,4]{1,2,0:T(4,128)S(1)} copy(f32[2,256,4]{2,1,0:T(8,128)} %bitcast.61) | data formatting | bytes 16384 | tf_op jit(solution)/shard_map/reshape | solution.py:255
  96.8 0.6 fusion.3
  (38 shorter events, 0.5 us)
Async XLA Ops:
  0.0 0.7 copy-start.7
  1.8 37.6 %collective-permute-start = (f32[2,32,4,256]{3,2,1,0:T(4,128)S(1)}, f32[2,32,4,256]{3,2,1,0:T(4,128)S(1)}, u32[]{:S(2)}, u32[]{:S(2)}) collective-permute-start(f32[2,32,4,256]{3,2,1,0:T(4,128)S(1)} %bitcast_select_fusion), channel_id=1, source_target_pairs={{0,8},{2,10},{4,12},{6,14},{8,16},{10,18},{12,20},{14,22},{16,24},... | collective-permute-start | bytes 786440 | tf_op jit(solution)/shard_map/ppermute | solution.py:58
  3.4 36.0 %collective-permute-start.1 = (f32[2,32,4,256]{3,2,1,0:T(4,128)S(1)}, f32[2,32,4,256]{3,2,1,0:T(4,128)S(1)}, u32[]{:S(2)}, u32[]{:S(2)}) collective-permute-start(f32[2,32,4,256]{3,2,1,0:T(4,128)S(1)} %bitcast_select_fusion), channel_id=1, source_target_pairs={{0,24},{2,26},{4,28},{6,30},{8,0},{10,2},{12,4},{14,6},{16,8},{18,... | collective-permute-start | bytes 786440 | tf_op jit(solution)/shard_map/ppermute | solution.py:58
  5.1 34.3 %collective-permute-start.2 = (f32[2,32,4,256]{3,2,1,0:T(4,128)S(1)}, f32[2,32,4,256]{3,2,1,0:T(4,128)S(1)}, u32[]{:S(2)}, u32[]{:S(2)}) collective-permute-start(f32[2,32,4,256]{3,2,1,0:T(4,128)S(1)} %bitcast_select_fusion), channel_id=1, source_target_pairs={{0,16},{2,18},{4,20},{6,22},{8,24},{10,26},{12,28},{14,30},{16,0},... | collective-permute-start | bytes 786440 | tf_op jit(solution)/shard_map/ppermute | solution.py:58
  6.9 11.8 %collective-permute-start.10 = (s32[1]{0:T(128)}, s32[1]{0:T(128)}, u32[]{:S(2)}, u32[]{:S(2)}) collective-permute-start(s32[1]{0:T(128)} %param.13), channel_id=1, source_target_pairs={{96,0},{98,2},{100,4},{102,6},{104,8},{106,10},{108,12},{110,14},{... | collective-permute-start | bytes 20 | tf_op jit(solution)/shard_map/ppermute | solution.py:74
  13.7 6.8 %collective-permute-start.11 = (s32[1]{0:T(128)}, s32[1]{0:T(128)}, u32[]{:S(2)}, u32[]{:S(2)}) collective-permute-start(s32[1]{0:T(128)} %param.13), channel_id=1, source_target_pairs={{160,0},{162,2},{164,4},{166,6},{168,8},{170,10},{172,12},{174,14}... | collective-permute-start | bytes 20 | tf_op jit(solution)/shard_map/ppermute | solution.py:74
  14.4 0.7 copy-start.2
  15.1 0.8 copy-start.4
  15.9 0.7 copy-start.5
  16.0 23.5 %copy-start = (f32[1,4,32,4,256]{4,3,2,1,0:T(4,128)S(1)}, f32[1,4,32,4,256]{4,3,2,1,0:T(4,128)}, u32[]{:S(2)}) copy-start(f32[1,4,32,4,256]{4,3,2,1,0:T(4,128)} %param.11) | copy-start | bytes 1572868
  16.7 17.8 %copy-start.1 = (bf16[1,9,128,128]{3,2,1,0:T(8,128)(2,1)S(1)}, bf16[1,9,128,128]{3,2,1,0:T(8,128)(2,1)}, u32[]{:S(2)}) copy-start(bf16[1,9,128,128]{3,2,1,0:T(8,128)(2,1)} %param.17) | copy-start | bytes 884740
  17.4 0.7 copy-start.3
  18.8 18.8 %copy-start.6 = (bf16[1,128]{1,0:T(2,128)(2,1)S(1)}, bf16[1,128]{1,0:T(2,128)(2,1)}, u32[]{:S(2)}) copy-start(bf16[1,128]{1,0:T(2,128)(2,1)} %param.18) | copy-start | bytes 772
  18.8 5.7 %collective-permute-start.12 = (s32[1]{0:T(128)}, s32[1]{0:T(128)}, u32[]{:S(2)}, u32[]{:S(2)}) collective-permute-start(s32[1]{0:T(128)} %param.13), channel_id=1, source_target_pairs={{224,0},{226,2},{228,4},{230,6},{232,8},{234,10},{236,12},{238,14}... | collective-permute-start | bytes 20 | tf_op jit(solution)/shard_map/ppermute | solution.py:74
  20.5 6.5 %collective-permute-start.9 = (s32[1]{0:T(128)}, s32[1]{0:T(128)}, u32[]{:S(2)}, u32[]{:S(2)}) collective-permute-start(s32[1]{0:T(128)} %param.13), channel_id=1, source_target_pairs={{32,0},{34,2},{36,4},{38,6},{40,8},{42,10},{44,12},{46,14},{48,16}... | collective-permute-start | bytes 20 | tf_op jit(solution)/shard_map/ppermute | solution.py:74
  24.5 7.1 %collective-permute-start.6 = (s32[1]{0:T(128)}, s32[1]{0:T(128)}, u32[]{:S(2)}, u32[]{:S(2)}) collective-permute-start(s32[1]{0:T(128)} %param.13), channel_id=1, source_target_pairs={{64,0},{66,2},{68,4},{70,6},{72,8},{74,10},{76,12},{78,14},{80,16}... | collective-permute-start | bytes 20 | tf_op jit(solution)/shard_map/ppermute | solution.py:74
  27.0 7.6 %collective-permute-start.7 = (s32[1]{0:T(128)}, s32[1]{0:T(128)}, u32[]{:S(2)}, u32[]{:S(2)}) collective-permute-start(s32[1]{0:T(128)} %param.13), channel_id=1, source_target_pairs={{128,0},{130,2},{132,4},{134,6},{136,8},{138,10},{140,12},{142,14}... | collective-permute-start | bytes 20 | tf_op jit(solution)/shard_map/ppermute | solution.py:74
  31.6 5.9 %collective-permute-start.8 = (s32[1]{0:T(128)}, s32[1]{0:T(128)}, u32[]{:S(2)}, u32[]{:S(2)}) collective-permute-start(s32[1]{0:T(128)} %param.13), channel_id=1, source_target_pairs={{192,0},{194,2},{196,4},{198,6},{200,8},{202,10},{204,12},{206,14}... | collective-permute-start | bytes 20 | tf_op jit(solution)/shard_map/ppermute | solution.py:74
  34.5 22.9 %collective-permute-start.17 = (bf16[1,9,128,128]{3,2,1,0:T(8,128)(2,1)S(1)}, bf16[1,9,128,128]{3,2,1,0:T(8,128)(2,1)S(1)}, u32[]{:S(2)}, u32[]{:S(2)}) collective-permute-start(bf16[1,9,128,128]{3,2,1,0:T(8,128)(2,1)S(1)} %copy-done.1), channel_id=1, source_target_pairs={{0,1},{1,0},{2,3},{3,2},{4,5},{5,4},{6,7},{7,6},{8,9},{9,8},{10,11... | collective-permute-start | bytes 884744 | tf_op jit(solution)/shard_map/ppermute | solution.py:220
  37.6 6.5 %collective-permute-start.18 = (bf16[1,128]{1,0:T(2,128)(2,1)S(1)}, bf16[1,128]{1,0:T(2,128)(2,1)S(1)}, u32[]{:S(2)}, u32[]{:S(2)}) collective-permute-start(bf16[1,128]{1,0:T(2,128)(2,1)S(1)} %copy-done.6), channel_id=1, source_target_pairs={{0,1},{1,0},{2,3},{3,2},{4,5},{5,4},{6,7},{7,6},{8,9},{9,8},{10,11... | collective-permute-start | bytes 776 | tf_op jit(solution)/shard_map/ppermute | solution.py:221
  39.7 10.8 %collective-permute-start.5 = (f32[2,32,4,256]{3,2,1,0:T(4,128)S(1)}, f32[2,32,4,256]{3,2,1,0:T(4,128)S(1)}, u32[]{:S(2)}, u32[]{:S(2)}) collective-permute-start(f32[2,32,4,256]{3,2,1,0:T(4,128)S(1)} %add_add_fusion.1), channel_id=1, source_target_pairs={{0,4},{2,6},{4,0},{6,2},{8,12},{10,14},{12,8},{14,10},{16,20},{18,... | collective-permute-start | bytes 786440 | tf_op jit(solution)/shard_map/ppermute | solution.py:58
  42.0 13.5 %collective-permute-start.4 = (f32[2,32,4,256]{3,2,1,0:T(4,128)S(1)}, f32[2,32,4,256]{3,2,1,0:T(4,128)S(1)}, u32[]{:S(2)}, u32[]{:S(2)}) collective-permute-start(f32[2,32,4,256]{3,2,1,0:T(4,128)S(1)} %add_add_fusion.1), channel_id=1, source_target_pairs={{0,6},{2,0},{4,2},{6,4},{8,14},{10,8},{12,10},{14,12},{16,22},{18,... | collective-permute-start | bytes 786440 | tf_op jit(solution)/shard_map/ppermute | solution.py:58
  43.4 12.4 %collective-permute-start.3 = (f32[2,32,4,256]{3,2,1,0:T(4,128)S(1)}, f32[2,32,4,256]{3,2,1,0:T(4,128)S(1)}, u32[]{:S(2)}, u32[]{:S(2)}) collective-permute-start(f32[2,32,4,256]{3,2,1,0:T(4,128)S(1)} %add_add_fusion.1), channel_id=1, source_target_pairs={{0,2},{2,4},{4,6},{6,0},{8,10},{10,12},{12,14},{14,8},{16,18},{18,... | collective-permute-start | bytes 786440 | tf_op jit(solution)/shard_map/ppermute | solution.py:58
  56.4 5.2 %collective-permute-start.13 = (f32[2,4,4,256]{3,2,0,1:T(4,128)S(1)}, f32[2,4,4,256]{3,2,0,1:T(4,128)S(1)}, u32[]{:S(2)}, u32[]{:S(2)}) collective-permute-start(f32[2,4,4,256]{3,2,0,1:T(4,128)S(1)} %bitcast.68), channel_id=1, source_target_pairs={{0,32},{2,34},{4,36},{6,38},{8,40},{10,42},{12,44},{14,46},{16,48}... | collective-permute-start | bytes 98312 | tf_op jit(solution)/shard_map/ppermute | solution.py:82
  61.6 9.1 %collective-permute-start.14 = (f32[2,4,256]{2,1,0:T(4,128)S(1)}, f32[2,4,256]{2,1,0:T(4,128)S(1)}, u32[]{:S(2)}, u32[]{:S(2)}) collective-permute-start(f32[2,4,256]{2,1,0:T(4,128)S(1)} %get-tuple-element.7), channel_id=1, source_target_pairs={{0,64},{2,66},{4,68},{6,70},{8,72},{10,74},{12,76},{14,78},{16,80}... | collective-permute-start | bytes 24584 | tf_op jit(solution)/shard_map/ppermute | solution.py:84
  61.9 8.9 %collective-permute-start.15 = (f32[2,4,256]{2,1,0:T(4,128)S(1)}, f32[2,4,256]{2,1,0:T(4,128)S(1)}, u32[]{:S(2)}, u32[]{:S(2)}) collective-permute-start(f32[2,4,256]{2,1,0:T(4,128)S(1)} %get-tuple-element.9), channel_id=1, source_target_pairs={{0,128},{2,130},{4,132},{6,134},{8,136},{10,138},{12,140},{14,142}... | collective-permute-start | bytes 24584 | tf_op jit(solution)/shard_map/ppermute | solution.py:84
  65.8 5.4 %collective-permute-start.16 = (f32[2,4,256]{2,1,0:T(4,128)S(1)}, f32[2,4,256]{2,1,0:T(4,128)S(1)}, u32[]{:S(2)}, u32[]{:S(2)}) collective-permute-start(f32[2,4,256]{2,1,0:T(4,128)S(1)} %get-tuple-element.8), channel_id=1, source_target_pairs={{0,192},{2,194},{4,196},{6,198},{8,200},{10,202},{12,204},{14,206}... | collective-permute-start | bytes 24584 | tf_op jit(solution)/shard_map/ppermute | solution.py:84

commit v12 on v11

--- a/solution.py
+++ b/solution.py
@@ -70,13 +70,15 @@
     if size_z < 4 or size_z % 2:
         block = broadcast_sum(kept, rings)
         return lax.dynamic_index_in_dim(block, tile, 1, keepdims=False)
+    block = broadcast_sum(kept, rings[:1])
+    later, block = lax.optimization_barrier((tile, block))
     known = {
-        d: lax.ppermute(tile[None], "member", reversed_pairs(shifts_z[d]))[0]
+        d: lax.ppermute(later[None], "member", reversed_pairs(shifts_z[d]))[0]
         for d in range(1, size_z)
     }
     known[0] = tile
     evens = range(0, size_z, 2)
-    block = broadcast_sum(kept, rings[:-1])
+    block = broadcast_sum(block, rings[1:-1])
     sent = jnp.take(block, jnp.stack([known[1 + e] for e in evens]), axis=1, mode="clip")
     block = jnp.take(block, jnp.stack([known[e] for e in evens]), axis=1, mode="clip")
     block = block + lax.ppermute(sent, "member", shifts_z[1])

time: 97.8 us -> 98.9 us (1.011)
  the two profiles are of different devices: /device:TPU:8 before, /device:TPU:32 now
where the time goes in v12:
time: 98.9 us; the launch traced here: 97.7 us
  starting transfers between devices  35.2 us (36%)
  Pallas kernels  23.5 us (24%)
  waiting for transfers between devices  22.6 us (23%)
  other arithmetic  8.88 us (9%)
  local copies, waits for them, and re-layouts  6.74 us (7%)
    pallas_call x1, Pallas kernels, run_chain(): pl.pallas_call(chain_kernel, out_shape=jax.ShapeDtypeStruct(state.shape,...  23.5 us
    ppermute x7, starting transfers between devices, broadcast_mean(): lax.ppermute(later[None], 'member', reversed_pairs(shifts_z[d]))[0]  15.1 us
    ppermute x7, waiting for transfers between devices, broadcast_mean(): lax.ppermute(later[None], 'member', reversed_pairs(shifts_z[d]))[0]  13.3 us
    ppermute x6, starting transfers between devices, broadcast_sum(): arrived = [lax.ppermute(block, 'member', shifts[d]) for d in stage]  10.6 us
    ppermute x3, starting transfers between devices, broadcast_mean(): lax.ppermute(block[:, slot], 'member', shifts_z[e])  6.95 us
    ppermute x6, waiting for transfers between devices, broadcast_sum(): arrived = [lax.ppermute(block, 'member', shifts[d]) for d in stage]  5.39 us
    ppermute x3, waiting for transfers between devices, broadcast_mean(): lax.ppermute(block[:, slot], 'member', shifts_z[e])  2.63 us
    another operation x1, other arithmetic, broadcast_mean(): jnp.stack([known[1 + e] for e in evens])  2.59 us
  transfers between devices with their start and end apart: 19, of which 8 were waited for; matrix products, arithmetic and copies ran while one was open for 11% of the time, Pallas kernels for 0%

profile of v12, /device:TPU:32, one launch (start us, length us, event | category | flops | bytes accessed | tf_op | source)
XLA Modules:
  0.0 97.7 jit_solution(3094191147734945654)
XLA Ops:
  0.0 0.8 dynamic-slice_compare_fusion
  0.8 1.1 %bitcast_select_fusion = f32[2,32,4,256]{3,2,1,0:T(4,128)S(1)} fusion(f32[1,4,32,4,256]{4,3,2,1,0:T(4,128)} %param.11, s32[]{:T(128)S(6)} %select_n.37, pred[2]{0:T(512)(128)(4,1)S(1)} %dynamic-slice_compare_fusion), kind=kLoop, calls=%fused_computation.5 | loop fusion | flops 65536 | bytes 524294 | tf_op jit(solution)/shard_map/jit(_where)/select_n | solution.py:240
  1.9 1.6 %collective-permute-start = (f32[2,32,4,256]{3,2,1,0:T(4,128)S(1)}, f32[2,32,4,256]{3,2,1,0:T(4,128)S(1)}, u32[]{:S(2)}, u32[]{:S(2)}) collective-permute-start(f32[2,32,4,256]{3,2,1,0:T(4,128)S(1)} %bitcast_select_fusion), channel_id=1, source_target_pairs={{0,8},{2,10},{4,12},{6,14},{8,16},{10,18},{12,20},{14,22},{16,24},... | collective-permute-start | bytes 786440 | tf_op jit(solution)/shard_map/ppermute | solution.py:58
  3.4 1.7 %collective-permute-start.1 = (f32[2,32,4,256]{3,2,1,0:T(4,128)S(1)}, f32[2,32,4,256]{3,2,1,0:T(4,128)S(1)}, u32[]{:S(2)}, u32[]{:S(2)}) collective-permute-start(f32[2,32,4,256]{3,2,1,0:T(4,128)S(1)} %bitcast_select_fusion), channel_id=1, source_target_pairs={{0,24},{2,26},{4,28},{6,30},{8,0},{10,2},{12,4},{14,6},{16,8},{18,... | collective-permute-start | bytes 786440 | tf_op jit(solution)/shard_map/ppermute | solution.py:58
  5.2 1.8 %collective-permute-start.2 = (f32[2,32,4,256]{3,2,1,0:T(4,128)S(1)}, f32[2,32,4,256]{3,2,1,0:T(4,128)S(1)}, u32[]{:S(2)}, u32[]{:S(2)}) collective-permute-start(f32[2,32,4,256]{3,2,1,0:T(4,128)S(1)} %bitcast_select_fusion), channel_id=1, source_target_pairs={{0,16},{2,18},{4,20},{6,22},{8,24},{10,26},{12,28},{14,30},{16,0},... | collective-permute-start | bytes 786440 | tf_op jit(solution)/shard_map/ppermute | solution.py:58
  7.0 0.5 collective-permute-start.18
  8.3 0.1 copy.11
  8.4 0.6 reshape.20.coef_ref
  9.1 0.1 copy.12
  9.2 0.5 copy-done.5
  9.7 0.1 copy.14
  9.8 0.7 pad.16.state_ref
  10.5 0.6 pad.19.out_ref
  11.2 0.6 pad.18.lift_ref
  11.9 0.6 maximum_convert_fusion.gain_ref
  12.4 3.7 %collective-permute-done.1 = f32[2,32,4,256]{3,2,1,0:T(4,128)S(1)} collective-permute-done((f32[2,32,4,256]{3,2,1,0:T(4,128)S(1)}, f32[2,32,4,256]{3,2,1,0:T(4,128)S(1)}, u32[]{:S(2)}, u32[]{:S(2)}) %collective-permute-start.1) | collective-permute-done | bytes 262176 | tf_op jit(solution)/shard_map/ppermute | solution.py:58
  16.1 1.7 %collective-permute-done.2 = f32[2,32,4,256]{3,2,1,0:T(4,128)S(1)} collective-permute-done((f32[2,32,4,256]{3,2,1,0:T(4,128)S(1)}, f32[2,32,4,256]{3,2,1,0:T(4,128)S(1)}, u32[]{:S(2)}, u32[]{:S(2)}) %collective-permute-start.2) | collective-permute-done | bytes 262176 | tf_op jit(solution)/shard_map/ppermute | solution.py:58
  17.8 0.2 add_add_fusion.1
  18.0 5.5 %collective-permute-start.6 = (s32[1]{0:T(128)}, s32[1]{0:T(128)}, u32[]{:S(2)}, u32[]{:S(2)}) collective-permute-start(s32[1]{0:T(128)} %bitcast.2), channel_id=1, source_target_pairs={{64,0},{66,2},{68,4},{70,6},{72,8},{74,10},{76,12},{78,14},{80,16}... | collective-permute-start | bytes 20 | tf_op jit(solution)/shard_map/ppermute | solution.py:76
  23.5 1.4 %collective-permute-start.7 = (s32[1]{0:T(128)}, s32[1]{0:T(128)}, u32[]{:S(2)}, u32[]{:S(2)}) collective-permute-start(s32[1]{0:T(128)} %bitcast.2), channel_id=1, source_target_pairs={{128,0},{130,2},{132,4},{134,6},{136,8},{138,10},{140,12},{142,14}... | collective-permute-start | bytes 20 | tf_op jit(solution)/shard_map/ppermute | solution.py:76
  24.9 2.4 %collective-permute-start.8 = (s32[1]{0:T(128)}, s32[1]{0:T(128)}, u32[]{:S(2)}, u32[]{:S(2)}) collective-permute-start(s32[1]{0:T(128)} %bitcast.2), channel_id=1, source_target_pairs={{192,0},{194,2},{196,4},{198,6},{200,8},{202,10},{204,12},{206,14}... | collective-permute-start | bytes 20 | tf_op jit(solution)/shard_map/ppermute | solution.py:76
  27.3 3.2 %collective-permute-start.5 = (f32[2,32,4,256]{3,2,1,0:T(4,128)S(1)}, f32[2,32,4,256]{3,2,1,0:T(4,128)S(1)}, u32[]{:S(2)}, u32[]{:S(2)}) collective-permute-start(f32[2,32,4,256]{3,2,1,0:T(4,128)S(1)} %add_add_fusion.1), channel_id=1, source_target_pairs={{0,4},{2,6},{4,0},{6,2},{8,12},{10,14},{12,8},{14,10},{16,20},{18,... | collective-permute-start | bytes 786440 | tf_op jit(solution)/shard_map/ppermute | solution.py:58
  30.5 1.1 %collective-permute-start.4 = (f32[2,32,4,256]{3,2,1,0:T(4,128)S(1)}, f32[2,32,4,256]{3,2,1,0:T(4,128)S(1)}, u32[]{:S(2)}, u32[]{:S(2)}) collective-permute-start(f32[2,32,4,256]{3,2,1,0:T(4,128)S(1)} %add_add_fusion.1), channel_id=1, source_target_pairs={{0,6},{2,0},{4,2},{6,4},{8,14},{10,8},{12,10},{14,12},{16,22},{18,... | collective-permute-start | bytes 786440 | tf_op jit(solution)/shard_map/ppermute | solution.py:58
  31.6 1.2 %collective-permute-start.3 = (f32[2,32,4,256]{3,2,1,0:T(4,128)S(1)}, f32[2,32,4,256]{3,2,1,0:T(4,128)S(1)}, u32[]{:S(2)}, u32[]{:S(2)}) collective-permute-start(f32[2,32,4,256]{3,2,1,0:T(4,128)S(1)} %add_add_fusion.1), channel_id=1, source_target_pairs={{0,2},{2,4},{4,6},{6,0},{8,10},{10,12},{12,14},{14,8},{16,18},{18,... | collective-permute-start | bytes 786440 | tf_op jit(solution)/shard_map/ppermute | solution.py:58
  32.8 1.9 %collective-permute-start.10 = (s32[1]{0:T(128)}, s32[1]{0:T(128)}, u32[]{:S(2)}, u32[]{:S(2)}) collective-permute-start(s32[1]{0:T(128)} %bitcast.2), channel_id=1, source_target_pairs={{96,0},{98,2},{100,4},{102,6},{104,8},{106,10},{108,12},{110,14},{... | collective-permute-start | bytes 20 | tf_op jit(solution)/shard_map/ppermute | solution.py:76
  34.7 1.9 %pad_add_fusion = s32[4]{0:T(128)S(1)} fusion(s32[1]{0:T(128)} %collective-permute-done.8, s32[1]{0:T(128)} %collective-permute-done.7, s32[1]{0:T(128)} %collective-permute-done.6, s32[1]{0:T(128)S(6)} %copy.16), kind=kLoop, calls=%fused_computation.24 | loop fusion | flops 12 | bytes 32 | tf_op jit(solution)/shard_map/stack | solution.py:83
  36.6 2.9 %collective-permute-done.10 = s32[1]{0:T(128)} collective-permute-done((s32[1]{0:T(128)}, s32[1]{0:T(128)}, u32[]{:S(2)}, u32[]{:S(2)}) %collective-permute-start.10) | collective-permute-done | bytes 36 | tf_op jit(solution)/shard_map/ppermute | solution.py:76
  39.4 0.9 collective-permute-start.11
  40.3 5.9 %collective-permute-done.11 = s32[1]{0:T(128)} collective-permute-done((s32[1]{0:T(128)}, s32[1]{0:T(128)}, u32[]{:S(2)}, u32[]{:S(2)}) %collective-permute-start.11) | collective-permute-done | bytes 36 | tf_op jit(solution)/shard_map/ppermute | solution.py:76
  46.3 2.0 %collective-permute-start.12 = (s32[1]{0:T(128)}, s32[1]{0:T(128)}, u32[]{:S(2)}, u32[]{:S(2)}) collective-permute-start(s32[1]{0:T(128)} %bitcast.2), channel_id=1, source_target_pairs={{224,0},{226,2},{228,4},{230,6},{232,8},{234,10},{236,12},{238,14}... | collective-permute-start | bytes 20 | tf_op jit(solution)/shard_map/ppermute | solution.py:76
  48.2 1.8 %collective-permute-done.12 = s32[1]{0:T(128)} collective-permute-done((s32[1]{0:T(128)}, s32[1]{0:T(128)}, u32[]{:S(2)}, u32[]{:S(2)}) %collective-permute-start.12) | collective-permute-done | bytes 36 | tf_op jit(solution)/shard_map/ppermute | solution.py:76
  50.1 1.0 %collective-permute-start.9 = (s32[1]{0:T(128)}, s32[1]{0:T(128)}, u32[]{:S(2)}, u32[]{:S(2)}) collective-permute-start(s32[1]{0:T(128)} %bitcast.2), channel_id=1, source_target_pairs={{32,0},{34,2},{36,4},{38,6},{40,8},{42,10},{44,12},{46,14},{48,16}... | collective-permute-start | bytes 20 | tf_op jit(solution)/shard_map/ppermute | solution.py:76
  51.1 2.6 %collective-permute-done.9 = s32[1]{0:T(128)} collective-permute-done((s32[1]{0:T(128)}, s32[1]{0:T(128)}, u32[]{:S(2)}, u32[]{:S(2)}) %collective-permute-start.9) | collective-permute-done | bytes 36 | tf_op jit(solution)/shard_map/ppermute | solution.py:76
  53.7 2.6 %pad_add_fusion.1 = s32[4]{0:T(128)S(1)} fusion(s32[1]{0:T(128)} %collective-permute-done.12, s32[1]{0:T(128)} %collective-permute-done.11, s32[1]{0:T(128)} %collective-permute-done.10, s32[1]{0:T(128)} %collective-permute-done.9), kind=kLoop, calls=%fused_computation.25 | loop fusion | flops 12 | bytes 32 | tf_op jit(solution)/shard_map/stack | solution.py:82
  56.4 0.6 gather_fusion.1
  57.0 2.1 %collective-permute-start.13 = (f32[2,4,4,256]{3,2,0,1:T(4,128)S(1)}, f32[2,4,4,256]{3,2,0,1:T(4,128)S(1)}, u32[]{:S(2)}, u32[]{:S(2)}) collective-permute-start(f32[2,4,4,256]{3,2,0,1:T(4,128)S(1)} %bitcast.70), channel_id=1, source_target_pairs={{0,32},{2,34},{4,36},{6,38},{8,40},{10,42},{12,44},{14,46},{16,48}... | collective-permute-start | bytes 98312 | tf_op jit(solution)/shard_map/ppermute | solution.py:84
  59.1 0.6 gather_fusion
  59.7 1.3 %collective-permute-done.13 = f32[2,4,4,256]{3,2,0,1:T(4,128)S(1)} collective-permute-done((f32[2,4,4,256]{3,2,0,1:T(4,128)S(1)}, f32[2,4,4,256]{3,2,0,1:T(4,128)S(1)}, u32[]{:S(2)}, u32[]{:S(2)}) %collective-permute-start.13) | collective-permute-done | bytes 32800 | tf_op jit(solution)/shard_map/ppermute | solution.py:84
  61.0 2.9 %collective-permute-start.14 = (f32[2,4,256]{2,1,0:T(4,128)S(1)}, f32[2,4,256]{2,1,0:T(4,128)S(1)}, u32[]{:S(2)}, u32[]{:S(2)}) collective-permute-start(f32[2,4,256]{2,1,0:T(4,128)S(1)} %get-tuple-element.11), channel_id=1, source_target_pairs={{0,64},{2,66},{4,68},{6,70},{8,72},{10,74},{12,76},{14,78},{16,80}... | collective-permute-start | bytes 24584 | tf_op jit(solution)/shard_map/ppermute | solution.py:86
  63.9 1.6 %collective-permute-start.15 = (f32[2,4,256]{2,1,0:T(4,128)S(1)}, f32[2,4,256]{2,1,0:T(4,128)S(1)}, u32[]{:S(2)}, u32[]{:S(2)}) collective-permute-start(f32[2,4,256]{2,1,0:T(4,128)S(1)} %get-tuple-element.13), channel_id=1, source_target_pairs={{0,128},{2,130},{4,132},{6,134},{8,136},{10,138},{12,140},{14,142}... | collective-permute-start | bytes 24584 | tf_op jit(solution)/shard_map/ppermute | solution.py:86
  65.5 2.5 %collective-permute-start.16 = (f32[2,4,256]{2,1,0:T(4,128)S(1)}, f32[2,4,256]{2,1,0:T(4,128)S(1)}, u32[]{:S(2)}, u32[]{:S(2)}) collective-permute-start(f32[2,4,256]{2,1,0:T(4,128)S(1)} %get-tuple-element.12), channel_id=1, source_target_pairs={{0,192},{2,194},{4,196},{6,198},{8,200},{10,202},{12,204},{14,206}... | collective-permute-start | bytes 24584 | tf_op jit(solution)/shard_map/ppermute | solution.py:86
  68.0 0.9 pad_maximum_fusion.conv_ref
  68.9 2.6 %collective-permute-done.15 = f32[2,4,256]{2,1,0:T(4,128)S(1)} collective-permute-done((f32[2,4,256]{2,1,0:T(4,128)S(1)}, f32[2,4,256]{2,1,0:T(4,128)S(1)}, u32[]{:S(2)}, u32[]{:S(2)}) %collective-permute-start.15) | collective-permute-done | bytes 8224 | tf_op jit(solution)/shard_map/ppermute | solution.py:86
  71.5 0.1 copy.13
  71.7 0.9 pad.17.means_ref
  72.5 23.5 %shard_map.100 = f32[512,128]{1,0:T(8,128)} custom-call(f32[40]{0:T(128)} %reshape.20.coef_ref, f32[512,128]{1,0:T(8,128)} %pad.16.state_ref, f32[512,128]{1,0:T(8,128)} %pad.17.means_ref, f32[128,128]{1,0:T(8,128)} %pad.18.lift_ref, f32[1,128]{1,0:T(1,128)} %bitcast.72, bf16[2,1152,128]{2,1,0:T(8,128)(2,1)} %pad_maximum_fusion.conv_ref, ...), custom_call_target="tpu_custom_call" | custom-call | tf_op jit(solution)/shard_map/pallas_call | solution.py:169
  96.0 1.1 %copy.15 = f32[2,256,4]{1,2,0:T(4,128)S(1)} copy(f32[2,256,4]{2,1,0:T(8,128)} %bitcast.63) | data formatting | bytes 16384 | tf_op jit(solution)/shard_map/reshape | solution.py:257
  97.1 0.6 fusion.3
  (36 shorter events, 0.4 us)
Async XLA Ops:
  0.0 7.0 %copy-start.1 = (bf16[1,9,128,128]{3,2,1,0:T(8,128)(2,1)S(1)}, bf16[1,9,128,128]{3,2,1,0:T(8,128)(2,1)}, u32[]{:S(2)}) copy-start(bf16[1,9,128,128]{3,2,1,0:T(8,128)(2,1)} %param.17) | copy-start | bytes 884740
  0.8 6.2 %copy-start.6 = (bf16[1,128]{1,0:T(2,128)(2,1)S(1)}, bf16[1,128]{1,0:T(2,128)(2,1)}, u32[]{:S(2)}) copy-start(bf16[1,128]{1,0:T(2,128)(2,1)} %param.18) | copy-start | bytes 772
  1.9 10.6 %collective-permute-start = (f32[2,32,4,256]{3,2,1,0:T(4,128)S(1)}, f32[2,32,4,256]{3,2,1,0:T(4,128)S(1)}, u32[]{:S(2)}, u32[]{:S(2)}) collective-permute-start(f32[2,32,4,256]{3,2,1,0:T(4,128)S(1)} %bitcast_select_fusion), channel_id=1, source_target_pairs={{0,8},{2,10},{4,12},{6,14},{8,16},{10,18},{12,20},{14,22},{16,24},... | collective-permute-start | bytes 786440 | tf_op jit(solution)/shard_map/ppermute | solution.py:58
  3.4 12.7 %collective-permute-start.1 = (f32[2,32,4,256]{3,2,1,0:T(4,128)S(1)}, f32[2,32,4,256]{3,2,1,0:T(4,128)S(1)}, u32[]{:S(2)}, u32[]{:S(2)}) collective-permute-start(f32[2,32,4,256]{3,2,1,0:T(4,128)S(1)} %bitcast_select_fusion), channel_id=1, source_target_pairs={{0,24},{2,26},{4,28},{6,30},{8,0},{10,2},{12,4},{14,6},{16,8},{18,... | collective-permute-start | bytes 786440 | tf_op jit(solution)/shard_map/ppermute | solution.py:58
  5.2 12.6 %collective-permute-start.2 = (f32[2,32,4,256]{3,2,1,0:T(4,128)S(1)}, f32[2,32,4,256]{3,2,1,0:T(4,128)S(1)}, u32[]{:S(2)}, u32[]{:S(2)}) collective-permute-start(f32[2,32,4,256]{3,2,1,0:T(4,128)S(1)} %bitcast_select_fusion), channel_id=1, source_target_pairs={{0,16},{2,18},{4,20},{6,22},{8,24},{10,26},{12,28},{14,30},{16,0},... | collective-permute-start | bytes 786440 | tf_op jit(solution)/shard_map/ppermute | solution.py:58
  7.0 52.1 %collective-permute-start.17 = (bf16[1,9,128,128]{3,2,1,0:T(8,128)(2,1)S(1)}, bf16[1,9,128,128]{3,2,1,0:T(8,128)(2,1)S(1)}, u32[]{:S(2)}, u32[]{:S(2)}) collective-permute-start(bf16[1,9,128,128]{3,2,1,0:T(8,128)(2,1)S(1)} %copy-done.1), channel_id=1, source_target_pairs={{0,1},{1,0},{2,3},{3,2},{4,5},{5,4},{6,7},{7,6},{8,9},{9,8},{10,11... | collective-permute-start | bytes 884744 | tf_op jit(solution)/shard_map/ppermute | solution.py:222
  7.0 4.8 %collective-permute-start.18 = (bf16[1,128]{1,0:T(2,128)(2,1)S(1)}, bf16[1,128]{1,0:T(2,128)(2,1)S(1)}, u32[]{:S(2)}, u32[]{:S(2)}) collective-permute-start(bf16[1,128]{1,0:T(2,128)(2,1)S(1)} %copy-done.6), channel_id=1, source_target_pairs={{0,1},{1,0},{2,3},{3,2},{4,5},{5,4},{6,7},{7,6},{8,9},{9,8},{10,11... | collective-permute-start | bytes 776 | tf_op jit(solution)/shard_map/ppermute | solution.py:223
  7.5 0.7 copy-start.2
  8.3 0.7 copy-start.4
  9.0 0.7 copy-start.5
  9.1 8.7 %copy-start = (f32[1,4,32,4,256]{4,3,2,1,0:T(4,128)S(1)}, f32[1,4,32,4,256]{4,3,2,1,0:T(4,128)}, u32[]{:S(2)}) copy-start(f32[1,4,32,4,256]{4,3,2,1,0:T(4,128)} %param.11) | copy-start | bytes 1572868
  10.5 0.7 copy-start.3
  18.0 12.5 %collective-permute-start.6 = (s32[1]{0:T(128)}, s32[1]{0:T(128)}, u32[]{:S(2)}, u32[]{:S(2)}) collective-permute-start(s32[1]{0:T(128)} %bitcast.2), channel_id=1, source_target_pairs={{64,0},{66,2},{68,4},{70,6},{72,8},{74,10},{76,12},{78,14},{80,16}... | collective-permute-start | bytes 20 | tf_op jit(solution)/shard_map/ppermute | solution.py:76
  23.5 8.1 %collective-permute-start.7 = (s32[1]{0:T(128)}, s32[1]{0:T(128)}, u32[]{:S(2)}, u32[]{:S(2)}) collective-permute-start(s32[1]{0:T(128)} %bitcast.2), channel_id=1, source_target_pairs={{128,0},{130,2},{132,4},{134,6},{136,8},{138,10},{140,12},{142,14}... | collective-permute-start | bytes 20 | tf_op jit(solution)/shard_map/ppermute | solution.py:76
  24.9 7.9 %collective-permute-start.8 = (s32[1]{0:T(128)}, s32[1]{0:T(128)}, u32[]{:S(2)}, u32[]{:S(2)}) collective-permute-start(s32[1]{0:T(128)} %bitcast.2), channel_id=1, source_target_pairs={{192,0},{194,2},{196,4},{198,6},{200,8},{202,10},{204,12},{206,14}... | collective-permute-start | bytes 20 | tf_op jit(solution)/shard_map/ppermute | solution.py:76
  27.3 29.0 %collective-permute-start.5 = (f32[2,32,4,256]{3,2,1,0:T(4,128)S(1)}, f32[2,32,4,256]{3,2,1,0:T(4,128)S(1)}, u32[]{:S(2)}, u32[]{:S(2)}) collective-permute-start(f32[2,32,4,256]{3,2,1,0:T(4,128)S(1)} %add_add_fusion.1), channel_id=1, source_target_pairs={{0,4},{2,6},{4,0},{6,2},{8,12},{10,14},{12,8},{14,10},{16,20},{18,... | collective-permute-start | bytes 786440 | tf_op jit(solution)/shard_map/ppermute | solution.py:58
  30.5 25.9 %collective-permute-start.4 = (f32[2,32,4,256]{3,2,1,0:T(4,128)S(1)}, f32[2,32,4,256]{3,2,1,0:T(4,128)S(1)}, u32[]{:S(2)}, u32[]{:S(2)}) collective-permute-start(f32[2,32,4,256]{3,2,1,0:T(4,128)S(1)} %add_add_fusion.1), channel_id=1, source_target_pairs={{0,6},{2,0},{4,2},{6,4},{8,14},{10,8},{12,10},{14,12},{16,22},{18,... | collective-permute-start | bytes 786440 | tf_op jit(solution)/shard_map/ppermute | solution.py:58
  31.6 24.8 %collective-permute-start.3 = (f32[2,32,4,256]{3,2,1,0:T(4,128)S(1)}, f32[2,32,4,256]{3,2,1,0:T(4,128)S(1)}, u32[]{:S(2)}, u32[]{:S(2)}) collective-permute-start(f32[2,32,4,256]{3,2,1,0:T(4,128)S(1)} %add_add_fusion.1), channel_id=1, source_target_pairs={{0,2},{2,4},{4,6},{6,0},{8,10},{10,12},{12,14},{14,8},{16,18},{18,... | collective-permute-start | bytes 786440 | tf_op jit(solution)/shard_map/ppermute | solution.py:58
  32.8 6.7 %collective-permute-start.10 = (s32[1]{0:T(128)}, s32[1]{0:T(128)}, u32[]{:S(2)}, u32[]{:S(2)}) collective-permute-start(s32[1]{0:T(128)} %bitcast.2), channel_id=1, source_target_pairs={{96,0},{98,2},{100,4},{102,6},{104,8},{106,10},{108,12},{110,14},{... | collective-permute-start | bytes 20 | tf_op jit(solution)/shard_map/ppermute | solution.py:76
  39.4 6.8 %collective-permute-start.11 = (s32[1]{0:T(128)}, s32[1]{0:T(128)}, u32[]{:S(2)}, u32[]{:S(2)}) collective-permute-start(s32[1]{0:T(128)} %bitcast.2), channel_id=1, source_target_pairs={{160,0},{162,2},{164,4},{166,6},{168,8},{170,10},{172,12},{174,14}... | collective-permute-start | bytes 20 | tf_op jit(solution)/shard_map/ppermute | solution.py:76
  46.3 3.8 %collective-permute-start.12 = (s32[1]{0:T(128)}, s32[1]{0:T(128)}, u32[]{:S(2)}, u32[]{:S(2)}) collective-permute-start(s32[1]{0:T(128)} %bitcast.2), channel_id=1, source_target_pairs={{224,0},{226,2},{228,4},{230,6},{232,8},{234,10},{236,12},{238,14}... | collective-permute-start | bytes 20 | tf_op jit(solution)/shard_map/ppermute | solution.py:76
  50.1 3.7 %collective-permute-start.9 = (s32[1]{0:T(128)}, s32[1]{0:T(128)}, u32[]{:S(2)}, u32[]{:S(2)}) collective-permute-start(s32[1]{0:T(128)} %bitcast.2), channel_id=1, source_target_pairs={{32,0},{34,2},{36,4},{38,6},{40,8},{42,10},{44,12},{46,14},{48,16}... | collective-permute-start | bytes 20 | tf_op jit(solution)/shard_map/ppermute | solution.py:76
  57.0 4.0 %collective-permute-start.13 = (f32[2,4,4,256]{3,2,0,1:T(4,128)S(1)}, f32[2,4,4,256]{3,2,0,1:T(4,128)S(1)}, u32[]{:S(2)}, u32[]{:S(2)}) collective-permute-start(f32[2,4,4,256]{3,2,0,1:T(4,128)S(1)} %bitcast.70), channel_id=1, source_target_pairs={{0,32},{2,34},{4,36},{6,38},{8,40},{10,42},{12,44},{14,46},{16,48}... | collective-permute-start | bytes 98312 | tf_op jit(solution)/shard_map/ppermute | solution.py:84
  61.0 7.8 %collective-permute-start.14 = (f32[2,4,256]{2,1,0:T(4,128)S(1)}, f32[2,4,256]{2,1,0:T(4,128)S(1)}, u32[]{:S(2)}, u32[]{:S(2)}) collective-permute-start(f32[2,4,256]{2,1,0:T(4,128)S(1)} %get-tuple-element.11), channel_id=1, source_target_pairs={{0,64},{2,66},{4,68},{6,70},{8,72},{10,74},{12,76},{14,78},{16,80}... | collective-permute-start | bytes 24584 | tf_op jit(solution)/shard_map/ppermute | solution.py:86
  63.9 7.6 %collective-permute-start.15 = (f32[2,4,256]{2,1,0:T(4,128)S(1)}, f32[2,4,256]{2,1,0:T(4,128)S(1)}, u32[]{:S(2)}, u32[]{:S(2)}) collective-permute-start(f32[2,4,256]{2,1,0:T(4,128)S(1)} %get-tuple-element.13), channel_id=1, source_target_pairs={{0,128},{2,130},{4,132},{6,134},{8,136},{10,138},{12,140},{14,142}... | collective-permute-start | bytes 24584 | tf_op jit(solution)/shard_map/ppermute | solution.py:86
  65.5 6.0 %collective-permute-start.16 = (f32[2,4,256]{2,1,0:T(4,128)S(1)}, f32[2,4,256]{2,1,0:T(4,128)S(1)}, u32[]{:S(2)}, u32[]{:S(2)}) collective-permute-start(f32[2,4,256]{2,1,0:T(4,128)S(1)} %get-tuple-element.12), channel_id=1, source_target_pairs={{0,192},{2,194},{4,196},{6,198},{8,200},{10,202},{12,204},{14,206}... | collective-permute-start | bytes 24584 | tf_op jit(solution)/shard_map/ppermute | solution.py:86

commit v13 on v9

--- a/solution.py
+++ b/solution.py
@@ -216,8 +216,13 @@
         channels = section_conv.shape[-1]
 
         swap = [(0, 1), (1, 0)]
-        other_conv = lax.ppermute(section_conv, "segment", swap)
-        other_gain = lax.ppermute(section_gain, "segment", swap)
+        taps = section_conv.shape[1]
+        packed = jnp.concatenate(
+            [section_conv.reshape(1, taps * channels, channels), section_gain[:, None, :]], axis=1
+        )
+        other = lax.ppermute(packed, "segment", swap)
+        other_conv = other[:, : taps * channels].reshape(section_conv.shape)
+        other_gain = other[:, taps * channels]
         kernels = jnp.stack(
             [
                 jnp.where(is_first, section_conv[0], other_conv[0]),

time: 86.5 us -> 92.7 us (1.072)
  starting transfers between devices: 31.4 us -> 33.7 us
  waiting for transfers between devices: 13.6 us -> 15.8 us
  local copies, waits for them, and re-layouts: 7.45 us -> 8.62 us
    ppermute x3, starting transfers between devices: 10.1 us -> 13.7 us  [broadcast_mean(): lax.ppermute(tile[None], 'member', reversed_pairs(shifts_z[d]))[0]]
    ppermute x3, waiting for transfers between devices: 1.13 us -> 3.78 us  [broadcast_mean(): lax.ppermute(tile[None], 'member', reversed_pairs(shifts_z[d]))[0]]
    ppermute x6, waiting for transfers between devices: 3.89 us -> 6.42 us  [broadcast_sum(): arrived = [lax.ppermute(block, 'member', shifts[d]) for d in stage]]
    ppermute x3, waiting for transfers between devices: 3.13 us -> 0.8 us  [broadcast_mean(): lax.ppermute(lax.dynamic_index_in_dim(block, wanted[d], 1, keepdims=False...]
    ppermute x1, starting transfers between devices: 2.68 us -> 0.87 us  [broadcast_mean(): block = block + lax.ppermute(block, 'member', shifts_z[1])]
    unnamed x20, local copies, waits for them, and re-layouts: 2.4 us -> 3.64 us
    ppermute x3, starting transfers between devices: 8.03 us -> 9.24 us  [broadcast_mean(): lax.ppermute(lax.dynamic_index_in_dim(block, wanted[d], 1, keepdims=False...]
  transfers between devices with their start and end apart: 15 -> 14, of which waited for: 6 -> 7; matrix products, arithmetic and copies ran while one was open for 6% -> 5% of each run, Pallas kernels for 0% -> 0%
where the time goes in v13:
time: 92.7 us; the launch traced here: 90.9 us
  starting transfers between devices  33.7 us (36%)
  Pallas kernels  23.5 us (25%)
  waiting for transfers between devices  15.8 us (17%)
  local copies, waits for them, and re-layouts  8.62 us (9%)
  between operations  6.48 us (7%)
  other arithmetic  2.73 us (3%)
    pallas_call x1, Pallas kernels, run_chain(): pl.pallas_call(chain_kernel, out_shape=jax.ShapeDtypeStruct(state.shape,...  23.5 us
    ppermute x3, starting transfers between devices, broadcast_mean(): lax.ppermute(tile[None], 'member', reversed_pairs(shifts_z[d]))[0]  13.7 us
    ppermute x6, starting transfers between devices, broadcast_sum(): arrived = [lax.ppermute(block, 'member', shifts[d]) for d in stage]  9.83 us
    ppermute x3, starting transfers between devices, broadcast_mean(): lax.ppermute(lax.dynamic_index_in_dim(block, wanted[d], 1, keepdims=False...  9.24 us
    ppermute x6, waiting for transfers between devices, broadcast_sum(): arrived = [lax.ppermute(block, 'member', shifts[d]) for d in stage]  6.42 us
    ppermute x1, waiting for transfers between devices, broadcast_mean(): block = block + lax.ppermute(block, 'member', shifts_z[1])  4.76 us
    ppermute x3, waiting for transfers between devices, broadcast_mean(): lax.ppermute(tile[None], 'member', reversed_pairs(shifts_z[d]))[0]  3.78 us
    unnamed x20, local copies, waits for them, and re-layouts  3.64 us
  transfers between devices with their start and end apart: 14, of which 7 were waited for; matrix products, arithmetic and copies ran while one was open for 5% of the time, Pallas kernels for 0%

profile of v13, /device:TPU:32, one launch (start us, length us, event | category | flops | bytes accessed | tf_op | source)
XLA Modules:
  0.0 90.9 jit_solution(9046105702387484596)
XLA Ops:
  0.0 1.0 %copy-done = f32[1,4,32,4,256]{4,3,2,1,0:T(4,128)S(1)} copy-done((f32[1,4,32,4,256]{4,3,2,1,0:T(4,128)S(1)}, f32[1,4,32,4,256]{4,3,2,1,0:T(4,128)}, u32[]{:S(2)}) %copy-start) | copy-done | bytes 524312
  1.1 0.6 copy-done.7
  1.7 0.1 dynamic-slice_compare_fusion
  1.8 0.1 fusion
  1.9 2.8 %collective-permute-start.1 = (f32[2,32,4,256]{3,1,2,0:T(8,128)S(1)}, f32[2,32,4,256]{3,1,2,0:T(8,128)S(1)}, u32[]{:S(2)}, u32[]{:S(2)}) collective-permute-start(f32[2,32,4,256]{3,1,2,0:T(8,128)S(1)} %fusion), channel_id=1, source_target_pairs={{0,24},{2,26},{4,28},{6,30},{8,0},{10,2},{12,4},{14,6},{16,8},{18,... | collective-permute-start | bytes 786440 | tf_op jit(solution)/shard_map/ppermute | solution.py:58
  4.7 0.8 collective-permute-start.2
  5.5 0.9 collective-permute-start
  6.4 5.4 %collective-permute-start.7 = (s32[1]{0:T(128)}, s32[1]{0:T(128)}, u32[]{:S(2)}, u32[]{:S(2)}) collective-permute-start(s32[1]{0:T(128)} %param.13), channel_id=1, source_target_pairs={{64,0},{66,2},{68,4},{70,6},{72,8},{74,10},{76,12},{78,14},{80,16}... | collective-permute-start | bytes 20 | tf_op jit(solution)/shard_map/ppermute | solution.py:75
  11.8 0.7 copy-done.6
  12.5 0.1 collective-permute-start.13
  12.6 0.5 copy-done.2
  13.1 0.1 fusion.4
  13.2 2.7 %collective-permute-done.1 = f32[2,32,4,256]{3,1,2,0:T(8,128)S(1)} collective-permute-done((f32[2,32,4,256]{3,1,2,0:T(8,128)S(1)}, f32[2,32,4,256]{3,1,2,0:T(8,128)S(1)}, u32[]{:S(2)}, u32[]{:S(2)}) %collective-permute-start.1) | collective-permute-done | bytes 262176 | tf_op jit(solution)/shard_map/ppermute | solution.py:58
  15.9 3.7 %collective-permute-done = f32[2,32,4,256]{3,1,2,0:T(8,128)S(1)} collective-permute-done((f32[2,32,4,256]{3,1,2,0:T(8,128)S(1)}, f32[2,32,4,256]{3,1,2,0:T(8,128)S(1)}, u32[]{:S(2)}, u32[]{:S(2)}) %collective-permute-start) | collective-permute-done | bytes 262176 | tf_op jit(solution)/shard_map/ppermute | solution.py:58
  19.6 0.2 add_add_fusion.1
  19.8 3.3 %collective-permute-start.5 = (f32[2,32,4,256]{3,1,2,0:T(8,128)S(1)}, f32[2,32,4,256]{3,1,2,0:T(8,128)S(1)}, u32[]{:S(2)}, u32[]{:S(2)}) collective-permute-start(f32[2,32,4,256]{3,1,2,0:T(8,128)S(1)} %add_add_fusion.1), channel_id=1, source_target_pairs={{0,4},{2,6},{4,0},{6,2},{8,12},{10,14},{12,8},{14,10},{16,20},{18,... | collective-permute-start | bytes 786440 | tf_op jit(solution)/shard_map/ppermute | solution.py:58
  23.0 1.1 %collective-permute-start.4 = (f32[2,32,4,256]{3,1,2,0:T(8,128)S(1)}, f32[2,32,4,256]{3,1,2,0:T(8,128)S(1)}, u32[]{:S(2)}, u32[]{:S(2)}) collective-permute-start(f32[2,32,4,256]{3,1,2,0:T(8,128)S(1)} %add_add_fusion.1), channel_id=1, source_target_pairs={{0,6},{2,0},{4,2},{6,4},{8,14},{10,8},{12,10},{14,12},{16,22},{18,... | collective-permute-start | bytes 786440 | tf_op jit(solution)/shard_map/ppermute | solution.py:58
  24.1 1.0 %collective-permute-start.3 = (f32[2,32,4,256]{3,1,2,0:T(8,128)S(1)}, f32[2,32,4,256]{3,1,2,0:T(8,128)S(1)}, u32[]{:S(2)}, u32[]{:S(2)}) collective-permute-start(f32[2,32,4,256]{3,1,2,0:T(8,128)S(1)} %add_add_fusion.1), channel_id=1, source_target_pairs={{0,2},{2,4},{4,6},{6,0},{8,10},{10,12},{12,14},{14,8},{16,18},{18,... | collective-permute-start | bytes 786440 | tf_op jit(solution)/shard_map/ppermute | solution.py:58
  25.8 0.1 copy.17
  25.9 0.6 reshape.27.coef_ref
  26.5 0.1 copy-done.5
  26.6 0.1 copy.20
  26.7 0.6 copy-done.3
  27.2 0.6 pad.18.lift_ref
  27.9 0.6 pad.19.out_ref
  28.5 0.1 copy.18
  28.6 0.7 pad.16.state_ref
  29.4 0.0 collective-permute-done.7
  29.4 3.3 %collective-permute-start.11 = (s32[1]{0:T(128)}, s32[1]{0:T(128)}, u32[]{:S(2)}, u32[]{:S(2)}) collective-permute-start(s32[1]{0:T(128)} %param.13), channel_id=1, source_target_pairs={{192,0},{194,2},{196,4},{198,6},{200,8},{202,10},{204,12},{206,14}... | collective-permute-start | bytes 20 | tf_op jit(solution)/shard_map/ppermute | solution.py:75
  33.8 2.6 %collective-permute-done.11 = s32[1]{0:T(128)} collective-permute-done((s32[1]{0:T(128)}, s32[1]{0:T(128)}, u32[]{:S(2)}, u32[]{:S(2)}) %collective-permute-start.11) | collective-permute-done | bytes 36 | tf_op jit(solution)/shard_map/ppermute | solution.py:75
  36.4 5.0 %collective-permute-start.9 = (s32[1]{0:T(128)}, s32[1]{0:T(128)}, u32[]{:S(2)}, u32[]{:S(2)}) collective-permute-start(s32[1]{0:T(128)} %param.13), channel_id=1, source_target_pairs={{128,0},{130,2},{132,4},{134,6},{136,8},{138,10},{140,12},{142,14}... | collective-permute-start | bytes 20 | tf_op jit(solution)/shard_map/ppermute | solution.py:75
  42.8 1.2 %collective-permute-done.9 = s32[1]{0:T(128)} collective-permute-done((s32[1]{0:T(128)}, s32[1]{0:T(128)}, u32[]{:S(2)}, u32[]{:S(2)}) %collective-permute-start.9) | collective-permute-done | bytes 36 | tf_op jit(solution)/shard_map/ppermute | solution.py:75
  47.2 0.1 broadcast_select_fusion.1
  47.3 0.1 add_add_fusion
  47.4 0.9 collective-permute-start.6
  48.2 0.9 pad_maximum_fusion.conv_ref
  49.1 4.8 %collective-permute-done.6 = f32[2,32,4,256]{3,1,2,0:T(8,128)S(1)} collective-permute-done((f32[2,32,4,256]{3,1,2,0:T(8,128)S(1)}, f32[2,32,4,256]{3,1,2,0:T(8,128)S(1)}, u32[]{:S(2)}, u32[]{:S(2)}) %collective-permute-start.6) | collective-permute-done | bytes 262176 | tf_op jit(solution)/shard_map/ppermute | solution.py:78
  54.0 2.7 %collective-permute-start.8 = (f32[2,4,256]{2,1,0:T(4,128)S(1)}, f32[2,4,256]{2,1,0:T(4,128)S(1)}, u32[]{:S(2)}, u32[]{:S(2)}) collective-permute-start(f32[2,4,256]{2,1,0:T(4,128)S(1)} %bitcast.77), channel_id=1, source_target_pairs={{0,64},{2,66},{4,68},{6,70},{8,72},{10,74},{12,76},{14,78},{16,80}... | collective-permute-start | bytes 24584 | tf_op jit(solution)/shard_map/ppermute | solution.py:80
  56.8 2.6 %collective-permute-start.10 = (f32[2,4,256]{2,1,0:T(4,128)S(1)}, f32[2,4,256]{2,1,0:T(4,128)S(1)}, u32[]{:S(2)}, u32[]{:S(2)}) collective-permute-start(f32[2,4,256]{2,1,0:T(4,128)S(1)} %bitcast.76), channel_id=1, source_target_pairs={{0,128},{2,130},{4,132},{6,134},{8,136},{10,138},{12,140},{14,142}... | collective-permute-start | bytes 24584 | tf_op jit(solution)/shard_map/ppermute | solution.py:80
  59.4 3.9 %collective-permute-start.12 = (f32[2,4,256]{2,1,0:T(4,128)S(1)}, f32[2,4,256]{2,1,0:T(4,128)S(1)}, u32[]{:S(2)}, u32[]{:S(2)}) collective-permute-start(f32[2,4,256]{2,1,0:T(4,128)S(1)} %bitcast.75), channel_id=1, source_target_pairs={{0,192},{2,194},{4,196},{6,198},{8,200},{10,202},{12,204},{14,206}... | collective-permute-start | bytes 24584 | tf_op jit(solution)/shard_map/ppermute | solution.py:80
  63.3 0.6 maximum_convert_fusion.gain_ref
  63.8 0.5 collective-permute-done.10
  64.3 0.3 collective-permute-done.12
  64.6 0.1 copy.19
  64.8 0.9 pad.17.means_ref
  65.7 23.5 %shard_map.100 = f32[512,128]{1,0:T(8,128)} custom-call(f32[40]{0:T(128)} %reshape.27.coef_ref, f32[512,128]{1,0:T(8,128)} %pad.16.state_ref, f32[512,128]{1,0:T(8,128)} %pad.17.means_ref, f32[128,128]{1,0:T(8,128)} %pad.18.lift_ref, f32[1,128]{1,0:T(1,128)} %bitcast.80, bf16[2,1152,128]{2,1,0:T(8,128)(2,1)} %pad_maximum_fusion.conv_ref, ...), custom_call_target="tpu_custom_call" | custom-call | tf_op jit(solution)/shard_map/pallas_call | solution.py:166
  89.2 1.1 %copy.21 = f32[2,256,4]{1,2,0:T(4,128)S(1)} copy(f32[2,256,4]{2,1,0:T(8,128)} %bitcast.73) | data formatting | bytes 16384 | tf_op jit(solution)/shard_map/reshape | solution.py:259
  90.2 0.6 fusion.3
  (28 shorter events, 0.3 us)
Async XLA Ops:
  0.0 1.0 %copy-start = (f32[1,4,32,4,256]{4,3,2,1,0:T(4,128)S(1)}, f32[1,4,32,4,256]{4,3,2,1,0:T(4,128)}, u32[]{:S(2)}) copy-start(f32[1,4,32,4,256]{4,3,2,1,0:T(4,128)} %param.11) | copy-start | bytes 1572868
  1.0 0.7 copy-start.7
  1.7 10.1 %copy-start.1 = (bf16[1,9,128,128]{3,2,1,0:T(8,128)(2,1)S(1)}, bf16[1,9,128,128]{3,2,1,0:T(8,128)(2,1)}, u32[]{:S(2)}) copy-start(bf16[1,9,128,128]{3,2,1,0:T(8,128)(2,1)} %param.17) | copy-start | bytes 884740
  1.9 14.1 %collective-permute-start.1 = (f32[2,32,4,256]{3,1,2,0:T(8,128)S(1)}, f32[2,32,4,256]{3,1,2,0:T(8,128)S(1)}, u32[]{:S(2)}, u32[]{:S(2)}) collective-permute-start(f32[2,32,4,256]{3,1,2,0:T(8,128)S(1)} %fusion), channel_id=1, source_target_pairs={{0,24},{2,26},{4,28},{6,30},{8,0},{10,2},{12,4},{14,6},{16,8},{18,... | collective-permute-start | bytes 786440 | tf_op jit(solution)/shard_map/ppermute | solution.py:58
  4.7 11.2 %collective-permute-start.2 = (f32[2,32,4,256]{3,1,2,0:T(8,128)S(1)}, f32[2,32,4,256]{3,1,2,0:T(8,128)S(1)}, u32[]{:S(2)}, u32[]{:S(2)}) collective-permute-start(f32[2,32,4,256]{3,1,2,0:T(8,128)S(1)} %fusion), channel_id=1, source_target_pairs={{0,16},{2,18},{4,20},{6,22},{8,24},{10,26},{12,28},{14,30},{16,0},... | collective-permute-start | bytes 786440 | tf_op jit(solution)/shard_map/ppermute | solution.py:58
  5.5 14.1 %collective-permute-start = (f32[2,32,4,256]{3,1,2,0:T(8,128)S(1)}, f32[2,32,4,256]{3,1,2,0:T(8,128)S(1)}, u32[]{:S(2)}, u32[]{:S(2)}) collective-permute-start(f32[2,32,4,256]{3,1,2,0:T(8,128)S(1)} %fusion), channel_id=1, source_target_pairs={{0,8},{2,10},{4,12},{6,14},{8,16},{10,18},{12,20},{14,22},{16,24},... | collective-permute-start | bytes 786440 | tf_op jit(solution)/shard_map/ppermute | solution.py:58
  6.4 23.0 %collective-permute-start.7 = (s32[1]{0:T(128)}, s32[1]{0:T(128)}, u32[]{:S(2)}, u32[]{:S(2)}) collective-permute-start(s32[1]{0:T(128)} %param.13), channel_id=1, source_target_pairs={{64,0},{66,2},{68,4},{70,6},{72,8},{74,10},{76,12},{78,14},{80,16}... | collective-permute-start | bytes 20 | tf_op jit(solution)/shard_map/ppermute | solution.py:75
  11.8 0.7 copy-start.6
  12.5 0.7 copy-start.2
  12.5 34.7 %collective-permute-start.13 = (bf16[1,1153,128]{2,1,0:T(8,128)(2,1)S(1)}, bf16[1,1153,128]{2,1,0:T(8,128)(2,1)S(1)}, u32[]{:S(2)}, u32[]{:S(2)}) collective-permute-start(bf16[1,1153,128]{2,1,0:T(8,128)(2,1)S(1)} %pad_maximum_fusion.1), channel_id=1, source_target_pairs={{0,1},{1,0},{2,3},{3,2},{4,5},{5,4},{6,7},{7,6},{8,9},{9,8},{10,11... | collective-permute-start | bytes 885512 | tf_op jit(solution)/shard_map/ppermute | solution.py:223
  13.2 11.9 %copy-start.4 = (f32[1,4,4,256]{3,2,1,0:T(4,128)S(1)}, f32[1,4,4,256]{3,2,1,0:T(4,128)}, u32[]{:S(2)}) copy-start(f32[1,4,4,256]{3,2,1,0:T(4,128)} %param.10) | copy-start | bytes 49156
  19.8 27.5 %collective-permute-start.5 = (f32[2,32,4,256]{3,1,2,0:T(8,128)S(1)}, f32[2,32,4,256]{3,1,2,0:T(8,128)S(1)}, u32[]{:S(2)}, u32[]{:S(2)}) collective-permute-start(f32[2,32,4,256]{3,1,2,0:T(8,128)S(1)} %add_add_fusion.1), channel_id=1, source_target_pairs={{0,4},{2,6},{4,0},{6,2},{8,12},{10,14},{12,8},{14,10},{16,20},{18,... | collective-permute-start | bytes 786440 | tf_op jit(solution)/shard_map/ppermute | solution.py:58
  23.0 24.2 %collective-permute-start.4 = (f32[2,32,4,256]{3,1,2,0:T(8,128)S(1)}, f32[2,32,4,256]{3,1,2,0:T(8,128)S(1)}, u32[]{:S(2)}, u32[]{:S(2)}) collective-permute-start(f32[2,32,4,256]{3,1,2,0:T(8,128)S(1)} %add_add_fusion.1), channel_id=1, source_target_pairs={{0,6},{2,0},{4,2},{6,4},{8,14},{10,8},{12,10},{14,12},{16,22},{18,... | collective-permute-start | bytes 786440 | tf_op jit(solution)/shard_map/ppermute | solution.py:58
  24.1 23.2 %collective-permute-start.3 = (f32[2,32,4,256]{3,1,2,0:T(8,128)S(1)}, f32[2,32,4,256]{3,1,2,0:T(8,128)S(1)}, u32[]{:S(2)}, u32[]{:S(2)}) collective-permute-start(f32[2,32,4,256]{3,1,2,0:T(8,128)S(1)} %add_add_fusion.1), channel_id=1, source_target_pairs={{0,2},{2,4},{4,6},{6,0},{8,10},{10,12},{12,14},{14,8},{16,18},{18,... | collective-permute-start | bytes 786440 | tf_op jit(solution)/shard_map/ppermute | solution.py:58
  25.9 0.7 copy-start.5
  26.6 0.7 copy-start.3
  29.4 7.0 %collective-permute-start.11 = (s32[1]{0:T(128)}, s32[1]{0:T(128)}, u32[]{:S(2)}, u32[]{:S(2)}) collective-permute-start(s32[1]{0:T(128)} %param.13), channel_id=1, source_target_pairs={{192,0},{194,2},{196,4},{198,6},{200,8},{202,10},{204,12},{206,14}... | collective-permute-start | bytes 20 | tf_op jit(solution)/shard_map/ppermute | solution.py:75
  36.4 7.6 %collective-permute-start.9 = (s32[1]{0:T(128)}, s32[1]{0:T(128)}, u32[]{:S(2)}, u32[]{:S(2)}) collective-permute-start(s32[1]{0:T(128)} %param.13), channel_id=1, source_target_pairs={{128,0},{130,2},{132,4},{134,6},{136,8},{138,10},{140,12},{142,14}... | collective-permute-start | bytes 20 | tf_op jit(solution)/shard_map/ppermute | solution.py:75
  47.4 6.5 %collective-permute-start.6 = (f32[2,32,4,256]{3,1,2,0:T(8,128)S(1)}, f32[2,32,4,256]{3,1,2,0:T(8,128)S(1)}, u32[]{:S(2)}, u32[]{:S(2)}) collective-permute-start(f32[2,32,4,256]{3,1,2,0:T(8,128)S(1)} %add_add_fusion), channel_id=1, source_target_pairs={{0,32},{2,34},{4,36},{6,38},{8,40},{10,42},{12,44},{14,46},{16,48}... | collective-permute-start | bytes 786440 | tf_op jit(solution)/shard_map/ppermute | solution.py:78
  54.0 9.8 %collective-permute-start.8 = (f32[2,4,256]{2,1,0:T(4,128)S(1)}, f32[2,4,256]{2,1,0:T(4,128)S(1)}, u32[]{:S(2)}, u32[]{:S(2)}) collective-permute-start(f32[2,4,256]{2,1,0:T(4,128)S(1)} %bitcast.77), channel_id=1, source_target_pairs={{0,64},{2,66},{4,68},{6,70},{8,72},{10,74},{12,76},{14,78},{16,80}... | collective-permute-start | bytes 24584 | tf_op jit(solution)/shard_map/ppermute | solution.py:80
  56.8 7.6 %collective-permute-start.10 = (f32[2,4,256]{2,1,0:T(4,128)S(1)}, f32[2,4,256]{2,1,0:T(4,128)S(1)}, u32[]{:S(2)}, u32[]{:S(2)}) collective-permute-start(f32[2,4,256]{2,1,0:T(4,128)S(1)} %bitcast.76), channel_id=1, source_target_pairs={{0,128},{2,130},{4,132},{6,134},{8,136},{10,138},{12,140},{14,142}... | collective-permute-start | bytes 24584 | tf_op jit(solution)/shard_map/ppermute | solution.py:80
  59.4 5.3 %collective-permute-start.12 = (f32[2,4,256]{2,1,0:T(4,128)S(1)}, f32[2,4,256]{2,1,0:T(4,128)S(1)}, u32[]{:S(2)}, u32[]{:S(2)}) collective-permute-start(f32[2,4,256]{2,1,0:T(4,128)S(1)} %bitcast.75), channel_id=1, source_target_pairs={{0,192},{2,194},{4,196},{6,198},{8,200},{10,202},{12,204},{14,206}... | collective-permute-start | bytes 24584 | tf_op jit(solution)/shard_map/ppermute | solution.py:80
